TPU v7x, 32 devices: a whole 2x2x4 slice. The times are simulated.
32 devices in a mesh: cache: 8 (over z, x), stream: 4 (over y, core).
Axes of the slice: x: 2, y: 2, z: 4, core: 2. Of those that a mesh axis runs over, the one named last changes fastest.
Arguments:
- queries: bfloat16 [2048, 4096], P('cache', 'stream'), may hold values from -12.5 to 12.5
- own_kv: bfloat16 [2048, 1024], P('cache', 'stream'), may hold values from -6 to 6
- passage_store: bfloat16 [128, 512, 1024], P('cache', None, 'stream'), may hold values from -6 to 6
- out_weight: bfloat16 [4096, 8192], P('stream', 'cache'), may hold values from -0.375 to 0.375
- passage_slot: int32 [128], replicated, may hold values from 0 to 127, as said below
- retrieved: int32 [16, 16], P('cache'), may hold values from 0 to 127, as said below
Outputs:
- layer_out: bfloat16 [2048, 8192], P('cache', 'stream')
Inputs may be any that keep to these rules, and one draw needn't show every extreme that they name: `passage_slot`: a permutation. `retrieved`: over the 2 queries of one index of cache all ids are distinct; at most 8 of their slots fall in any one block of 16 consecutive slots, and some block holds exactly 8 of them for every index of cache.
All inputs are finite; a program needn't handle non-finite values.
Results may differ from a plain program's by a relative error of at most 0.015.
Values may be sent and summed in bfloat16 or wider, within the bound.
No kernel may reach another device: no remote copies, remote signals or barrier semaphores. Data moves between devices by JAX's collectives and lax.ppermute only.
A program may use at most 192 MiB of HBM per device.

v0:
```python
import math

import jax
import jax.numpy as jnp
from jax import lax
from jax.sharding import PartitionSpec as P

HD = 128
QLEN = 128
PLEN = 512


def attend_query(query_rows, own_rows, passages):
    kv_count = own_rows.shape[1] // (2 * HD)
    groups = query_rows.shape[1] // (kv_count * HD)
    tokens_here = query_rows.shape[0]
    passage_len = passages.shape[0]
    length = passage_len + tokens_here
    context = jnp.concatenate([passages, own_rows], axis=0).reshape(length, kv_count, 2, HD)
    key_part = context[:, :, 0, :]
    value_part = context[:, :, 1, :]
    query_part = query_rows.reshape(tokens_here, kv_count, groups, HD)
    scores = jnp.einsum(
        "tkgd,lkd->kgtl", query_part, key_part, preferred_element_type=jnp.float32
    ) / math.sqrt(HD)
    position = jnp.arange(length)[None, :] - passage_len
    visible = position <= jnp.arange(tokens_here)[:, None]
    scores = jnp.where(visible, scores, -jnp.inf)
    row_peak = jnp.max(scores, axis=-1, keepdims=True)
    powers = jnp.exp(scores - row_peak)
    totals = jnp.sum(powers, axis=-1)
    soft_weights = powers.astype(jnp.bfloat16)
    weighted = jnp.einsum(
        "kgtl,lkd->tkgd", soft_weights, value_part, preferred_element_type=jnp.float32
    )
    attended = weighted / jnp.transpose(totals, (2, 0, 1))[..., None]
    return attended.reshape(tokens_here, kv_count * groups * HD).astype(jnp.bfloat16)


def shards(queries, own_kv, passage_store, out_weight, passage_slot, retrieved):
    n_cache = lax.axis_size("cache")
    store_count = passage_store.shape[0]
    width_kv = passage_store.shape[2]
    slot_total = passage_slot.shape[0]
    query_count, per_query = retrieved.shape
    wanted_count = query_count * per_query
    capacity = max(2, (2 * wanted_count + n_cache - 1) // n_cache)
    wanted = retrieved.reshape(wanted_count)
    id_match = wanted[:, None] == jnp.arange(slot_total, dtype=jnp.int32)[None, :]
    store_slots = jnp.sum(jnp.where(id_match, passage_slot[None, :], 0), axis=1)
    owners = store_slots // store_count
    local_rows = store_slots % store_count
    places = jnp.arange(wanted_count, dtype=jnp.int32)
    earlier = (owners[None, :] == owners[:, None]) & (places[None, :] < places[:, None])
    order_rank = jnp.sum(earlier, axis=1)
    flat_slot = owners * capacity + order_rank
    slot_match = flat_slot[:, None] == jnp.arange(n_cache * capacity, dtype=jnp.int32)[None, :]
    send_rows = jnp.sum(jnp.where(slot_match, local_rows[:, None], 0), axis=0).reshape(
        n_cache, capacity
    )
    asked_rows = lax.all_to_all(send_rows, "cache", split_axis=0, concat_axis=0, tiled=True)
    outgoing = passage_store[asked_rows]
    arrived = lax.all_to_all(outgoing, "cache", split_axis=0, concat_axis=0, tiled=True)
    picked = arrived.reshape(n_cache * capacity, PLEN, width_kv)[flat_slot]

    def per_query_block(inputs):
        query_rows, own_rows, passages = inputs
        return attend_query(query_rows, own_rows, passages)

    attended = lax.map(
        per_query_block,
        (
            queries.reshape(query_count, QLEN, queries.shape[1]),
            own_kv.reshape(query_count, QLEN, own_kv.shape[1]),
            picked.reshape(query_count, per_query * PLEN, width_kv),
        ),
    )
    attended = attended.reshape(query_count * QLEN, queries.shape[1])
    partial_sums = jnp.dot(
        attended,
        lax.all_gather(out_weight, "cache", axis=1, tiled=True),
        preferred_element_type=jnp.float32,
    )
    return lax.psum_scatter(
        partial_sums.astype(jnp.bfloat16), "stream", scatter_dimension=1, tiled=True
    )


def solution(mesh):
    return jax.shard_map(
        shards,
        mesh=mesh,
        in_specs=(
            P("cache", "stream"),
            P("cache", "stream"),
            P("cache", None, "stream"),
            P("stream", "cache"),
            P(),
            P("cache", None),
        ),
        out_specs=P("cache", "stream"),
        check_vma=False,
    )
```

profile of v0, /device:TPU:4, one launch (start us, length us, event | category | flops | bytes accessed | tf_op | source)
XLA Modules:
  0.0 805.9 jit_solution(13889245432415470989)
XLA Ops:
  6.5 0.8 eq.22
  7.3 0.8 select_reduce_fusion.1
  8.1 0.2 convert_reduce_fusion
  8.3 0.1 select_reduce_fusion
  8.4 0.1 all_to_all.11
  8.5 12.1 %all_to_all.17 = s32[8,1,8]{2,1,0:T(1,128)S(1)} all-to-all(s32[8,1,8]{2,1,0:T(1,128)S(1)} %bitcast.127), channel_id=1, replica_groups=mesh['cache'=8,'stream'=4] {'cache'}, dimensions={0} | all-to-all | bytes 512 | tf_op jit(solution)/shard_map/all_to_all | solution.py:61
  20.6 0.1 reshape.245
  20.7 9.5 %gather_fusion = bf16[64,512,256]{2,1,0:T(8,128)(2,1)} fusion(bf16[16,512,256]{2,1,0:T(8,128)(2,1)} %param.10, s32[1024]{0:T(1024)S(1)} %pad_clamp_fusion.1), kind=kCustom, calls=%fused_computation | custom fusion | bytes 33554688 | tf_op jit(solution)/shard_map/gather | solution.py:62
  30.2 5.8 all-to-all-start.1
  36.0 0.0 all-gather.2.cloned.1.call-start
  36.0 0.7 all-gather.2.cloned.1.call-update
  36.7 0.0 reduce-scatter.2.cloned.1.call-start
  36.8 563.2 %all-to-all-done.1 = bf16[8,8,512,256]{3,2,1,0:T(8,128)(2,1)} async-done(((bf16[8,8,512,256]{3,2,1,0:T(8,128)(2,1)}), bf16[8,8,512,256]{3,2,1,0:T(8,128)(2,1)}, u32[]{:S(2)}, u32[]{:S(2)}) %all-to-all-start.1) | async-done | bytes 16777248 | tf_op jit(solution)/shard_map/all_to_all | solution.py:63
  600.0 0.0 copy-start
  600.0 0.0 copy-start.1
  600.0 10.9 %gather_fusion.1 = bf16[32,512,256]{2,1,0:T(8,128)(2,1)} fusion(bf16[64,512,256]{2,1,0:T(8,128)(2,1)} %bitcast.19, s32[1024]{0:T(1024)S(1)} %pad_clamp_fusion), kind=kCustom, calls=%fused_computation.1 | custom fusion | bytes 16777344 | tf_op jit(solution)/shard_map/gather | solution.py:64
  610.9 0.0 copy-done
  610.9 0.0 copy-done.1
  610.9 133.7 %while.12 = (s32[]{:T(128)}, bf16[2,128,1024]{2,1,0:T(8,128)(2,1)S(1)}, bf16[2,8192,256]{2,1,0:T(8,128)(2,1)}, bf16[2,128,256]{2,1,0:T(8,128)(2,1)S(1)}, bf16[2,128,1024]{2,1,0:T(8,128)(2,1)S(1)}, /*index=5*/s32[]{:T(128)}) while((s32[]{:T(128)}, bf16[2,128,1024]{2,1,0:T(8,128)(2,1)S(1)}, bf16[2,8192,256]{2,1,0:T(8,128)(2,1)}, ...), condition=%wide.region_6.7_spmd, body=%wide.region_3.6_spmd.sunk | while | flops 4465645568 | bytes 143283296 | solution.py:70
  610.9 4.4 constant_dynamic-slice_fusion.8
  615.3 6.4 copy.62
  621.7 6.3 copy.63
  628.0 0.1 copy.60
  628.1 0.1 copy.61
  628.3 0.2 copy.59
  628.5 3.8 iota_compare_fusion.5
  632.3 14.9 %fusion.47 = (f32[8,128]{1,0:T(8,128)S(1)}, f32[8320,128,8]{1,0,2:T(8,128)}) fusion(pred[128,8320]{0,1:T(8,128)(4,1)S(1)} %iota_compare_fusion.5, bf16[128,8,128]{0,2,1:T(8,128)(2,1)S(1)} %bitcast.121, bf16[128,1,2,128]{3,0,2,1:T(8,128)(2,1)S(1)} %copy.61, bf16[8192,1,2,128]{3,0,2,1:T(8,128)(2,1)} %copy.63), kind=kOutput, calls=%fused_computation.6.clone.1 | convolution fusion | flops 2210855936 | bytes 39669760 | tf_op jit(solution)/shard_map/while/body/eval_jaxpr/tkgd,lkd->kgtl/dot_general | solution.py:23
  647.1 14.4 %fusion.48 = f32[8,128]{1,0:T(8,128)S(1)} fusion(f32[8320,128,8]{1,0,2:T(8,128)} %get-tuple-element.133, f32[8,128]{1,0:T(8,128)S(1)} %get-tuple-element.134, pred[128,8320]{0,1:T(8,128)(4,1)S(1)} %iota_compare_fusion.5), kind=kLoop, calls=%fused_computation.4.clone.1 | loop fusion | flops 34077696 | bytes 35151872 | tf_op jit(solution)/shard_map/while/body/eval_jaxpr/reduce_sum | solution.py:31
  661.5 16.1 %fusion.49 = bf16[128,1,8,128]{0,3,2,1:T(8,128)(2,1)S(1)} fusion(f32[8320,128,8]{1,0,2:T(8,128)} %get-tuple-element.133, f32[8,128]{1,0:T(8,128)S(1)} %get-tuple-element.134, pred[128,8320]{0,1:T(8,128)(4,1)S(1)} %iota_compare_fusion.5, bf16[8192,1,2,128]{3,0,2,1:T(8,128)(2,1)} %copy.63, bf16[128,1,2,128]{3,0,2,1:T(8,128)(2,1)S(1)} %copy.61, ...), kind=kOutput, calls=%fused_computation.21.clone.1 | convolution fusion | flops 2219638784 | bytes 39673856 | tf_op jit(solution)/shard_map/while/body/eval_jaxpr/kgtl,lkd->tkgd/dot_general | solution.py:33
  677.6 0.1 copy.64
  677.8 4.4 constant_dynamic-slice_fusion.8
  682.2 6.4 copy.62
  688.6 6.3 copy.63
  694.9 0.1 copy.60
  695.0 0.1 copy.61
  695.2 0.2 copy.59
  695.4 3.8 iota_compare_fusion.5
  699.1 14.9 %fusion.47 = (f32[8,128]{1,0:T(8,128)S(1)}, f32[8320,128,8]{1,0,2:T(8,128)}) fusion(pred[128,8320]{0,1:T(8,128)(4,1)S(1)} %iota_compare_fusion.5, bf16[128,8,128]{0,2,1:T(8,128)(2,1)S(1)} %bitcast.121, bf16[128,1,2,128]{3,0,2,1:T(8,128)(2,1)S(1)} %copy.61, bf16[8192,1,2,128]{3,0,2,1:T(8,128)(2,1)} %copy.63), kind=kOutput, calls=%fused_computation.6.clone.1 | convolution fusion | flops 2210855936 | bytes 39669760 | tf_op jit(solution)/shard_map/while/body/eval_jaxpr/tkgd,lkd->kgtl/dot_general | solution.py:23
  714.0 14.4 %fusion.48 = f32[8,128]{1,0:T(8,128)S(1)} fusion(f32[8320,128,8]{1,0,2:T(8,128)} %get-tuple-element.133, f32[8,128]{1,0:T(8,128)S(1)} %get-tuple-element.134, pred[128,8320]{0,1:T(8,128)(4,1)S(1)} %iota_compare_fusion.5), kind=kLoop, calls=%fused_computation.4.clone.1 | loop fusion | flops 34077696 | bytes 35151872 | tf_op jit(solution)/shard_map/while/body/eval_jaxpr/reduce_sum | solution.py:31
  728.4 16.1 %fusion.49 = bf16[128,1,8,128]{0,3,2,1:T(8,128)(2,1)S(1)} fusion(f32[8320,128,8]{1,0,2:T(8,128)} %get-tuple-element.133, f32[8,128]{1,0:T(8,128)S(1)} %get-tuple-element.134, pred[128,8320]{0,1:T(8,128)(4,1)S(1)} %iota_compare_fusion.5, bf16[8192,1,2,128]{3,0,2,1:T(8,128)(2,1)} %copy.63, bf16[128,1,2,128]{3,0,2,1:T(8,128)(2,1)S(1)} %copy.61, ...), kind=kOutput, calls=%fused_computation.21.clone.1 | convolution fusion | flops 2219638784 | bytes 39673856 | tf_op jit(solution)/shard_map/while/body/eval_jaxpr/kgtl,lkd->tkgd/dot_general | solution.py:33
  744.4 0.1 copy.64
  744.6 0.0 all-gather.2.cloned.1.call-done
  744.7 12.0 %convolution_convert_fusion = bf16[256,8192]{1,0:T(8,128)(2,1)} fusion(bf16[256,1024]{1,0:T(8,128)(2,1)S(1)} %bitcast.129, bf16[1024,8192]{1,0:T(8,128)(2,1)} %all-gather.2.cloned.1.call-done), kind=kOutput, calls=%fused_computation.31 | convolution fusion | flops 4297064448 | bytes 21495808 | tf_op jit(solution)/shard_map/dot_general | solution.py:79
  756.7 0.0 reduce-scatter.2.cloned.1.call-update
  756.7 42.3 %reduce-scatter.2.cloned.1.call-done = bf16[256,2048]{1,0:T(8,128)(2,1)} async-done(((bf16[256,8192]{1,0:T(8,128)(2,1)}), bf16[256,2048]{1,0:T(8,128)(2,1)}) %reduce-scatter.2.cloned.1.call-update) | async-done | bytes 1048592 | tf_op jit(solution)/shard_map/reduce_scatter | solution.py:84
  (15 shorter events, 0.2 us)
Async XLA Ops:
  30.2 569.8 %all-to-all-start.1 = ((bf16[8,8,512,256]{3,2,1,0:T(8,128)(2,1)}), bf16[8,8,512,256]{3,2,1,0:T(8,128)(2,1)}, u32[]{:S(2)}, u32[]{:S(2)}) async-start(bf16[8,8,512,256]{3,2,1,0:T(8,128)(2,1)} %bitcast.120), calls=%async_computation.1 | async-start | bytes 33554432 | tf_op jit(solution)/shard_map/all_to_all | solution.py:63
  36.0 708.7 %all-gather.2.cloned.1.call-start = ((), (), s32[]{:S(2)}) async-start(), calls=%async_computation.3 | async-start | bytes 18874368 | tf_op jit(solution)/shard_map/all_gather | solution.py:81
  36.7 762.3 %reduce-scatter.2.cloned.1.call-start = ((), (), s32[]{:S(2)}) async-start(), calls=%async_computation.4 | async-start | bytes 5242880 | tf_op jit(solution)/shard_map/reduce_scatter | solution.py:84
  600.0 10.9 %copy-start = (bf16[256,1024]{1,0:T(8,128)(2,1)S(1)}, bf16[256,1024]{1,0:T(8,128)(2,1)}, u32[]{:S(2)}) copy-start(bf16[256,1024]{1,0:T(8,128)(2,1)} %param.8) | copy-start | bytes 1572868
  600.0 10.9 %copy-start.1 = (bf16[256,256]{1,0:T(8,128)(2,1)S(1)}, bf16[256,256]{1,0:T(8,128)(2,1)}, u32[]{:S(2)}) copy-start(bf16[256,256]{1,0:T(8,128)(2,1)} %param.9) | copy-start | bytes 393220
Sparse Core Ops, SparseCore 0:
  39.0 540.0 all-gather.1
  756.8 42.1 reduce-scatter.1
where the time goes:
time: 810 us; the launch traced here: 806 us
  waiting for transfers between devices  606 us (75%)
  matrix products  73.8 us (9%)
  local copies, waits for them, and re-layouts  56.8 us (7%)
  other arithmetic  37.4 us (5%)
  between operations  13.5 us (2%)
  blocking collectives  12.1 us (1%)
    all_to_all x1, waiting for transfers between devices, shards(): lax.all_to_all(outgoing, 'cache', split_axis=0, concat_axis=0, tiled=True)  563 us
    reduce_scatter x1, waiting for transfers between devices, shards(): lax.psum_scatter(partial_sums.astype(jnp.bfloat16), 'stream', scatter_dim...  42.3 us
    dot_general x2, matrix products, attend_query(): jnp.einsum('kgtl,lkd->tkgd', soft_weights, value_part, preferred_element_...  32.1 us
    dot_general x2, matrix products, attend_query(): jnp.einsum('tkgd,lkd->kgtl', query_part, key_part, preferred_element_type...  29.7 us
    reduce_sum x2, other arithmetic, attend_query(): totals = jnp.sum(powers, axis=-1)  28.7 us
    dynamic_slice x12, local copies, waits for them, and re-layouts, shards(): lax.map(per_query_block, (queries.reshape(query_count, QLEN, queries.shap...  22.2 us
  transfers between devices with their start and end apart: 3, of which 2 were waited for; matrix products, arithmetic and copies ran while one was open for 18% of the time, Pallas kernels for 0%

commit v1 on v0

--- a/solution.py
+++ b/solution.py
@@ -76,14 +76,35 @@
         ),
     )
     attended = attended.reshape(query_count * QLEN, queries.shape[1])
-    partial_sums = jnp.dot(
-        attended,
-        lax.all_gather(out_weight, "cache", axis=1, tiled=True),
-        preferred_element_type=jnp.float32,
+    return project(attended, out_weight)
+
+
+def project(attended, out_weight):
+    n_cache = lax.axis_size("cache")
+    n_stream = lax.axis_size("stream")
+    rows = attended.shape[0]
+    group = n_cache // n_stream
+    everyone = lax.all_gather(attended, "cache", axis=0, tiled=True)
+    partial_sums = jnp.dot(everyone, out_weight, preferred_element_type=jnp.float32)
+    reduced = lax.psum_scatter(
+        partial_sums.astype(jnp.bfloat16), "stream", scatter_dimension=0, tiled=True
     )
-    return lax.psum_scatter(
-        partial_sums.astype(jnp.bfloat16), "stream", scatter_dimension=1, tiled=True
-    )
+    me = lax.axis_index("cache")
+    width = reduced.shape[1]
+    out = jnp.zeros((rows, group * width), reduced.dtype)
+    for r in range(group):
+        take = (me % group + r) % group
+        piece = lax.dynamic_slice_in_dim(reduced, take * rows, rows, axis=0)
+        perm = []
+        for c in range(n_cache):
+            for s in range(n_stream):
+                dst_c = s * group + (c % group + r) % group
+                dst_s = c // group
+                perm.append((c * n_stream + s, dst_c * n_stream + dst_s))
+        got = lax.ppermute(piece, ("cache", "stream"), perm)
+        put = (me - r) % group
+        out = lax.dynamic_update_slice_in_dim(out, got, put * width, axis=1)
+    return out
 
 
 def solution(mesh):

time: 810 us -> 731 us (0.902)
  waiting for transfers between devices: 606 us -> 522 us
    all_to_all x1, waiting for transfers between devices: 563 us -> 362 us  [shards(): lax.all_to_all(outgoing, 'cache', split_axis=0, concat_axis=0, tiled=True)]
    all_gather x1, waiting for transfers between devices: 0.02 us -> 72.3 us  [project(): everyone = lax.all_gather(attended, 'cache', axis=0, tiled=True)]
    ppermute x0 -> x2, waiting for transfers between devices: none -> 45.9 us  [project(): got = lax.ppermute(piece, ('cache', 'stream'), perm)]
  transfers between devices with their start and end apart: 3 -> 5, of which waited for: 2 -> 5; matrix products, arithmetic and copies ran while one was open for 18% -> 0% of each run, Pallas kernels for 0% -> 0%
where the time goes in v1:
time: 731 us; the launch traced here: 730 us
  waiting for transfers between devices  522 us (71%)
  matrix products  70.2 us (10%)
  local copies, waits for them, and re-layouts  61.7 us (8%)
  other arithmetic  37.4 us (5%)
  between operations  13.5 us (2%)
  starting transfers between devices  12.9 us (2%)
  blocking collectives  12.1 us (2%)
    all_to_all x1, waiting for transfers between devices, shards(): lax.all_to_all(outgoing, 'cache', split_axis=0, concat_axis=0, tiled=True)  362 us
    all_gather x1, waiting for transfers between devices, project(): everyone = lax.all_gather(attended, 'cache', axis=0, tiled=True)  72.3 us
    ppermute x2, waiting for transfers between devices, project(): got = lax.ppermute(piece, ('cache', 'stream'), perm)  45.9 us
    reduce_scatter x1, waiting for transfers between devices, project(): lax.psum_scatter(partial_sums.astype(jnp.bfloat16), 'stream', scatter_dim...  41.7 us
    dot_general x2, matrix products, attend_query(): jnp.einsum('kgtl,lkd->tkgd', soft_weights, value_part, preferred_element_...  32.1 us
    dot_general x2, matrix products, attend_query(): jnp.einsum('tkgd,lkd->kgtl', query_part, key_part, preferred_element_type...  29.7 us
    reduce_sum x2, other arithmetic, attend_query(): totals = jnp.sum(powers, axis=-1)  28.7 us
    dynamic_slice x12, local copies, waits for them, and re-layouts, shards(): lax.map(per_query_block, (queries.reshape(query_count, QLEN, queries.shap...  22.3 us
  transfers between devices with their start and end apart: 5, of which 5 were waited for; matrix products, arithmetic and copies ran while one was open for 0% of the time, Pallas kernels for 0%

profile of v1, /device:TPU:4, one launch (start us, length us, event | category | flops | bytes accessed | tf_op | source)
XLA Modules:
  0.0 729.5 jit_solution(13120011358236367580)
XLA Ops:
  6.5 0.0 copy-start
  6.5 0.9 eq.50
  7.4 0.8 select_reduce_fusion.1
  8.3 0.2 convert_reduce_fusion
  8.5 0.1 select_reduce_fusion
  8.6 0.1 all_to_all.11
  8.7 12.1 %all_to_all.17 = s32[8,1,8]{2,1,0:T(1,128)S(1)} all-to-all(s32[8,1,8]{2,1,0:T(1,128)S(1)} %bitcast.128), channel_id=1, replica_groups=mesh['cache'=8,'stream'=4] {'cache'}, dimensions={0} | all-to-all | bytes 512 | tf_op jit(solution)/shard_map/all_to_all | solution.py:61
  20.7 0.1 reshape.245
  20.8 9.5 %gather_fusion = bf16[64,512,256]{2,1,0:T(8,128)(2,1)} fusion(bf16[16,512,256]{2,1,0:T(8,128)(2,1)} %param.10, s32[1024]{0:T(1024)S(1)} %pad_clamp_fusion.1), kind=kCustom, calls=%fused_computation | custom fusion | bytes 33554688 | tf_op jit(solution)/shard_map/gather | solution.py:62
  30.3 5.8 all-to-all-start.1
  36.1 0.0 all-gather.2.cloned.1.call-start
  36.2 361.6 %all-to-all-done.1 = bf16[8,8,512,256]{3,2,1,0:T(8,128)(2,1)} async-done(((bf16[8,8,512,256]{3,2,1,0:T(8,128)(2,1)}), bf16[8,8,512,256]{3,2,1,0:T(8,128)(2,1)}, u32[]{:S(2)}, u32[]{:S(2)}) %all-to-all-start.1) | async-done | bytes 16777248 | tf_op jit(solution)/shard_map/all_to_all | solution.py:63
  397.8 0.0 copy-start.1
  397.8 0.0 copy-start.3
  397.8 10.9 %gather_fusion.1 = bf16[32,512,256]{2,1,0:T(8,128)(2,1)} fusion(bf16[64,512,256]{2,1,0:T(8,128)(2,1)} %bitcast.19, s32[1024]{0:T(1024)S(1)} %pad_clamp_fusion), kind=kCustom, calls=%fused_computation.1 | custom fusion | bytes 16777344 | tf_op jit(solution)/shard_map/gather | solution.py:64
  408.7 0.0 copy-done.1
  408.7 0.0 copy-done.3
  408.7 135.2 %while.12 = (s32[]{:T(128)}, bf16[2,128,1024]{2,1,0:T(8,128)(2,1)}, bf16[2,8192,256]{2,1,0:T(8,128)(2,1)}, bf16[2,128,256]{2,1,0:T(8,128)(2,1)S(1)}, bf16[2,128,1024]{2,1,0:T(8,128)(2,1)S(1)}, /*index=5*/s32[]{:T(128)}) while((s32[]{:T(128)}, bf16[2,128,1024]{2,1,0:T(8,128)(2,1)}, bf16[2,8192,256]{2,1,0:T(8,128)(2,1)}, ...), condition=%wide.region_6.7_spmd, body=%wide.region_3.6_spmd.sunk | while | flops 4465645568 | bytes 143283808 | solution.py:70
  408.7 4.4 constant_dynamic-slice_fusion.10
  413.1 6.4 copy.62
  419.5 6.3 copy.63
  425.9 0.1 copy.60
  426.0 0.1 copy.61
  426.1 0.2 copy.59
  426.3 3.8 iota_compare_fusion.5
  430.1 14.9 %fusion.47 = (f32[8,128]{1,0:T(8,128)S(1)}, f32[8320,128,8]{1,0,2:T(8,128)}) fusion(pred[128,8320]{0,1:T(8,128)(4,1)S(1)} %iota_compare_fusion.5, bf16[128,8,128]{0,2,1:T(8,128)(2,1)S(1)} %bitcast.121, bf16[128,1,2,128]{3,0,2,1:T(8,128)(2,1)S(1)} %copy.61, bf16[8192,1,2,128]{3,0,2,1:T(8,128)(2,1)} %copy.63), kind=kOutput, calls=%fused_computation.6.clone.1 | convolution fusion | flops 2210855936 | bytes 39669760 | tf_op jit(solution)/shard_map/while/body/eval_jaxpr/tkgd,lkd->kgtl/dot_general | solution.py:23
  445.0 14.4 %fusion.48 = f32[8,128]{1,0:T(8,128)S(1)} fusion(f32[8320,128,8]{1,0,2:T(8,128)} %get-tuple-element.135, f32[8,128]{1,0:T(8,128)S(1)} %get-tuple-element.136, pred[128,8320]{0,1:T(8,128)(4,1)S(1)} %iota_compare_fusion.5), kind=kLoop, calls=%fused_computation.4.clone.1 | loop fusion | flops 34077696 | bytes 35151872 | tf_op jit(solution)/shard_map/while/body/eval_jaxpr/reduce_sum | solution.py:31
  459.3 16.1 %fusion.49 = bf16[128,1,8,128]{0,3,2,1:T(8,128)(2,1)S(1)} fusion(f32[8320,128,8]{1,0,2:T(8,128)} %get-tuple-element.135, f32[8,128]{1,0:T(8,128)S(1)} %get-tuple-element.136, pred[128,8320]{0,1:T(8,128)(4,1)S(1)} %iota_compare_fusion.5, bf16[8192,1,2,128]{3,0,2,1:T(8,128)(2,1)} %copy.63, bf16[128,1,2,128]{3,0,2,1:T(8,128)(2,1)S(1)} %copy.61, ...), kind=kOutput, calls=%fused_computation.21.clone.1 | convolution fusion | flops 2219638784 | bytes 39673856 | tf_op jit(solution)/shard_map/while/body/eval_jaxpr/kgtl,lkd->tkgd/dot_general | solution.py:33
  475.4 0.1 copy.64
  475.6 0.7 constant_dynamic-update-slice_fusion.4
  476.3 4.4 constant_dynamic-slice_fusion.10
  480.7 6.4 copy.62
  487.1 6.3 copy.63
  493.5 0.1 copy.60
  493.6 0.1 copy.61
  493.8 0.2 copy.59
  493.9 3.8 iota_compare_fusion.5
  497.7 14.9 %fusion.47 = (f32[8,128]{1,0:T(8,128)S(1)}, f32[8320,128,8]{1,0,2:T(8,128)}) fusion(pred[128,8320]{0,1:T(8,128)(4,1)S(1)} %iota_compare_fusion.5, bf16[128,8,128]{0,2,1:T(8,128)(2,1)S(1)} %bitcast.121, bf16[128,1,2,128]{3,0,2,1:T(8,128)(2,1)S(1)} %copy.61, bf16[8192,1,2,128]{3,0,2,1:T(8,128)(2,1)} %copy.63), kind=kOutput, calls=%fused_computation.6.clone.1 | convolution fusion | flops 2210855936 | bytes 39669760 | tf_op jit(solution)/shard_map/while/body/eval_jaxpr/tkgd,lkd->kgtl/dot_general | solution.py:23
  512.6 14.4 %fusion.48 = f32[8,128]{1,0:T(8,128)S(1)} fusion(f32[8320,128,8]{1,0,2:T(8,128)} %get-tuple-element.135, f32[8,128]{1,0:T(8,128)S(1)} %get-tuple-element.136, pred[128,8320]{0,1:T(8,128)(4,1)S(1)} %iota_compare_fusion.5), kind=kLoop, calls=%fused_computation.4.clone.1 | loop fusion | flops 34077696 | bytes 35151872 | tf_op jit(solution)/shard_map/while/body/eval_jaxpr/reduce_sum | solution.py:31
  527.0 16.1 %fusion.49 = bf16[128,1,8,128]{0,3,2,1:T(8,128)(2,1)S(1)} fusion(f32[8320,128,8]{1,0,2:T(8,128)} %get-tuple-element.135, f32[8,128]{1,0:T(8,128)S(1)} %get-tuple-element.136, pred[128,8320]{0,1:T(8,128)(4,1)S(1)} %iota_compare_fusion.5, bf16[8192,1,2,128]{3,0,2,1:T(8,128)(2,1)} %copy.63, bf16[128,1,2,128]{3,0,2,1:T(8,128)(2,1)S(1)} %copy.61, ...), kind=kOutput, calls=%fused_computation.21.clone.1 | convolution fusion | flops 2219638784 | bytes 39673856 | tf_op jit(solution)/shard_map/while/body/eval_jaxpr/kgtl,lkd->tkgd/dot_general | solution.py:33
  543.0 0.1 copy.64
  543.2 0.7 constant_dynamic-update-slice_fusion.4
  543.9 0.0 all-gather.2.cloned.1.call-update
  543.9 0.2 reduce-scatter.2.cloned.1.call-start
  544.2 72.3 %all-gather.2.cloned.1.call-done = bf16[2048,1024]{1,0:T(8,128)(2,1)} async-done(((bf16[256,1024]{1,0:T(8,128)(2,1)}), bf16[2048,1024]{1,0:T(8,128)(2,1)}) %all-gather.2.cloned.1.call-update) | async-done | bytes 4194320 | tf_op jit(solution)/shard_map/all_gather | solution.py:87
  616.5 0.0 copy-done
  616.5 8.3 %convolution_convert_fusion = bf16[2048,1024]{1,0:T(8,128)(2,1)} fusion(bf16[2048,1024]{1,0:T(8,128)(2,1)} %all-gather.2.cloned.1.call-done, bf16[1024,1024]{1,0:T(8,128)(2,1)S(1)} %copy-done), kind=kOutput, calls=%fused_computation.31 | convolution fusion | flops 4297064448 | bytes 10485760 | tf_op jit(solution)/shard_map/dot_general | solution.py:88
  624.8 0.0 reduce-scatter.2.cloned.1.call-update
  624.9 41.7 %reduce-scatter.2.cloned.1.call-done = bf16[512,1024]{1,0:T(8,128)(2,1)} async-done(((bf16[2048,1024]{1,0:T(8,128)(2,1)}), bf16[512,1024]{1,0:T(8,128)(2,1)}) %reduce-scatter.2.cloned.1.call-update) | async-done | bytes 1048592 | tf_op jit(solution)/shard_map/reduce_scatter | solution.py:89
  666.6 2.2 constant_dynamic-slice_fusion.3
  668.9 5.5 collective-permute-start
  674.3 1.5 collective-permute-start.1
  675.8 34.2 %collective-permute-done = bf16[256,1024]{1,0:T(8,128)(2,1)S(1)} collective-permute-done((bf16[256,1024]{1,0:T(8,128)(2,1)}, bf16[256,1024]{1,0:T(8,128)(2,1)S(1)}, u32[]{:S(2)}, u32[]{:S(2)}) %collective-permute-start) | collective-permute-done | bytes 524320 | tf_op jit(solution)/shard_map/ppermute | solution.py:104
  710.0 0.1 broadcast_in_dim.61
  710.1 0.1 constant_dynamic-update-slice_fusion.1
  710.2 0.0 copy-start.2
  710.2 11.6 %collective-permute-done.1 = bf16[256,1024]{1,0:T(8,128)(2,1)S(1)} collective-permute-done((bf16[256,1024]{1,0:T(8,128)(2,1)}, bf16[256,1024]{1,0:T(8,128)(2,1)S(1)}, u32[]{:S(2)}, u32[]{:S(2)}) %collective-permute-start.1) | collective-permute-done | bytes 524320 | tf_op jit(solution)/shard_map/ppermute | solution.py:104
  721.8 0.0 copy-done.2
  721.8 0.8 constant_dynamic-update-slice_fusion.2
  (13 shorter events, 0.1 us)
Async XLA Ops:
  6.5 610.0 %copy-start = (bf16[1024,1024]{1,0:T(8,128)(2,1)S(1)}, bf16[1024,1024]{1,0:T(8,128)(2,1)}, u32[]{:S(2)}) copy-start(bf16[1024,1024]{1,0:T(8,128)(2,1)} %param.11) | copy-start | bytes 6291460
  30.3 367.4 %all-to-all-start.1 = ((bf16[8,8,512,256]{3,2,1,0:T(8,128)(2,1)}), bf16[8,8,512,256]{3,2,1,0:T(8,128)(2,1)}, u32[]{:S(2)}, u32[]{:S(2)}) async-start(bf16[8,8,512,256]{3,2,1,0:T(8,128)(2,1)} %bitcast.120), calls=%async_computation.1 | async-start | bytes 33554432 | tf_op jit(solution)/shard_map/all_to_all | solution.py:63
  36.1 580.4 %all-gather.2.cloned.1.call-start = ((), (), s32[]{:S(2)}) async-start(), calls=%async_computation.3 | async-start | bytes 4718592 | tf_op jit(solution)/shard_map/all_gather | solution.py:87
  397.8 10.9 %copy-start.1 = (bf16[256,1024]{1,0:T(8,128)(2,1)S(1)}, bf16[256,1024]{1,0:T(8,128)(2,1)}, u32[]{:S(2)}) copy-start(bf16[256,1024]{1,0:T(8,128)(2,1)} %param.8) | copy-start | bytes 1572868
  397.8 10.9 %copy-start.3 = (bf16[256,256]{1,0:T(8,128)(2,1)S(1)}, bf16[256,256]{1,0:T(8,128)(2,1)}, u32[]{:S(2)}) copy-start(bf16[256,256]{1,0:T(8,128)(2,1)} %param.9) | copy-start | bytes 393220
  543.9 122.7 %reduce-scatter.2.cloned.1.call-start = ((), (), s32[]{:S(2)}) async-start(), calls=%async_computation.4 | async-start | bytes 5242880 | tf_op jit(solution)/shard_map/reduce_scatter | solution.py:89
  668.9 41.2 %collective-permute-start = (bf16[256,1024]{1,0:T(8,128)(2,1)}, bf16[256,1024]{1,0:T(8,128)(2,1)S(1)}, u32[]{:S(2)}, u32[]{:S(2)}) collective-permute-start(bf16[256,1024]{1,0:T(8,128)(2,1)} %get-tuple-element.99), channel_id=1, source_target_pairs={{0,0},{1,8},{2,16},{3,24},{4,4},{5,12},{6,20},{7,28},{8,1},{9,9},{... | collective-permute-start | bytes 1572872 | tf_op jit(solution)/shard_map/ppermute | solution.py:104
  674.3 47.5 %collective-permute-start.1 = (bf16[256,1024]{1,0:T(8,128)(2,1)}, bf16[256,1024]{1,0:T(8,128)(2,1)S(1)}, u32[]{:S(2)}, u32[]{:S(2)}) collective-permute-start(bf16[256,1024]{1,0:T(8,128)(2,1)} %get-tuple-element.98), channel_id=1, source_target_pairs={{0,4},{1,12},{2,20},{3,28},{4,0},{5,8},{6,16},{7,24},{8,5},{9,13},... | collective-permute-start | bytes 1572872 | tf_op jit(solution)/shard_map/ppermute | solution.py:104
  710.2 11.6 %copy-start.2 = (bf16[256,2048]{1,0:T(8,128)(2,1)}, bf16[256,2048]{1,0:T(8,128)(2,1)S(1)}, u32[]{:S(2)}) copy-start(bf16[256,2048]{1,0:T(8,128)(2,1)S(1)} %constant_dynamic-update-slice_fusion.1) | copy-start | bytes 3145732
Sparse Core Ops, SparseCore 0:
  544.1 72.3 all-gather.1
  625.0 41.6 reduce-scatter.1

commit v2 on v1

v2 whole, which is shorter than its diff:
```python
import math

import jax
import jax.numpy as jnp
from jax import lax
from jax.experimental import pallas as pl
from jax.experimental.pallas import tpu as pltpu
from jax.sharding import PartitionSpec as P

HD = 128
QLEN = 128
PLEN = 512
FLOOR = -1e30


def slot_kernel(rows_ref, pick_ref, q_ref, kv_ref, acc_ref, peak_ref, total_ref):
    heads = q_ref.shape[2] // HD
    keys = kv_ref[0, :, 0:HD]
    values = kv_ref[0, :, HD:2 * HD]
    for h in range(heads):
        q = q_ref[0, :, h * HD:(h + 1) * HD]
        s = lax.dot_general(
            q, keys, (((1,), (1,)), ((), ())), preferred_element_type=jnp.float32
        ) / math.sqrt(HD)
        m = jnp.max(s, axis=1, keepdims=True)
        p = jnp.exp(s - m)
        peak_ref[0, h] = m
        total_ref[0, h] = jnp.sum(p, axis=1, keepdims=True)
        acc_ref[0, h] = jnp.dot(
            p.astype(jnp.bfloat16), values, preferred_element_type=jnp.float32
        )


def slot_attention(rows, pick, q_blocks, store):
    n_slots = rows.shape[0]
    width = q_blocks.shape[2]
    heads = width // HD
    flops = n_slots * heads * QLEN * PLEN * HD * 4
    return pl.pallas_call(
        slot_kernel,
        out_shape=(
            jax.ShapeDtypeStruct((n_slots, heads, QLEN, HD), jnp.float32),
            jax.ShapeDtypeStruct((n_slots, heads, QLEN, 1), jnp.float32),
            jax.ShapeDtypeStruct((n_slots, heads, QLEN, 1), jnp.float32),
        ),
        grid_spec=pltpu.PrefetchScalarGridSpec(
            num_scalar_prefetch=2,
            grid=(n_slots,),
            in_specs=[
                pl.BlockSpec((1, QLEN, width), lambda i, r, p: (p[i], 0, 0)),
                pl.BlockSpec((1, PLEN, 2 * HD), lambda i, r, p: (r[i], 0, 0)),
            ],
            out_specs=[
                pl.BlockSpec((1, heads, QLEN, HD), lambda i, r, p: (i, 0, 0, 0)),
                pl.BlockSpec((1, heads, QLEN, 1), lambda i, r, p: (i, 0, 0, 0)),
                pl.BlockSpec((1, heads, QLEN, 1), lambda i, r, p: (i, 0, 0, 0)),
            ],
        ),
        cost_estimate=pl.CostEstimate(
            flops=flops,
            transcendentals=n_slots * heads * QLEN * PLEN,
            bytes_accessed=n_slots * (QLEN * width * 2 + PLEN * 2 * HD * 2 + heads * QLEN * HD * 4),
        ),
    )(rows, pick, q_blocks, store)


def own_part(query_rows, own_rows):
    count, tokens, width = query_rows.shape
    heads = width // HD
    q = query_rows.reshape(count, tokens, heads, HD)
    keys = own_rows[:, :, 0:HD]
    values = own_rows[:, :, HD:2 * HD]
    s = jnp.einsum("qthd,qld->qhtl", q, keys, preferred_element_type=jnp.float32) / math.sqrt(HD)
    visible = jnp.arange(tokens)[None, :] <= jnp.arange(tokens)[:, None]
    s = jnp.where(visible, s, -jnp.inf)
    m = jnp.max(s, axis=-1, keepdims=True)
    p = jnp.exp(s - m)
    total = jnp.sum(p, axis=-1, keepdims=True)
    acc = jnp.einsum(
        "qhtl,qld->qhtd", p.astype(jnp.bfloat16), values, preferred_element_type=jnp.float32
    )
    return acc, m, total


def shards(queries, own_kv, passage_store, out_weight, passage_slot, retrieved):
    n_cache = lax.axis_size("cache")
    store_count = passage_store.shape[0]
    slot_total = passage_slot.shape[0]
    query_count, per_query = retrieved.shape
    width = queries.shape[1]
    heads = width // HD
    wanted_count = query_count * per_query
    capacity = max(2, (2 * wanted_count + n_cache - 1) // n_cache)
    wanted = retrieved.reshape(wanted_count)
    id_match = wanted[:, None] == jnp.arange(slot_total, dtype=jnp.int32)[None, :]
    store_slots = jnp.sum(jnp.where(id_match, passage_slot[None, :], 0), axis=1)
    owners = store_slots // store_count
    local_rows = store_slots % store_count
    places = jnp.arange(wanted_count, dtype=jnp.int32)
    earlier = (owners[None, :] == owners[:, None]) & (places[None, :] < places[:, None])
    order_rank = jnp.sum(earlier, axis=1)
    flat_slot = owners * capacity + order_rank
    slot_match = flat_slot[:, None] == jnp.arange(n_cache * capacity, dtype=jnp.int32)[None, :]
    send_rows = jnp.sum(jnp.where(slot_match, local_rows[:, None], 0), axis=0)
    send_query = jnp.sum(jnp.where(slot_match, (places // per_query)[:, None], 0), axis=0)
    send_valid = jnp.sum(slot_match.astype(jnp.int32), axis=0)
    info = jnp.stack([send_rows, send_query, send_valid], axis=0).reshape(3, n_cache, capacity)
    asked = lax.all_to_all(info, "cache", split_axis=1, concat_axis=1, tiled=True)
    asked_rows = asked[0].reshape(n_cache * capacity)
    asked_query = asked[1]
    asked_valid = asked[2] > 0
    requester = jnp.arange(n_cache, dtype=jnp.int32)[:, None]
    pick = (requester * query_count + asked_query).reshape(n_cache * capacity)

    everyone_q = lax.all_gather(queries, "cache", axis=0, tiled=True)
    q_blocks = everyone_q.reshape(n_cache * query_count, QLEN, width)
    acc, peak, total = slot_attention(asked_rows, pick, q_blocks, passage_store)
    acc = acc.reshape(n_cache, capacity, 1, heads, QLEN, HD)
    peak = peak.reshape(n_cache, capacity, 1, heads, QLEN, 1)
    total = total.reshape(n_cache, capacity, 1, heads, QLEN, 1)
    chosen = asked_valid[:, :, None] & (
        asked_query[:, :, None] == jnp.arange(query_count, dtype=jnp.int32)[None, None, :]
    )
    chosen = chosen[:, :, :, None, None, None]
    merged_peak = jnp.max(jnp.where(chosen, peak, FLOOR), axis=1)
    scale = jnp.where(chosen, jnp.exp(peak - merged_peak[:, None]), 0.0)
    merged_acc = jnp.sum(scale * acc, axis=1)
    merged_total = jnp.sum(scale * total, axis=1)
    stats = jnp.concatenate([merged_peak, merged_total], axis=-1)
    back_acc = lax.all_to_all(
        merged_acc.astype(jnp.bfloat16), "cache", split_axis=0, concat_axis=0, tiled=True
    )
    back_stats = lax.all_to_all(stats, "cache", split_axis=0, concat_axis=0, tiled=True)

    own_acc, own_peak, own_total = own_part(
        queries.reshape(query_count, QLEN, width),
        own_kv.reshape(query_count, QLEN, own_kv.shape[1]),
    )
    far_peak = back_stats[..., 0:1]
    far_total = back_stats[..., 1:2]
    top = jnp.maximum(jnp.max(far_peak, axis=0), own_peak)
    far_scale = jnp.exp(far_peak - top[None])
    own_scale = jnp.exp(own_peak - top)
    numer = jnp.sum(far_scale * back_acc.astype(jnp.float32), axis=0) + own_scale * own_acc
    denom = jnp.sum(far_scale * far_total, axis=0) + own_scale * own_total
    attended = (numer / denom).astype(jnp.bfloat16)
    attended = jnp.transpose(attended, (0, 2, 1, 3)).reshape(query_count * QLEN, width)
    return project(attended, out_weight)


def project(attended, out_weight):
    n_cache = lax.axis_size("cache")
    n_stream = lax.axis_size("stream")
    rows = attended.shape[0]
    group = n_cache // n_stream
    everyone = lax.all_gather(attended, "cache", axis=0, tiled=True)
    partial_sums = jnp.dot(everyone, out_weight, preferred_element_type=jnp.float32)
    reduced = lax.psum_scatter(
        partial_sums.astype(jnp.bfloat16), "stream", scatter_dimension=0, tiled=True
    )
    me = lax.axis_index("cache")
    width = reduced.shape[1]
    out = jnp.zeros((rows, group * width), reduced.dtype)
    for r in range(group):
        take = (me % group + r) % group
        piece = lax.dynamic_slice_in_dim(reduced, take * rows, rows, axis=0)
        perm = []
        for c in range(n_cache):
            for s in range(n_stream):
                dst_c = s * group + (c % group + r) % group
                dst_s = c // group
                perm.append((c * n_stream + s, dst_c * n_stream + dst_s))
        got = lax.ppermute(piece, ("cache", "stream"), perm)
        put = (me - r) % group
        out = lax.dynamic_update_slice_in_dim(out, got, put * width, axis=1)
    return out


def solution(mesh):
    return jax.shard_map(
        shards,
        mesh=mesh,
        in_specs=(
            P("cache", "stream"),
            P("cache", "stream"),
            P("cache", None, "stream"),
            P("stream", "cache"),
            P(),
            P("cache", None),
        ),
        out_specs=P("cache", "stream"),
        check_vma=False,
    )
```

time: 731 us -> 586 us (0.80)
  waiting for transfers between devices: 522 us -> 319 us
  Pallas kernels: 0 us -> 150 us
  matrix products: 70.2 us -> 9.57 us
  local copies, waits for them, and re-layouts: 61.7 us -> 7.69 us
  other arithmetic: 37.4 us -> 62.4 us
  blocking collectives: 12.1 us -> 0 us
  starting transfers between devices: 12.9 us -> 22.2 us
    all_to_all x1 -> x3, waiting for transfers between devices: 362 us -> 98.2 us  [the longest x1 91.7 us: shards(): lax.all_to_all(merged_acc.astype(jnp.bfloat16), 'cache', split_axis=0, co...]
    pallas_call x0 -> x1, Pallas kernels: none -> 150 us  [slot_attention(): pl.pallas_call(slot_kernel, out_shape=(jax.ShapeDtypeStruct((n_slots, hea...]
    dot_general x4 -> x2, matrix products: 61.8 us -> 1.24 us  [the longest x1 0.92 us: own_part(): jnp.einsum('qhtl,qld->qhtd', p.astype(jnp.bfloat16), values, preferred_el...]
    all_gather x0 -> x1, waiting for transfers between devices: none -> 60.3 us  [shards(): everyone_q = lax.all_gather(queries, 'cache', axis=0, tiled=True)]
    pallas_call x0 -> x2, other arithmetic: none -> 30.5 us  [slot_attention(): pl.pallas_call(slot_kernel, out_shape=(jax.ShapeDtypeStruct((n_slots, hea...]
    dynamic_slice x12 -> x0, local copies, waits for them, and re-layouts: 22.3 us -> none  [shards(): lax.map(per_query_block, (queries.reshape(query_count, QLEN, queries.shap...]
    gather x2 -> x0, local copies, waits for them, and re-layouts: 20.4 us -> none  [the longest x1 10.9 us: shards(): picked = arrived.reshape(n_cache * capacity, PLEN, width_kv)[flat_slot]]
    concatenate x4 -> x1, local copies, waits for them, and re-layouts: 12.9 us -> 0.66 us  [shards(): stats = jnp.concatenate([merged_peak, merged_total], axis=-1)]
  transfers between devices with their start and end apart: 5 -> 8, of which waited for: 5 -> 7; matrix products, arithmetic and copies ran while one was open for 0% -> 5% of each run, Pallas kernels for 0% -> 0%
where the time goes in v2:
time: 586 us; the launch traced here: 585 us
  waiting for transfers between devices  319 us (54%)
  Pallas kernels  150 us (26%)
  other arithmetic  62.4 us (11%)
  starting transfers between devices  22.2 us (4%)
  between operations  13.4 us (2%)
  matrix products  9.57 us (2%)
  local copies, waits for them, and re-layouts  7.69 us (1%)
    pallas_call x1, Pallas kernels, slot_attention(): pl.pallas_call(slot_kernel, out_shape=(jax.ShapeDtypeStruct((n_slots, hea...  150 us
    all_to_all x1, waiting for transfers between devices, shards(): lax.all_to_all(merged_acc.astype(jnp.bfloat16), 'cache', split_axis=0, co...  91.7 us
    all_gather x1, waiting for transfers between devices, project(): everyone = lax.all_gather(attended, 'cache', axis=0, tiled=True)  72.5 us
    all_gather x1, waiting for transfers between devices, shards(): everyone_q = lax.all_gather(queries, 'cache', axis=0, tiled=True)  60.3 us
    ppermute x2, waiting for transfers between devices, project(): got = lax.ppermute(piece, ('cache', 'stream'), perm)  45.9 us
    reduce_scatter x1, waiting for transfers between devices, project(): lax.psum_scatter(partial_sums.astype(jnp.bfloat16), 'stream', scatter_dim...  41.7 us
    pallas_call x2, other arithmetic, slot_attention(): pl.pallas_call(slot_kernel, out_shape=(jax.ShapeDtypeStruct((n_slots, hea...  30.5 us
    reduce_sum x1, other arithmetic, shards(): merged_acc = jnp.sum(scale * acc, axis=1)  24.8 us
  transfers between devices with their start and end apart: 8, of which 7 were waited for; matrix products, arithmetic and copies ran while one was open for 5% of the time, Pallas kernels for 0%

profile of v2, /device:TPU:4, one launch (start us, length us, event | category | flops | bytes accessed | tf_op | source)
XLA Modules:
  0.0 584.8 jit_solution(13566067598275376073)
XLA Ops:
  6.5 0.0 copy-start
  6.5 0.0 all-gather.3.cloned.1.call-start
  6.5 0.7 all-gather.3.cloned.1.call-update
  7.3 0.8 eq.69
  8.0 0.8 select_reduce_fusion.3
  8.9 0.2 convert_reduce_fusion.1
  9.1 0.1 select_reduce_fusion.2
  9.2 0.1 stack.12
  9.2 0.1 stack.13
  9.3 0.1 stack.14
  9.4 0.6 copy.18
  10.0 5.8 all-to-all-start
  15.8 0.1 add.93
  15.9 0.1 add.94
  16.0 6.5 %all-to-all-done = s32[3,8,8]{2,0,1:T(4,128)S(1)} async-done(((s32[3,8,8]{2,0,1:T(4,128)}), s32[3,8,8]{2,0,1:T(4,128)S(1)}, u32[]{:S(2)}, u32[]{:S(2)}) %all-to-all-start) | async-done | bytes 800 | tf_op jit(solution)/shard_map/all_to_all | solution.py:108
  22.5 0.1 squeeze.4
  22.6 0.6 reshape_squeeze.3.rows_ref
  23.2 0.5 add.95.pick_ref
  23.7 0.1 fusion.13
  23.8 60.3 %all-gather.3.cloned.1.call-done = bf16[2048,1024]{1,0:T(8,128)(2,1)} async-done(((bf16[256,1024]{1,0:T(8,128)(2,1)}), bf16[2048,1024]{1,0:T(8,128)(2,1)}) %all-gather.3.cloned.1.call-update) | async-done | bytes 4194320 | tf_op jit(solution)/shard_map/all_gather | solution.py:115
  84.1 150.2 %shard_map.64 = (f32[64,8,128,128]{3,2,1,0:T(8,128)}, f32[64,8,128,1]{3,2,1,0:T(8,128)}, f32[64,8,128,1]{3,2,1,0:T(8,128)}) custom-call(s32[64]{0:T(128)} %reshape_squeeze.3.rows_ref, s32[64]{0:T(128)} %add.95.pick_ref, bf16[16,128,1024]{2,1,0:T(8,128)(2,1)} %bitcast.81, bf16[16,512,256]{2,1,0:T(8,128)(2,1)} %kv_ref.1), custom_call_target="tpu_custom_call" | custom-call | flops 17179869184 | bytes 67108864 | tf_op jit(solution)/shard_map/pallas_call | solution.py:39
  234.3 15.3 %reduce.5 = f32[64,8,128]{2,1,0:T(8,128)S(1)} reduce(f32[64,8,128,1]{3,2,1,0:T(8,128)} %get-tuple-element.8, f32[]{:T(128)} %constant.98), dimensions={3}, to_apply=%get-tuple-element.8.reduce_sub_computation | reduce | bytes 524292 | tf_op jit(solution)/shard_map/pallas_call | solution.py:39
  249.5 15.3 %reduce.6 = f32[64,8,128]{2,1,0:T(8,128)S(1)} reduce(f32[64,8,128,1]{3,2,1,0:T(8,128)} %get-tuple-element.9, f32[]{:T(128)} %constant.98), dimensions={3}, to_apply=%get-tuple-element.9.reduce_sub_computation | reduce | bytes 524292 | tf_op jit(solution)/shard_map/pallas_call | solution.py:39
  264.8 0.2 select_reduce_fusion
  265.0 0.2 exponential_select_fusion
  265.2 0.2 multiply_reduce_fusion.2
  265.5 0.7 copy.21
  266.1 3.4 all-to-all-start.1
  269.5 24.8 %multiply_reduce_fusion = bf16[8,2,8,128,128]{4,3,2,1,0:T(8,128)(2,1)} fusion(f32[8,8,8,128,128]{4,3,2,1,0:T(8,128)} %bitcast.65, f32[8,8,2,8,128]{4,3,2,1,0:T(8,128)S(1)} %exponential_select_fusion), kind=kLoop, calls=%fused_computation | loop fusion | flops 31457280 | bytes 38273024 | tf_op jit(solution)/shard_map/reduce_sum | solution.py:127
  294.3 0.0 copy-start.1
  294.3 0.0 copy-start.3
  294.3 0.0 all-to-all-done.1
  294.3 6.1 %all-to-all-start.2 = ((bf16[8,2,8,128,128]{4,3,2,1,0:T(8,128)(2,1)}), bf16[8,2,8,128,128]{4,3,2,1,0:T(8,128)(2,1)}, u32[]{:S(2)}, u32[]{:S(2)}) async-start(bf16[8,2,8,128,128]{4,3,2,1,0:T(8,128)(2,1)} %multiply_reduce_fusion), calls=%async_computation.2 | async-start | bytes 8388608 | tf_op jit(solution)/shard_map/all_to_all | solution.py:130
  300.3 0.0 all-gather.5.cloned.1.call-start
  300.4 0.0 copy-done.1
  300.4 0.1 copy.30
  300.5 0.0 copy-done.3
  300.5 0.3 fusion.19
  300.9 0.2 fusion.6
  301.1 91.7 %all-to-all-done.2 = bf16[8,2,8,128,128]{4,3,2,1,0:T(8,128)(2,1)} async-done(((bf16[8,2,8,128,128]{4,3,2,1,0:T(8,128)(2,1)}), bf16[8,2,8,128,128]{4,3,2,1,0:T(8,128)(2,1)}, u32[]{:S(2)}, u32[]{:S(2)}) %all-to-all-start.2) | async-done | bytes 4194336 | tf_op jit(solution)/shard_map/all_to_all | solution.py:130
  392.8 4.5 multiply_reduce_fusion.1
  397.3 0.9 fusion.5
  398.2 0.3 copy.24
  398.6 0.9 copy.37
  399.5 0.0 all-gather.5.cloned.1.call-update
  399.5 0.0 reduce-scatter.2.cloned.1.call-start
  399.5 72.5 %all-gather.5.cloned.1.call-done = bf16[2048,1024]{1,0:T(8,128)(2,1)} async-done(((bf16[256,1024]{1,0:T(8,128)(2,1)}), bf16[2048,1024]{1,0:T(8,128)(2,1)}) %all-gather.5.cloned.1.call-update) | async-done | bytes 4194320 | tf_op jit(solution)/shard_map/all_gather | solution.py:156
  472.1 0.0 copy-done
  472.1 8.3 %convolution_convert_fusion = bf16[2048,1024]{1,0:T(8,128)(2,1)} fusion(bf16[2048,1024]{1,0:T(8,128)(2,1)} %all-gather.5.cloned.1.call-done, bf16[1024,1024]{1,0:T(8,128)(2,1)S(1)} %copy-done), kind=kOutput, calls=%fused_computation.2 | convolution fusion | flops 4297064448 | bytes 10485760 | tf_op jit(solution)/shard_map/dot_general | solution.py:157
  480.4 0.0 reduce-scatter.2.cloned.1.call-update
  480.5 41.7 %reduce-scatter.2.cloned.1.call-done = bf16[512,1024]{1,0:T(8,128)(2,1)} async-done(((bf16[2048,1024]{1,0:T(8,128)(2,1)}), bf16[512,1024]{1,0:T(8,128)(2,1)}) %reduce-scatter.2.cloned.1.call-update) | async-done | bytes 1048592 | tf_op jit(solution)/shard_map/reduce_scatter | solution.py:158
  522.2 2.2 constant_dynamic-slice_fusion
  524.5 5.5 collective-permute-start
  529.9 1.5 collective-permute-start.1
  531.4 34.2 %collective-permute-done = bf16[256,1024]{1,0:T(8,128)(2,1)S(1)} collective-permute-done((bf16[256,1024]{1,0:T(8,128)(2,1)}, bf16[256,1024]{1,0:T(8,128)(2,1)S(1)}, u32[]{:S(2)}, u32[]{:S(2)}) %collective-permute-start) | collective-permute-done | bytes 524320 | tf_op jit(solution)/shard_map/ppermute | solution.py:173
  565.6 0.1 broadcast_in_dim.99
  565.7 0.1 constant_dynamic-update-slice_fusion.1
  565.8 0.0 copy-start.2
  565.8 11.6 %collective-permute-done.1 = bf16[256,1024]{1,0:T(8,128)(2,1)S(1)} collective-permute-done((bf16[256,1024]{1,0:T(8,128)(2,1)}, bf16[256,1024]{1,0:T(8,128)(2,1)S(1)}, u32[]{:S(2)}, u32[]{:S(2)}) %collective-permute-start.1) | collective-permute-done | bytes 524320 | tf_op jit(solution)/shard_map/ppermute | solution.py:173
  577.4 0.0 copy-done.2
  577.4 0.8 constant_dynamic-update-slice_fusion
  (12 shorter events, 0.1 us)
Async XLA Ops:
  6.5 465.6 %copy-start = (bf16[1024,1024]{1,0:T(8,128)(2,1)S(1)}, bf16[1024,1024]{1,0:T(8,128)(2,1)}, u32[]{:S(2)}) copy-start(bf16[1024,1024]{1,0:T(8,128)(2,1)} %param.9) | copy-start | bytes 6291460
  6.5 77.6 %all-gather.3.cloned.1.call-start = ((), (), s32[]{:S(2)}) async-start(), calls=%async_computation.4 | async-start | bytes 4718592 | tf_op jit(solution)/shard_map/all_gather | solution.py:115
  10.0 12.5 %all-to-all-start = ((s32[3,8,8]{2,0,1:T(4,128)}), s32[3,8,8]{2,0,1:T(4,128)S(1)}, u32[]{:S(2)}, u32[]{:S(2)}) async-start(s32[3,8,8]{2,0,1:T(4,128)} %copy.18), calls=%async_computation | async-start | bytes 32768 | tf_op jit(solution)/shard_map/all_to_all | solution.py:108
  266.1 28.1 %all-to-all-start.1 = ((f32[8,2,8,128,2]{3,2,1,4,0:T(8,128)}), f32[8,2,8,128,2]{3,2,1,4,0:T(8,128)S(1)}, u32[]{:S(2)}, u32[]{:S(2)}) async-start(f32[8,2,8,128,2]{3,2,1,4,0:T(8,128)} %copy.21), calls=%async_computation.1 | async-start | bytes 262144 | tf_op jit(solution)/shard_map/all_to_all | solution.py:133
  294.3 6.1 %copy-start.1 = (bf16[256,1024]{1,0:T(8,128)(2,1)S(1)}, bf16[256,1024]{1,0:T(8,128)(2,1)}, u32[]{:S(2)}) copy-start(bf16[256,1024]{1,0:T(8,128)(2,1)} %param.6) | copy-start | bytes 1572868
  294.3 6.2 %copy-start.3 = (bf16[256,256]{1,0:T(8,128)(2,1)S(1)}, bf16[256,256]{1,0:T(8,128)(2,1)}, u32[]{:S(2)}) copy-start(bf16[256,256]{1,0:T(8,128)(2,1)} %param.7) | copy-start | bytes 393220
  294.3 98.5 %all-to-all-start.2 = ((bf16[8,2,8,128,128]{4,3,2,1,0:T(8,128)(2,1)}), bf16[8,2,8,128,128]{4,3,2,1,0:T(8,128)(2,1)}, u32[]{:S(2)}, u32[]{:S(2)}) async-start(bf16[8,2,8,128,128]{4,3,2,1,0:T(8,128)(2,1)} %multiply_reduce_fusion), calls=%async_computation.2 | async-start | bytes 8388608 | tf_op jit(solution)/shard_map/all_to_all | solution.py:130
  300.3 171.7 %all-gather.5.cloned.1.call-start = ((), (), s32[]{:S(2)}) async-start(), calls=%async_computation.5 | async-start | bytes 4718592 | tf_op jit(solution)/shard_map/all_gather | solution.py:156
  399.5 122.7 %reduce-scatter.2.cloned.1.call-start = ((), (), s32[]{:S(2)}) async-start(), calls=%async_computation.6 | async-start | bytes 5242880 | tf_op jit(solution)/shard_map/reduce_scatter | solution.py:158
  524.5 41.2 %collective-permute-start = (bf16[256,1024]{1,0:T(8,128)(2,1)}, bf16[256,1024]{1,0:T(8,128)(2,1)S(1)}, u32[]{:S(2)}, u32[]{:S(2)}) collective-permute-start(bf16[256,1024]{1,0:T(8,128)(2,1)} %get-tuple-element.17), channel_id=1, source_target_pairs={{0,0},{1,8},{2,16},{3,24},{4,4},{5,12},{6,20},{7,28},{8,1},{9,9},{... | collective-permute-start | bytes 1572872 | tf_op jit(solution)/shard_map/ppermute | solution.py:173
  529.9 47.5 %collective-permute-start.1 = (bf16[256,1024]{1,0:T(8,128)(2,1)}, bf16[256,1024]{1,0:T(8,128)(2,1)S(1)}, u32[]{:S(2)}, u32[]{:S(2)}) collective-permute-start(bf16[256,1024]{1,0:T(8,128)(2,1)} %get-tuple-element.16), channel_id=1, source_target_pairs={{0,4},{1,12},{2,20},{3,28},{4,0},{5,8},{6,16},{7,24},{8,5},{9,13},... | collective-permute-start | bytes 1572872 | tf_op jit(solution)/shard_map/ppermute | solution.py:173
  565.8 11.6 %copy-start.2 = (bf16[256,2048]{1,0:T(8,128)(2,1)}, bf16[256,2048]{1,0:T(8,128)(2,1)S(1)}, u32[]{:S(2)}) copy-start(bf16[256,2048]{1,0:T(8,128)(2,1)S(1)} %constant_dynamic-update-slice_fusion.1) | copy-start | bytes 3145732
Sparse Core Ops, SparseCore 0:
  9.5 74.5 all-gather.2
  399.6 72.4 all-gather.4
  480.6 41.6 reduce-scatter.1

commit v3 on v2

--- a/solution.py
+++ b/solution.py
@@ -13,55 +13,85 @@
 FLOOR = -1e30
 
 
-def slot_kernel(rows_ref, pick_ref, q_ref, kv_ref, acc_ref, peak_ref, total_ref):
+def slot_kernel(rows_ref, pick_ref, valid_ref, which_ref, q_ref, kv_ref,
+                acc_out, peak_out, total_out, acc_sc, peak_sc, total_sc):
+    r = pl.program_id(0)
+    k = pl.program_id(1)
+    cap = pl.num_programs(1)
     heads = q_ref.shape[2] // HD
-    keys = kv_ref[0, :, 0:HD]
-    values = kv_ref[0, :, HD:2 * HD]
-    for h in range(heads):
-        q = q_ref[0, :, h * HD:(h + 1) * HD]
+
+    @pl.when(k == 0)
+    def _():
+        acc_sc[...] = jnp.zeros_like(acc_sc)
+        peak_sc[...] = jnp.full_like(peak_sc, FLOOR)
+        total_sc[...] = jnp.zeros_like(total_sc)
+
+    i = r * cap + k
+
+    @pl.when(valid_ref[i] > 0)
+    def _():
+        j = which_ref[i]
+        keys = kv_ref[0, :, 0:HD]
+        values = kv_ref[0, :, HD:2 * HD]
+        q = jnp.concatenate([q_ref[0, :, h * HD:(h + 1) * HD] for h in range(heads)], axis=0)
         s = lax.dot_general(
             q, keys, (((1,), (1,)), ((), ())), preferred_element_type=jnp.float32
-        ) / math.sqrt(HD)
-        m = jnp.max(s, axis=1, keepdims=True)
-        p = jnp.exp(s - m)
-        peak_ref[0, h] = m
-        total_ref[0, h] = jnp.sum(p, axis=1, keepdims=True)
-        acc_ref[0, h] = jnp.dot(
+        ) * (1.0 / math.sqrt(HD))
+        old = peak_sc[j]
+        new = jnp.maximum(old, jnp.max(s, axis=1, keepdims=True))
+        fade = jnp.exp(old - new)
+        p = jnp.exp(s - new)
+        total_sc[j] = fade * total_sc[j] + jnp.sum(p, axis=1, keepdims=True)
+        acc_sc[j] = fade * acc_sc[j] + jnp.dot(
             p.astype(jnp.bfloat16), values, preferred_element_type=jnp.float32
         )
-
-
-def slot_attention(rows, pick, q_blocks, store):
-    n_slots = rows.shape[0]
+        peak_sc[j] = new
+
+    @pl.when(k == cap - 1)
+    def _():
+        acc_out[0] = acc_sc[...].astype(acc_out.dtype)
+        peak_out[0] = peak_sc[...]
+        total_out[0] = total_sc[...]
+
+
+def slot_attention(rows, pick, valid, which, q_blocks, store, n_req, cap, n_query):
     width = q_blocks.shape[2]
     heads = width // HD
+    n_slots = n_req * cap
+    stacked = heads * QLEN
     flops = n_slots * heads * QLEN * PLEN * HD * 4
     return pl.pallas_call(
         slot_kernel,
         out_shape=(
-            jax.ShapeDtypeStruct((n_slots, heads, QLEN, HD), jnp.float32),
-            jax.ShapeDtypeStruct((n_slots, heads, QLEN, 1), jnp.float32),
-            jax.ShapeDtypeStruct((n_slots, heads, QLEN, 1), jnp.float32),
+            jax.ShapeDtypeStruct((n_req, n_query, stacked, HD), jnp.bfloat16),
+            jax.ShapeDtypeStruct((n_req, n_query, stacked, 1), jnp.float32),
+            jax.ShapeDtypeStruct((n_req, n_query, stacked, 1), jnp.float32),
         ),
         grid_spec=pltpu.PrefetchScalarGridSpec(
-            num_scalar_prefetch=2,
-            grid=(n_slots,),
+            num_scalar_prefetch=4,
+            grid=(n_req, cap),
             in_specs=[
-                pl.BlockSpec((1, QLEN, width), lambda i, r, p: (p[i], 0, 0)),
-                pl.BlockSpec((1, PLEN, 2 * HD), lambda i, r, p: (r[i], 0, 0)),
+                pl.BlockSpec((1, QLEN, width), lambda r, k, rw, pk, vd, wh: (pk[r * cap + k], 0, 0)),
+                pl.BlockSpec((1, PLEN, 2 * HD), lambda r, k, rw, pk, vd, wh: (rw[r * cap + k], 0, 0)),
             ],
             out_specs=[
-                pl.BlockSpec((1, heads, QLEN, HD), lambda i, r, p: (i, 0, 0, 0)),
-                pl.BlockSpec((1, heads, QLEN, 1), lambda i, r, p: (i, 0, 0, 0)),
-                pl.BlockSpec((1, heads, QLEN, 1), lambda i, r, p: (i, 0, 0, 0)),
+                pl.BlockSpec((1, n_query, stacked, HD), lambda r, k, rw, pk, vd, wh: (r, 0, 0, 0)),
+                pl.BlockSpec((1, n_query, stacked, 1), lambda r, k, rw, pk, vd, wh: (r, 0, 0, 0)),
+                pl.BlockSpec((1, n_query, stacked, 1), lambda r, k, rw, pk, vd, wh: (r, 0, 0, 0)),
+            ],
+            scratch_shapes=[
+                pltpu.VMEM((n_query, stacked, HD), jnp.float32),
+                pltpu.VMEM((n_query, stacked, 1), jnp.float32),
+                pltpu.VMEM((n_query, stacked, 1), jnp.float32),
             ],
         ),
         cost_estimate=pl.CostEstimate(
             flops=flops,
             transcendentals=n_slots * heads * QLEN * PLEN,
-            bytes_accessed=n_slots * (QLEN * width * 2 + PLEN * 2 * HD * 2 + heads * QLEN * HD * 4),
-        ),
-    )(rows, pick, q_blocks, store)
+            bytes_accessed=n_slots * (QLEN * width * 2 + PLEN * 2 * HD * 2)
+            + n_req * n_query * stacked * HD * 2,
+        ),
+    )(rows, pick, valid, which, q_blocks, store)
 
 
 def own_part(query_rows, own_rows):
@@ -108,27 +138,21 @@
     asked = lax.all_to_all(info, "cache", split_axis=1, concat_axis=1, tiled=True)
     asked_rows = asked[0].reshape(n_cache * capacity)
     asked_query = asked[1]
-    asked_valid = asked[2] > 0
     requester = jnp.arange(n_cache, dtype=jnp.int32)[:, None]
     pick = (requester * query_count + asked_query).reshape(n_cache * capacity)
 
     everyone_q = lax.all_gather(queries, "cache", axis=0, tiled=True)
     q_blocks = everyone_q.reshape(n_cache * query_count, QLEN, width)
-    acc, peak, total = slot_attention(asked_rows, pick, q_blocks, passage_store)
-    acc = acc.reshape(n_cache, capacity, 1, heads, QLEN, HD)
-    peak = peak.reshape(n_cache, capacity, 1, heads, QLEN, 1)
-    total = total.reshape(n_cache, capacity, 1, heads, QLEN, 1)
-    chosen = asked_valid[:, :, None] & (
-        asked_query[:, :, None] == jnp.arange(query_count, dtype=jnp.int32)[None, None, :]
-    )
-    chosen = chosen[:, :, :, None, None, None]
-    merged_peak = jnp.max(jnp.where(chosen, peak, FLOOR), axis=1)
-    scale = jnp.where(chosen, jnp.exp(peak - merged_peak[:, None]), 0.0)
-    merged_acc = jnp.sum(scale * acc, axis=1)
-    merged_total = jnp.sum(scale * total, axis=1)
-    stats = jnp.concatenate([merged_peak, merged_total], axis=-1)
+    merged_acc, merged_peak, merged_total = slot_attention(
+        asked_rows, pick, asked[2].reshape(n_cache * capacity), asked_query.reshape(n_cache * capacity),
+        q_blocks, passage_store, n_cache, capacity, query_count,
+    )
+    merged_acc = merged_acc.reshape(n_cache, query_count, heads, QLEN, HD)
+    stats = jnp.concatenate([merged_peak, merged_total], axis=-1).reshape(
+        n_cache, query_count, heads, QLEN, 2
+    )
     back_acc = lax.all_to_all(
-        merged_acc.astype(jnp.bfloat16), "cache", split_axis=0, concat_axis=0, tiled=True
+        merged_acc, "cache", split_axis=0, concat_axis=0, tiled=True
     )
     back_stats = lax.all_to_all(stats, "cache", split_axis=0, concat_axis=0, tiled=True)
 

time: 586 us -> 585 us (level)
  blocking collectives: 0 us -> 120 us
  Pallas kernels: 150 us -> 80.8 us
  other arithmetic: 62.4 us -> 6.4 us
  local copies, waits for them, and re-layouts: 7.69 us -> 18.1 us
    all_to_all x0 -> x1, blocking collectives: none -> 120 us  [shards(): lax.all_to_all(stats, 'cache', split_axis=0, concat_axis=0, tiled=True)]
    pallas_call x1, Pallas kernels: 150 us -> 80.8 us  [slot_attention(): pl.pallas_call(slot_kernel, out_shape=(jax.ShapeDtypeStruct((n_req, n_que...]
    pallas_call x2 -> x0, other arithmetic: 30.5 us -> none  [slot_attention(): pl.pallas_call(slot_kernel, out_shape=(jax.ShapeDtypeStruct((n_slots, hea...]
    reduce_sum x2 -> x0, other arithmetic: 25 us -> none  [the longest x1 24.8 us: shards(): merged_acc = jnp.sum(scale * acc, axis=1)]
    pallas_call x0 -> x2, local copies, waits for them, and re-layouts: none -> 10.4 us  [slot_attention(): pl.pallas_call(slot_kernel, out_shape=(jax.ShapeDtypeStruct((n_req, n_que...]
    all_to_all x2 -> x1, waiting for transfers between devices: 91.7 us -> 91.5 us  [shards(): lax.all_to_all(merged_acc, 'cache', split_axis=0, concat_axis=0, tiled=True)]
  transfers between devices with their start and end apart: 8 -> 7, of which waited for: 7 -> 7; matrix products, arithmetic and copies ran while one was open for 5% -> 1% of each run, Pallas kernels for 0% -> 0%
where the time goes in v3:
time: 585 us; the launch traced here: 584 us
  waiting for transfers between devices  319 us (55%)
  blocking collectives  120 us (21%)
  Pallas kernels  80.8 us (14%)
  local copies, waits for them, and re-layouts  18.1 us (3%)
  starting transfers between devices  17.5 us (3%)
  between operations  13.3 us (2%)
  matrix products  9.57 us (2%)
  other arithmetic  6.4 us (1%)
    all_to_all x1, blocking collectives, shards(): lax.all_to_all(stats, 'cache', split_axis=0, concat_axis=0, tiled=True)  120 us
    all_to_all x1, waiting for transfers between devices, shards(): lax.all_to_all(merged_acc, 'cache', split_axis=0, concat_axis=0, tiled=True)  91.5 us
    pallas_call x1, Pallas kernels, slot_attention(): pl.pallas_call(slot_kernel, out_shape=(jax.ShapeDtypeStruct((n_req, n_que...  80.8 us
    all_gather x1, waiting for transfers between devices, project(): everyone = lax.all_gather(attended, 'cache', axis=0, tiled=True)  72.5 us
    all_gather x1, waiting for transfers between devices, shards(): everyone_q = lax.all_gather(queries, 'cache', axis=0, tiled=True)  59.8 us
    ppermute x2, waiting for transfers between devices, project(): got = lax.ppermute(piece, ('cache', 'stream'), perm)  45.9 us
    reduce_scatter x1, waiting for transfers between devices, project(): lax.psum_scatter(partial_sums.astype(jnp.bfloat16), 'stream', scatter_dim...  41.7 us
  transfers between devices with their start and end apart: 7, of which 7 were waited for; matrix products, arithmetic and copies ran while one was open for 1% of the time, Pallas kernels for 0%

profile of v3, /device:TPU:4, one launch (start us, length us, event | category | flops | bytes accessed | tf_op | source)
XLA Modules:
  0.0 584.1 jit_solution(2992119568605216737)
XLA Ops:
  6.5 0.0 copy-start
  6.5 0.0 all-gather.3.cloned.1.call-start
  6.5 0.7 all-gather.3.cloned.1.call-update
  7.3 0.8 eq.50
  8.0 0.8 select_reduce_fusion.2
  8.9 0.2 convert_reduce_fusion.1
  9.1 0.1 select_reduce_fusion.1
  9.2 0.1 stack.12
  9.2 0.1 stack.13
  9.3 0.1 stack.14
  9.4 0.6 copy.22
  10.0 5.8 all-to-all-start
  15.8 0.1 add.93
  15.9 0.1 add.94
  16.0 6.5 %all-to-all-done = s32[3,8,8]{2,0,1:T(4,128)S(1)} async-done(((s32[3,8,8]{2,0,1:T(4,128)}), s32[3,8,8]{2,0,1:T(4,128)S(1)}, u32[]{:S(2)}, u32[]{:S(2)}) %all-to-all-start) | async-done | bytes 800 | tf_op jit(solution)/shard_map/all_to_all | solution.py:138
  22.6 0.1 squeeze.3.which_ref
  22.6 0.0 copy-start.4
  22.6 0.6 reshape_squeeze.7.rows_ref
  23.2 0.6 reshape_squeeze.8.valid_ref
  23.8 0.5 add.95.pick_ref
  24.3 59.8 %all-gather.3.cloned.1.call-done = bf16[2048,1024]{1,0:T(8,128)(2,1)} async-done(((bf16[256,1024]{1,0:T(8,128)(2,1)}), bf16[2048,1024]{1,0:T(8,128)(2,1)}) %all-gather.3.cloned.1.call-update) | async-done | bytes 4194320 | tf_op jit(solution)/shard_map/all_gather | solution.py:144
  84.1 0.0 copy-done.4
  84.1 80.8 %shard_map.64 = (bf16[8,2,1024,128]{3,2,1,0:T(8,128)(2,1)}, f32[8,2,1024,1]{3,2,1,0:T(8,128)}, f32[8,2,1024,1]{3,2,1,0:T(8,128)}) custom-call(s32[64]{0:T(128)} %reshape_squeeze.7.rows_ref, s32[64]{0:T(128)} %add.95.pick_ref, s32[64]{0:T(128)} %reshape_squeeze.8.valid_ref, s32[64]{0:T(128)} %copy-done.4, bf16[16,128,1024]{2,1,0:T(8,128)(2,1)} %bitcast.88, ...), custom_call_target="tpu_custom_call" | custom-call | flops 17179869184 | bytes 37748736 | tf_op jit(solution)/shard_map/pallas_call | solution.py:63
  165.0 5.2 copy.23
  170.2 5.2 copy.24
  175.5 119.8 %all_to_all.15 = f32[8,2,8,128,2]{3,2,1,4,0:T(8,128)S(1)} all-to-all(f32[8,2,8,128,2]{3,2,1,4,0:T(8,128)S(1)} %copy.34), channel_id=1, replica_groups=mesh['cache'=8,'stream'=4] {'cache'}, dimensions={0} | all-to-all | bytes 262144 | tf_op jit(solution)/shard_map/all_to_all | solution.py:157
  295.2 0.0 copy-start.1
  295.2 0.0 copy-start.3
  295.2 4.7 all-to-all-start.2
  299.9 0.0 all-gather.5.cloned.1.call-start
  300.0 0.0 copy-done.1
  300.0 0.1 copy.38
  300.1 0.0 copy-done.3
  300.1 0.3 fusion.19
  300.4 0.2 fusion.6
  300.7 91.5 %all-to-all-done.2 = bf16[8,2,8,128,128]{4,3,2,1,0:T(8,128)(2,1)} async-done(((bf16[8,2,8,128,128]{4,3,2,1,0:T(8,128)(2,1)}), bf16[8,2,8,128,128]{4,3,2,1,0:T(8,128)(2,1)}, u32[]{:S(2)}, u32[]{:S(2)}) %all-to-all-start.2) | async-done | bytes 4194336 | tf_op jit(solution)/shard_map/all_to_all | solution.py:154
  392.1 4.5 multiply_reduce_fusion
  396.6 0.9 fusion.5
  397.6 0.3 copy.30
  397.9 0.9 copy.46
  398.8 0.0 all-gather.5.cloned.1.call-update
  398.8 0.0 reduce-scatter.2.cloned.1.call-start
  398.9 72.5 %all-gather.5.cloned.1.call-done = bf16[2048,1024]{1,0:T(8,128)(2,1)} async-done(((bf16[256,1024]{1,0:T(8,128)(2,1)}), bf16[2048,1024]{1,0:T(8,128)(2,1)}) %all-gather.5.cloned.1.call-update) | async-done | bytes 4194320 | tf_op jit(solution)/shard_map/all_gather | solution.py:180
  471.4 0.0 copy-done
  471.4 8.3 %convolution_convert_fusion = bf16[2048,1024]{1,0:T(8,128)(2,1)} fusion(bf16[2048,1024]{1,0:T(8,128)(2,1)} %all-gather.5.cloned.1.call-done, bf16[1024,1024]{1,0:T(8,128)(2,1)S(1)} %copy-done), kind=kOutput, calls=%fused_computation.1 | convolution fusion | flops 4297064448 | bytes 10485760 | tf_op jit(solution)/shard_map/dot_general | solution.py:181
  479.7 0.0 reduce-scatter.2.cloned.1.call-update
  479.8 41.7 %reduce-scatter.2.cloned.1.call-done = bf16[512,1024]{1,0:T(8,128)(2,1)} async-done(((bf16[2048,1024]{1,0:T(8,128)(2,1)}), bf16[512,1024]{1,0:T(8,128)(2,1)}) %reduce-scatter.2.cloned.1.call-update) | async-done | bytes 1048592 | tf_op jit(solution)/shard_map/reduce_scatter | solution.py:182
  521.5 2.2 constant_dynamic-slice_fusion
  523.8 5.5 collective-permute-start
  529.2 1.5 collective-permute-start.1
  530.7 34.2 %collective-permute-done = bf16[256,1024]{1,0:T(8,128)(2,1)S(1)} collective-permute-done((bf16[256,1024]{1,0:T(8,128)(2,1)}, bf16[256,1024]{1,0:T(8,128)(2,1)S(1)}, u32[]{:S(2)}, u32[]{:S(2)}) %collective-permute-start) | collective-permute-done | bytes 524320 | tf_op jit(solution)/shard_map/ppermute | solution.py:197
  564.9 0.1 broadcast_in_dim.57
  565.0 0.1 constant_dynamic-update-slice_fusion.1
  565.1 0.0 copy-start.2
  565.1 11.6 %collective-permute-done.1 = bf16[256,1024]{1,0:T(8,128)(2,1)S(1)} collective-permute-done((bf16[256,1024]{1,0:T(8,128)(2,1)}, bf16[256,1024]{1,0:T(8,128)(2,1)S(1)}, u32[]{:S(2)}, u32[]{:S(2)}) %collective-permute-start.1) | collective-permute-done | bytes 524320 | tf_op jit(solution)/shard_map/ppermute | solution.py:197
  576.7 0.0 copy-done.2
  576.7 0.8 constant_dynamic-update-slice_fusion
  (12 shorter events, 0.2 us)
Async XLA Ops:
  6.5 464.9 %copy-start = (bf16[1024,1024]{1,0:T(8,128)(2,1)S(1)}, bf16[1024,1024]{1,0:T(8,128)(2,1)}, u32[]{:S(2)}) copy-start(bf16[1024,1024]{1,0:T(8,128)(2,1)} %param.9) | copy-start | bytes 6291460
  6.5 77.6 %all-gather.3.cloned.1.call-start = ((), (), s32[]{:S(2)}) async-start(), calls=%async_computation.4 | async-start | bytes 4718592 | tf_op jit(solution)/shard_map/all_gather | solution.py:144
  10.0 12.5 %all-to-all-start = ((s32[3,8,8]{2,0,1:T(4,128)}), s32[3,8,8]{2,0,1:T(4,128)S(1)}, u32[]{:S(2)}, u32[]{:S(2)}) async-start(s32[3,8,8]{2,0,1:T(4,128)} %copy.22), calls=%async_computation | async-start | bytes 32768 | tf_op jit(solution)/shard_map/all_to_all | solution.py:138
  22.6 61.5 %copy-start.4 = (s32[64]{0:T(128)}, s32[64]{0:T(128)S(1)}, u32[]{:S(2)}) copy-start(s32[64]{0:T(128)S(1)} %squeeze.3.which_ref) | copy-start | bytes 772
  295.2 4.7 copy-start.1
  295.2 4.9 copy-start.3
  295.2 96.9 %all-to-all-start.2 = ((bf16[8,2,8,128,128]{4,3,2,1,0:T(8,128)(2,1)}), bf16[8,2,8,128,128]{4,3,2,1,0:T(8,128)(2,1)}, u32[]{:S(2)}, u32[]{:S(2)}) async-start(bf16[8,2,8,128,128]{4,3,2,1,0:T(8,128)(2,1)} %bitcast.81), calls=%async_computation.2 | async-start | bytes 8388608 | tf_op jit(solution)/shard_map/all_to_all | solution.py:154
  299.9 171.5 %all-gather.5.cloned.1.call-start = ((), (), s32[]{:S(2)}) async-start(), calls=%async_computation.5 | async-start | bytes 4718592 | tf_op jit(solution)/shard_map/all_gather | solution.py:180
  398.8 122.7 %reduce-scatter.2.cloned.1.call-start = ((), (), s32[]{:S(2)}) async-start(), calls=%async_computation.6 | async-start | bytes 5242880 | tf_op jit(solution)/shard_map/reduce_scatter | solution.py:182
  523.8 41.2 %collective-permute-start = (bf16[256,1024]{1,0:T(8,128)(2,1)}, bf16[256,1024]{1,0:T(8,128)(2,1)S(1)}, u32[]{:S(2)}, u32[]{:S(2)}) collective-permute-start(bf16[256,1024]{1,0:T(8,128)(2,1)} %get-tuple-element.20), channel_id=1, source_target_pairs={{0,0},{1,8},{2,16},{3,24},{4,4},{5,12},{6,20},{7,28},{8,1},{9,9},{... | collective-permute-start | bytes 1572872 | tf_op jit(solution)/shard_map/ppermute | solution.py:197
  529.2 47.5 %collective-permute-start.1 = (bf16[256,1024]{1,0:T(8,128)(2,1)}, bf16[256,1024]{1,0:T(8,128)(2,1)S(1)}, u32[]{:S(2)}, u32[]{:S(2)}) collective-permute-start(bf16[256,1024]{1,0:T(8,128)(2,1)} %get-tuple-element.19), channel_id=1, source_target_pairs={{0,4},{1,12},{2,20},{3,28},{4,0},{5,8},{6,16},{7,24},{8,5},{9,13},... | collective-permute-start | bytes 1572872 | tf_op jit(solution)/shard_map/ppermute | solution.py:197
  565.1 11.6 %copy-start.2 = (bf16[256,2048]{1,0:T(8,128)(2,1)}, bf16[256,2048]{1,0:T(8,128)(2,1)S(1)}, u32[]{:S(2)}) copy-start(bf16[256,2048]{1,0:T(8,128)(2,1)S(1)} %constant_dynamic-update-slice_fusion.1) | copy-start | bytes 3145732
Sparse Core Ops, SparseCore 0:
  9.5 74.5 all-gather.2
  398.9 72.3 all-gather.4
  479.9 41.6 reduce-scatter.1

commit v4 on v3

--- a/solution.py
+++ b/solution.py
@@ -50,8 +50,18 @@
     @pl.when(k == cap - 1)
     def _():
         acc_out[0] = acc_sc[...].astype(acc_out.dtype)
-        peak_out[0] = peak_sc[...]
-        total_out[0] = total_sc[...]
+        eye = lax.broadcasted_iota(jnp.int32, (QLEN, QLEN), 0) == lax.broadcasted_iota(
+            jnp.int32, (QLEN, QLEN), 1
+        )
+        for j in range(peak_sc.shape[0]):
+            for h in range(heads):
+                rows = pl.ds(h * QLEN, QLEN)
+                peak_out[0, j, pl.ds(h, 1), :] = jnp.sum(
+                    jnp.where(eye, peak_sc[j, rows, :], 0.0), axis=0, keepdims=True
+                )
+                total_out[0, j, pl.ds(h, 1), :] = jnp.sum(
+                    jnp.where(eye, total_sc[j, rows, :], 0.0), axis=0, keepdims=True
+                )
 
 
 def slot_attention(rows, pick, valid, which, q_blocks, store, n_req, cap, n_query):
@@ -64,8 +74,8 @@
         slot_kernel,
         out_shape=(
             jax.ShapeDtypeStruct((n_req, n_query, stacked, HD), jnp.bfloat16),
-            jax.ShapeDtypeStruct((n_req, n_query, stacked, 1), jnp.float32),
-            jax.ShapeDtypeStruct((n_req, n_query, stacked, 1), jnp.float32),
+            jax.ShapeDtypeStruct((n_req, n_query, heads, QLEN), jnp.float32),
+            jax.ShapeDtypeStruct((n_req, n_query, heads, QLEN), jnp.float32),
         ),
         grid_spec=pltpu.PrefetchScalarGridSpec(
             num_scalar_prefetch=4,
@@ -76,8 +86,8 @@
             ],
             out_specs=[
                 pl.BlockSpec((1, n_query, stacked, HD), lambda r, k, rw, pk, vd, wh: (r, 0, 0, 0)),
-                pl.BlockSpec((1, n_query, stacked, 1), lambda r, k, rw, pk, vd, wh: (r, 0, 0, 0)),
-                pl.BlockSpec((1, n_query, stacked, 1), lambda r, k, rw, pk, vd, wh: (r, 0, 0, 0)),
+                pl.BlockSpec((1, n_query, heads, QLEN), lambda r, k, rw, pk, vd, wh: (r, 0, 0, 0)),
+                pl.BlockSpec((1, n_query, heads, QLEN), lambda r, k, rw, pk, vd, wh: (r, 0, 0, 0)),
             ],
             scratch_shapes=[
                 pltpu.VMEM((n_query, stacked, HD), jnp.float32),
@@ -148,9 +158,7 @@
         q_blocks, passage_store, n_cache, capacity, query_count,
     )
     merged_acc = merged_acc.reshape(n_cache, query_count, heads, QLEN, HD)
-    stats = jnp.concatenate([merged_peak, merged_total], axis=-1).reshape(
-        n_cache, query_count, heads, QLEN, 2
-    )
+    stats = jnp.stack([merged_peak, merged_total], axis=2)
     back_acc = lax.all_to_all(
         merged_acc, "cache", split_axis=0, concat_axis=0, tiled=True
     )
@@ -160,8 +168,8 @@
         queries.reshape(query_count, QLEN, width),
         own_kv.reshape(query_count, QLEN, own_kv.shape[1]),
     )
-    far_peak = back_stats[..., 0:1]
-    far_total = back_stats[..., 1:2]
+    far_peak = back_stats[:, :, 0][..., None]
+    far_total = back_stats[:, :, 1][..., None]
     top = jnp.maximum(jnp.max(far_peak, axis=0), own_peak)
     far_scale = jnp.exp(far_peak - top[None])
     own_scale = jnp.exp(own_peak - top)

time: 585 us -> 577 us (0.986)
  local copies, waits for them, and re-layouts: 18.1 us -> 7.67 us
  blocking collectives: 120 us -> 126 us
    pallas_call x2 -> x0, local copies, waits for them, and re-layouts: 10.4 us -> none  [slot_attention(): pl.pallas_call(slot_kernel, out_shape=(jax.ShapeDtypeStruct((n_req, n_que...]
    all_to_all x1, blocking collectives: 120 us -> 126 us  [shards(): lax.all_to_all(stats, 'cache', split_axis=0, concat_axis=0, tiled=True)]
where the time goes in v4:
time: 577 us
  waiting for transfers between devices  318 us (55%)
  blocking collectives  126 us (22%)
  Pallas kernels  77.7 us (13%)
  starting transfers between devices  17.5 us (3%)
  between operations  13.3 us (2%)
  matrix products  9.57 us (2%)
  local copies, waits for them, and re-layouts  7.67 us (1%)
  other arithmetic  7.34 us (1%)
    all_to_all x1, blocking collectives, shards(): lax.all_to_all(stats, 'cache', split_axis=0, concat_axis=0, tiled=True)  126 us
    all_to_all x1, waiting for transfers between devices, shards(): lax.all_to_all(merged_acc, 'cache', split_axis=0, concat_axis=0, tiled=True)  90.8 us
    pallas_call x1, Pallas kernels, slot_attention(): pl.pallas_call(slot_kernel, out_shape=(jax.ShapeDtypeStruct((n_req, n_que...  77.7 us
    all_gather x1, waiting for transfers between devices, project(): everyone = lax.all_gather(attended, 'cache', axis=0, tiled=True)  72.5 us
    all_gather x1, waiting for transfers between devices, shards(): everyone_q = lax.all_gather(queries, 'cache', axis=0, tiled=True)  59.7 us
    ppermute x2, waiting for transfers between devices, project(): got = lax.ppermute(piece, ('cache', 'stream'), perm)  45.9 us
    reduce_scatter x1, waiting for transfers between devices, project(): lax.psum_scatter(partial_sums.astype(jnp.bfloat16), 'stream', scatter_dim...  41.7 us
  transfers between devices with their start and end apart: 7, of which 7 were waited for; matrix products, arithmetic and copies ran while one was open for 1% of the time, Pallas kernels for 0%

profile of v4, /device:TPU:4, one launch (start us, length us, event | category | flops | bytes accessed | tf_op | source)
XLA Modules:
  0.0 576.6 jit_solution(9947654682414410673)
XLA Ops:
  6.5 0.0 copy-start
  6.5 0.0 all-gather.3.cloned.1.call-start
  6.5 0.7 all-gather.3.cloned.1.call-update
  7.3 0.8 eq.50
  8.0 0.8 select_reduce_fusion.2
  8.9 0.2 convert_reduce_fusion.1
  9.1 0.1 select_reduce_fusion.1
  9.2 0.1 stack.21
  9.2 0.1 stack.23
  9.3 0.1 stack.22
  9.4 0.6 copy.18
  10.0 5.8 %all-to-all-start = ((s32[3,8,8]{2,0,1:T(4,128)}), s32[3,8,8]{2,0,1:T(4,128)S(1)}, u32[]{:S(2)}, u32[]{:S(2)}) async-start(s32[3,8,8]{2,0,1:T(4,128)} %copy.18), calls=%async_computation | async-start | bytes 32768 | tf_op jit(solution)/shard_map/all_to_all | solution.py:148
  15.8 0.1 add.93
  15.9 0.1 add.94
  16.0 6.5 %all-to-all-done = s32[3,8,8]{2,0,1:T(4,128)S(1)} async-done(((s32[3,8,8]{2,0,1:T(4,128)}), s32[3,8,8]{2,0,1:T(4,128)S(1)}, u32[]{:S(2)}, u32[]{:S(2)}) %all-to-all-start) | async-done | bytes 800 | tf_op jit(solution)/shard_map/all_to_all | solution.py:148
  22.6 0.6 reshape_squeeze.8.valid_ref
  23.2 0.1 squeeze.3.which_ref
  23.3 0.0 copy-start.4
  23.3 0.6 reshape_squeeze.7.rows_ref
  23.8 0.6 add.95.pick_ref
  24.4 59.7 %all-gather.3.cloned.1.call-done = bf16[2048,1024]{1,0:T(8,128)(2,1)} async-done(((bf16[256,1024]{1,0:T(8,128)(2,1)}), bf16[2048,1024]{1,0:T(8,128)(2,1)}) %all-gather.3.cloned.1.call-update) | async-done | bytes 4194320 | tf_op jit(solution)/shard_map/all_gather | solution.py:154
  84.1 0.0 copy-done.4
  84.1 77.7 %shard_map.64 = (bf16[8,2,1024,128]{3,2,1,0:T(8,128)(2,1)}, f32[8,2,8,128]{3,2,1,0:T(8,128)}, f32[8,2,8,128]{3,2,1,0:T(8,128)}) custom-call(s32[64]{0:T(128)} %reshape_squeeze.7.rows_ref, s32[64]{0:T(128)} %add.95.pick_ref, s32[64]{0:T(128)} %reshape_squeeze.8.valid_ref, s32[64]{0:T(128)} %copy-done.4, bf16[16,128,1024]{2,1,0:T(8,128)(2,1)} %bitcast.84, ...), custom_call_target="tpu_custom_call" | custom-call | flops 17179869184 | bytes 37748736 | tf_op jit(solution)/shard_map/pallas_call | solution.py:73
  161.8 0.9 pad_maximum_fusion
  162.7 125.7 %all_to_all.15 = f32[8,2,2,8,128]{4,3,1,2,0:T(8,128)S(1)} all-to-all(f32[8,2,2,8,128]{4,3,1,2,0:T(8,128)S(1)} %copy.19), channel_id=1, replica_groups=mesh['cache'=8,'stream'=4] {'cache'}, dimensions={0} | all-to-all | bytes 262144 | tf_op jit(solution)/shard_map/all_to_all | solution.py:165
  288.3 0.0 copy-start.1
  288.3 0.0 copy-start.3
  288.3 4.7 all-to-all-start.2
  293.0 0.0 all-gather.5.cloned.1.call-start
  293.1 0.0 copy-done.1
  293.1 0.1 copy.28
  293.2 0.0 copy-done.3
  293.2 0.3 fusion.19
  293.6 0.2 fusion.6
  293.8 90.8 %all-to-all-done.2 = bf16[8,2,8,128,128]{4,3,2,1,0:T(8,128)(2,1)} async-done(((bf16[8,2,8,128,128]{4,3,2,1,0:T(8,128)(2,1)}), bf16[8,2,8,128,128]{4,3,2,1,0:T(8,128)(2,1)}, u32[]{:S(2)}, u32[]{:S(2)}) %all-to-all-start.2) | async-done | bytes 4194336 | tf_op jit(solution)/shard_map/all_to_all | solution.py:162
  384.7 4.5 multiply_reduce_fusion
  389.2 0.9 fusion.5
  390.1 0.3 copy.23
  390.4 0.9 copy.35
  391.3 0.0 all-gather.5.cloned.1.call-update
  391.3 0.0 reduce-scatter.2.cloned.1.call-start
  391.4 72.5 %all-gather.5.cloned.1.call-done = bf16[2048,1024]{1,0:T(8,128)(2,1)} async-done(((bf16[256,1024]{1,0:T(8,128)(2,1)}), bf16[2048,1024]{1,0:T(8,128)(2,1)}) %all-gather.5.cloned.1.call-update) | async-done | bytes 4194320 | tf_op jit(solution)/shard_map/all_gather | solution.py:188
  463.9 0.0 copy-done
  463.9 8.3 %convolution_convert_fusion = bf16[2048,1024]{1,0:T(8,128)(2,1)} fusion(bf16[2048,1024]{1,0:T(8,128)(2,1)} %all-gather.5.cloned.1.call-done, bf16[1024,1024]{1,0:T(8,128)(2,1)S(1)} %copy-done), kind=kOutput, calls=%fused_computation.1 | convolution fusion | flops 4297064448 | bytes 10485760 | tf_op jit(solution)/shard_map/dot_general | solution.py:189
  472.3 0.0 reduce-scatter.2.cloned.1.call-update
  472.3 41.7 %reduce-scatter.2.cloned.1.call-done = bf16[512,1024]{1,0:T(8,128)(2,1)} async-done(((bf16[2048,1024]{1,0:T(8,128)(2,1)}), bf16[512,1024]{1,0:T(8,128)(2,1)}) %reduce-scatter.2.cloned.1.call-update) | async-done | bytes 1048592 | tf_op jit(solution)/shard_map/reduce_scatter | solution.py:190
  514.1 2.2 constant_dynamic-slice_fusion
  516.3 5.5 collective-permute-start
  521.8 1.5 collective-permute-start.1
  523.2 34.2 %collective-permute-done = bf16[256,1024]{1,0:T(8,128)(2,1)S(1)} collective-permute-done((bf16[256,1024]{1,0:T(8,128)(2,1)}, bf16[256,1024]{1,0:T(8,128)(2,1)S(1)}, u32[]{:S(2)}, u32[]{:S(2)}) %collective-permute-start) | collective-permute-done | bytes 524320 | tf_op jit(solution)/shard_map/ppermute | solution.py:205
  557.4 0.1 broadcast_in_dim.57
  557.6 0.1 constant_dynamic-update-slice_fusion.1
  557.6 0.0 copy-start.2
  557.6 11.6 %collective-permute-done.1 = bf16[256,1024]{1,0:T(8,128)(2,1)S(1)} collective-permute-done((bf16[256,1024]{1,0:T(8,128)(2,1)}, bf16[256,1024]{1,0:T(8,128)(2,1)S(1)}, u32[]{:S(2)}, u32[]{:S(2)}) %collective-permute-start.1) | collective-permute-done | bytes 524320 | tf_op jit(solution)/shard_map/ppermute | solution.py:205
  569.3 0.0 copy-done.2
  569.3 0.8 constant_dynamic-update-slice_fusion
  (12 shorter events, 0.2 us)
Async XLA Ops:
  6.5 457.4 %copy-start = (bf16[1024,1024]{1,0:T(8,128)(2,1)S(1)}, bf16[1024,1024]{1,0:T(8,128)(2,1)}, u32[]{:S(2)}) copy-start(bf16[1024,1024]{1,0:T(8,128)(2,1)} %param.9) | copy-start | bytes 6291460
  6.5 77.6 %all-gather.3.cloned.1.call-start = ((), (), s32[]{:S(2)}) async-start(), calls=%async_computation.4 | async-start | bytes 4718592 | tf_op jit(solution)/shard_map/all_gather | solution.py:154
  10.0 12.5 %all-to-all-start = ((s32[3,8,8]{2,0,1:T(4,128)}), s32[3,8,8]{2,0,1:T(4,128)S(1)}, u32[]{:S(2)}, u32[]{:S(2)}) async-start(s32[3,8,8]{2,0,1:T(4,128)} %copy.18), calls=%async_computation | async-start | bytes 32768 | tf_op jit(solution)/shard_map/all_to_all | solution.py:148
  23.3 60.8 %copy-start.4 = (s32[64]{0:T(128)}, s32[64]{0:T(128)S(1)}, u32[]{:S(2)}) copy-start(s32[64]{0:T(128)S(1)} %squeeze.3.which_ref) | copy-start | bytes 772
  288.3 4.7 copy-start.1
  288.3 4.9 copy-start.3
  288.3 96.3 %all-to-all-start.2 = ((bf16[8,2,8,128,128]{4,3,2,1,0:T(8,128)(2,1)}), bf16[8,2,8,128,128]{4,3,2,1,0:T(8,128)(2,1)}, u32[]{:S(2)}, u32[]{:S(2)}) async-start(bf16[8,2,8,128,128]{4,3,2,1,0:T(8,128)(2,1)} %bitcast.75), calls=%async_computation.2 | async-start | bytes 8388608 | tf_op jit(solution)/shard_map/all_to_all | solution.py:162
  293.0 170.9 %all-gather.5.cloned.1.call-start = ((), (), s32[]{:S(2)}) async-start(), calls=%async_computation.5 | async-start | bytes 4718592 | tf_op jit(solution)/shard_map/all_gather | solution.py:188
  391.3 122.7 %reduce-scatter.2.cloned.1.call-start = ((), (), s32[]{:S(2)}) async-start(), calls=%async_computation.6 | async-start | bytes 5242880 | tf_op jit(solution)/shard_map/reduce_scatter | solution.py:190
  516.3 41.2 %collective-permute-start = (bf16[256,1024]{1,0:T(8,128)(2,1)}, bf16[256,1024]{1,0:T(8,128)(2,1)S(1)}, u32[]{:S(2)}, u32[]{:S(2)}) collective-permute-start(bf16[256,1024]{1,0:T(8,128)(2,1)} %get-tuple-element.20), channel_id=1, source_target_pairs={{0,0},{1,8},{2,16},{3,24},{4,4},{5,12},{6,20},{7,28},{8,1},{9,9},{... | collective-permute-start | bytes 1572872 | tf_op jit(solution)/shard_map/ppermute | solution.py:205
  521.8 47.5 %collective-permute-start.1 = (bf16[256,1024]{1,0:T(8,128)(2,1)}, bf16[256,1024]{1,0:T(8,128)(2,1)S(1)}, u32[]{:S(2)}, u32[]{:S(2)}) collective-permute-start(bf16[256,1024]{1,0:T(8,128)(2,1)} %get-tuple-element.19), channel_id=1, source_target_pairs={{0,4},{1,12},{2,20},{3,28},{4,0},{5,8},{6,16},{7,24},{8,5},{9,13},... | collective-permute-start | bytes 1572872 | tf_op jit(solution)/shard_map/ppermute | solution.py:205
  557.6 11.6 %copy-start.2 = (bf16[256,2048]{1,0:T(8,128)(2,1)}, bf16[256,2048]{1,0:T(8,128)(2,1)S(1)}, u32[]{:S(2)}) copy-start(bf16[256,2048]{1,0:T(8,128)(2,1)S(1)} %constant_dynamic-update-slice_fusion.1) | copy-start | bytes 3145732
Sparse Core Ops, SparseCore 0:
  9.5 74.5 all-gather.2
  391.5 72.3 all-gather.4
  472.4 41.6 reduce-scatter.1

commit v5 on v4

--- a/solution.py
+++ b/solution.py
@@ -148,21 +148,32 @@
     asked = lax.all_to_all(info, "cache", split_axis=1, concat_axis=1, tiled=True)
     asked_rows = asked[0].reshape(n_cache * capacity)
     asked_query = asked[1]
-    requester = jnp.arange(n_cache, dtype=jnp.int32)[:, None]
-    pick = (requester * query_count + asked_query).reshape(n_cache * capacity)
-
-    everyone_q = lax.all_gather(queries, "cache", axis=0, tiled=True)
-    q_blocks = everyone_q.reshape(n_cache * query_count, QLEN, width)
-    merged_acc, merged_peak, merged_total = slot_attention(
-        asked_rows, pick, asked[2].reshape(n_cache * capacity), asked_query.reshape(n_cache * capacity),
-        q_blocks, passage_store, n_cache, capacity, query_count,
-    )
-    merged_acc = merged_acc.reshape(n_cache, query_count, heads, QLEN, HD)
-    stats = jnp.stack([merged_peak, merged_total], axis=2)
-    back_acc = lax.all_to_all(
-        merged_acc, "cache", split_axis=0, concat_axis=0, tiled=True
-    )
-    back_stats = lax.all_to_all(stats, "cache", split_axis=0, concat_axis=0, tiled=True)
+    me = lax.axis_index("cache")
+    q_local = queries.reshape(query_count, QLEN, width)
+    far_acc = []
+    far_stats = []
+    for off in range(n_cache):
+        source = (me + n_cache - off) % n_cache
+        if off == 0:
+            q_here = q_local
+        else:
+            q_here = lax.ppermute(
+                q_local, "cache", [(c, (c + off) % n_cache) for c in range(n_cache)]
+            )
+        mine = lax.dynamic_index_in_dim(asked, source, axis=1, keepdims=False)
+        acc_r, peak_r, total_r = slot_attention(
+            mine[0], mine[1], mine[2], mine[1], q_here, passage_store, 1, capacity, query_count,
+        )
+        acc_r = acc_r.reshape(query_count, heads, QLEN, HD)
+        stats_r = jnp.stack([peak_r[0], total_r[0]], axis=1)
+        if off != 0:
+            home = [(c, (c + n_cache - off) % n_cache) for c in range(n_cache)]
+            acc_r = lax.ppermute(acc_r, "cache", home)
+            stats_r = lax.ppermute(stats_r, "cache", home)
+        far_acc.append(acc_r)
+        far_stats.append(stats_r)
+    back_acc = jnp.stack(far_acc, axis=0)
+    back_stats = jnp.stack(far_stats, axis=0)
 
     own_acc, own_peak, own_total = own_part(
         queries.reshape(query_count, QLEN, width),

time: 577 us -> 578 us (level)
  blocking collectives: 126 us -> 0 us
  starting transfers between devices: 17.5 us -> 130 us
  waiting for transfers between devices: 318 us -> 277 us
  Pallas kernels: 77.7 us -> 112 us
  local copies, waits for them, and re-layouts: 7.67 us -> 23.8 us
    all_to_all x1 -> x0, blocking collectives: 126 us -> none  [shards(): lax.all_to_all(stats, 'cache', split_axis=0, concat_axis=0, tiled=True)]
    ppermute x0 -> x21, starting transfers between devices: none -> 120 us  [the longest x7 50.9 us: shards(): stats_r = lax.ppermute(stats_r, 'cache', home)]
    all_to_all x1 -> x0, waiting for transfers between devices: 90.8 us -> none  [shards(): lax.all_to_all(merged_acc, 'cache', split_axis=0, concat_axis=0, tiled=True)]
    all_gather x1 -> x0, waiting for transfers between devices: 59.7 us -> none  [shards(): everyone_q = lax.all_gather(queries, 'cache', axis=0, tiled=True)]
    all_to_all x1, waiting for transfers between devices: 6.52 us -> 66.1 us  [shards(): lax.all_to_all(info, 'cache', split_axis=1, concat_axis=1, tiled=True)]
    ppermute x0 -> x21, waiting for transfers between devices: none -> 52.7 us  [the longest x7 29.1 us: shards(): acc_r = lax.ppermute(acc_r, 'cache', home)]
    pallas_call x1 -> x8, Pallas kernels: 77.7 us -> 112 us  [slot_attention(): pl.pallas_call(slot_kernel, out_shape=(jax.ShapeDtypeStruct((n_req, n_que...]
    unnamed x12 -> x29, local copies, waits for them, and re-layouts: 1.01 us -> 13.2 us
  transfers between devices with their start and end apart: 7 -> 26, of which waited for: 7 -> 13; matrix products, arithmetic and copies ran while one was open for 1% -> 4% of each run, Pallas kernels for 0% -> 19%
where the time goes in v5:
time: 578 us; the launch traced here: 577 us
  waiting for transfers between devices  277 us (48%)
  starting transfers between devices  130 us (22%)
  Pallas kernels  112 us (19%)
  local copies, waits for them, and re-layouts  23.8 us (4%)
  between operations  13.9 us (2%)
  matrix products  10.4 us (2%)
  other arithmetic  10.2 us (2%)
    pallas_call x8, Pallas kernels, slot_attention(): pl.pallas_call(slot_kernel, out_shape=(jax.ShapeDtypeStruct((n_req, n_que...  112 us
    all_gather x1, waiting for transfers between devices, project(): everyone = lax.all_gather(attended, 'cache', axis=0, tiled=True)  70.7 us
    all_to_all x1, waiting for transfers between devices, shards(): lax.all_to_all(info, 'cache', split_axis=1, concat_axis=1, tiled=True)  66.1 us
    ppermute x7, starting transfers between devices, shards(): stats_r = lax.ppermute(stats_r, 'cache', home)  50.9 us
    ppermute x2, waiting for transfers between devices, project(): got = lax.ppermute(piece, ('cache', 'stream'), perm)  45.9 us
    ppermute x7, starting transfers between devices, shards(): acc_r = lax.ppermute(acc_r, 'cache', home)  43.4 us
    reduce_scatter x1, waiting for transfers between devices, project(): lax.psum_scatter(partial_sums.astype(jnp.bfloat16), 'stream', scatter_dim...  41.7 us
    ppermute x7, waiting for transfers between devices, shards(): acc_r = lax.ppermute(acc_r, 'cache', home)  29.1 us
  transfers between devices with their start and end apart: 26, of which 13 were waited for; matrix products, arithmetic and copies ran while one was open for 4% of the time, Pallas kernels for 19%

profile of v5, /device:TPU:4, one launch (start us, length us, event | category | flops | bytes accessed | tf_op | source)
XLA Modules:
  0.0 577.3 jit_solution(6836621814000497630)
XLA Ops:
  6.5 1.5 collective-permute-start
  8.0 1.6 collective-permute-start.2
  9.6 2.6 collective-permute-start.4
  12.2 1.2 collective-permute-start.6
  13.4 2.6 collective-permute-start.8
  16.0 0.8 eq.58
  16.8 0.8 select_reduce_fusion.2
  18.8 3.3 all-to-all-start
  22.3 1.1 copy.28
  23.4 1.2 fusion.20
  24.8 66.1 %all-to-all-done = s32[3,8,8]{2,0,1:T(4,128)S(1)} async-done(((s32[3,8,8]{2,0,1:T(4,128)}), s32[3,8,8]{2,0,1:T(4,128)S(1)}, u32[]{:S(2)}, u32[]{:S(2)}) %all-to-all-start) | async-done | bytes 800 | tf_op jit(solution)/shard_map/all_to_all | solution.py:148
  91.6 15.0 %shard_map.64 = (bf16[1,2,1024,128]{3,2,1,0:T(8,128)(2,1)}, f32[1,2,8,128]{3,2,1,0:T(8,128)}, f32[1,2,8,128]{3,2,1,0:T(8,128)}) custom-call(s32[8]{0:T(128)} %get-tuple-element.91.rows_ref, s32[8]{0:T(128)} %get-tuple-element.90.pick_ref.which_ref, s32[8]{0:T(128)} %get-tuple-element.89.valid_ref, s32[8]{0:T(128)} %get-tuple-element.90.pick_ref.which_ref, ...), custom_call_target="tpu_custom_call" | custom-call | flops 2147483648 | bytes 4718592 | tf_op jit(solution)/shard_map/pallas_call | solution.py:73
  106.5 1.9 constant_dynamic-update-slice_fusion.8
  111.3 0.7 constant_dynamic-update-slice_fusion.7
  113.2 9.4 %shard_map.65 = (bf16[1,2,1024,128]{3,2,1,0:T(8,128)(2,1)}, f32[1,2,8,128]{3,2,1,0:T(8,128)}, f32[1,2,8,128]{3,2,1,0:T(8,128)}) custom-call(s32[8]{0:T(128)} %get-tuple-element.88.rows_ref, s32[8]{0:T(128)} %get-tuple-element.87.pick_ref.which_ref, s32[8]{0:T(128)} %get-tuple-element.86.valid_ref, s32[8]{0:T(128)} %get-tuple-element.87.pick_ref.which_ref, ...), custom_call_target="tpu_custom_call" | custom-call | flops 2147483648 | bytes 4718592 | tf_op jit(solution)/shard_map/pallas_call | solution.py:73
  122.6 0.7 pad_maximum_fusion
  123.3 16.2 %collective-permute-start.12 = (bf16[2,128,1024]{2,1,0:T(8,128)(2,1)}, bf16[2,128,1024]{2,1,0:T(8,128)(2,1)}, u32[]{:S(2)}, u32[]{:S(2)}) collective-permute-start(bf16[2,128,1024]{2,1,0:T(8,128)(2,1)} %bitcast.187), channel_id=1, source_target_pairs={{0,28},{4,0},{8,4},{12,8},{16,12},{20,16},{24,20},{28,24},{1,29},{... | collective-permute-start | bytes 1572872 | tf_op jit(solution)/shard_map/ppermute | solution.py:160
  139.5 15.0 %shard_map.66 = (bf16[1,2,1024,128]{3,2,1,0:T(8,128)(2,1)}, f32[1,2,8,128]{3,2,1,0:T(8,128)}, f32[1,2,8,128]{3,2,1,0:T(8,128)}) custom-call(s32[8]{0:T(128)} %get-tuple-element.85.rows_ref, s32[8]{0:T(128)} %get-tuple-element.84.pick_ref.which_ref, s32[8]{0:T(128)} %get-tuple-element.83.valid_ref, s32[8]{0:T(128)} %get-tuple-element.84.pick_ref.which_ref, ...), custom_call_target="tpu_custom_call" | custom-call | flops 2147483648 | bytes 4718592 | tf_op jit(solution)/shard_map/pallas_call | solution.py:73
  154.5 0.7 pad_maximum_fusion.1
  155.2 15.0 %shard_map.67 = (bf16[1,2,1024,128]{3,2,1,0:T(8,128)(2,1)}, f32[1,2,8,128]{3,2,1,0:T(8,128)}, f32[1,2,8,128]{3,2,1,0:T(8,128)}) custom-call(s32[8]{0:T(128)} %get-tuple-element.82.rows_ref, s32[8]{0:T(128)} %get-tuple-element.81.pick_ref.which_ref, s32[8]{0:T(128)} %get-tuple-element.80.valid_ref, s32[8]{0:T(128)} %get-tuple-element.81.pick_ref.which_ref, ...), custom_call_target="tpu_custom_call" | custom-call | flops 2147483648 | bytes 4718592 | tf_op jit(solution)/shard_map/pallas_call | solution.py:73
  170.2 22.5 %collective-permute-start.15 = (bf16[2,8,128,128]{3,2,1,0:T(8,128)(2,1)}, bf16[2,8,128,128]{3,2,1,0:T(8,128)(2,1)}, u32[]{:S(2)}, u32[]{:S(2)}) collective-permute-start(bf16[2,8,128,128]{3,2,1,0:T(8,128)(2,1)} %bitcast.208), channel_id=1, source_target_pairs={{0,24},{4,28},{8,0},{12,4},{16,8},{20,12},{24,16},{28,20},{1,25},{... | collective-permute-start | bytes 1572872 | tf_op jit(solution)/shard_map/ppermute | solution.py:171
  192.8 20.6 %shard_map.68 = (bf16[1,2,1024,128]{3,2,1,0:T(8,128)(2,1)}, f32[1,2,8,128]{3,2,1,0:T(8,128)}, f32[1,2,8,128]{3,2,1,0:T(8,128)}) custom-call(s32[8]{0:T(128)} %get-tuple-element.79.rows_ref, s32[8]{0:T(128)} %get-tuple-element.78.pick_ref.which_ref, s32[8]{0:T(128)} %get-tuple-element.77.valid_ref, s32[8]{0:T(128)} %get-tuple-element.78.pick_ref.which_ref, ...), custom_call_target="tpu_custom_call" | custom-call | flops 2147483648 | bytes 4718592 | tf_op jit(solution)/shard_map/pallas_call | solution.py:73
  213.4 18.3 %collective-permute-start.16 = (bf16[2,8,128,128]{3,2,1,0:T(8,128)(2,1)}, bf16[2,8,128,128]{3,2,1,0:T(8,128)(2,1)}, u32[]{:S(2)}, u32[]{:S(2)}) collective-permute-start(bf16[2,8,128,128]{3,2,1,0:T(8,128)(2,1)} %bitcast.209), channel_id=1, source_target_pairs={{0,20},{4,24},{8,28},{12,0},{16,4},{20,8},{24,12},{28,16},{1,21},{... | collective-permute-start | bytes 1572872 | tf_op jit(solution)/shard_map/ppermute | solution.py:171
  231.7 12.2 %shard_map.69 = (bf16[1,2,1024,128]{3,2,1,0:T(8,128)(2,1)}, f32[1,2,8,128]{3,2,1,0:T(8,128)}, f32[1,2,8,128]{3,2,1,0:T(8,128)}) custom-call(s32[8]{0:T(128)} %get-tuple-element.76.rows_ref, s32[8]{0:T(128)} %get-tuple-element.75.pick_ref.which_ref, s32[8]{0:T(128)} %get-tuple-element.74.valid_ref, s32[8]{0:T(128)} %get-tuple-element.75.pick_ref.which_ref, ...), custom_call_target="tpu_custom_call" | custom-call | flops 2147483648 | bytes 4718592 | tf_op jit(solution)/shard_map/pallas_call | solution.py:73
  243.9 0.7 pad_maximum_fusion.4
  244.6 12.2 %shard_map.70 = (bf16[1,2,1024,128]{3,2,1,0:T(8,128)(2,1)}, f32[1,2,8,128]{3,2,1,0:T(8,128)}, f32[1,2,8,128]{3,2,1,0:T(8,128)}) custom-call(s32[8]{0:T(128)} %get-tuple-element.73.rows_ref, s32[8]{0:T(128)} %get-tuple-element.72.pick_ref.which_ref, s32[8]{0:T(128)} %get-tuple-element.71.valid_ref, s32[8]{0:T(128)} %get-tuple-element.72.pick_ref.which_ref, ...), custom_call_target="tpu_custom_call" | custom-call | flops 2147483648 | bytes 4718592 | tf_op jit(solution)/shard_map/pallas_call | solution.py:73
  256.8 0.7 pad_maximum_fusion.5
  257.6 4.3 collective-permute-start.1
  261.8 12.2 %shard_map.71 = (bf16[1,2,1024,128]{3,2,1,0:T(8,128)(2,1)}, f32[1,2,8,128]{3,2,1,0:T(8,128)}, f32[1,2,8,128]{3,2,1,0:T(8,128)}) custom-call(s32[8]{0:T(128)} %get-tuple-element.70.rows_ref, s32[8]{0:T(128)} %get-tuple-element.69.pick_ref.which_ref, s32[8]{0:T(128)} %get-tuple-element.68.valid_ref, s32[8]{0:T(128)} %get-tuple-element.69.pick_ref.which_ref, ...), custom_call_target="tpu_custom_call" | custom-call | flops 2147483648 | bytes 4718592 | tf_op jit(solution)/shard_map/pallas_call | solution.py:73
  274.8 1.9 collective-permute-done.1
  276.7 37.4 %collective-permute-start.3 = (f32[2,2,8,128]{3,2,0,1:T(8,128)S(1)}, f32[2,2,8,128]{3,2,0,1:T(8,128)S(1)}, u32[]{:S(2)}, u32[]{:S(2)}) collective-permute-start(f32[2,2,8,128]{3,2,0,1:T(8,128)S(1)} %pad_maximum_fusion.1), channel_id=1, source_target_pairs={{0,24},{4,28},{8,0},{12,4},{16,8},{20,12},{24,16},{28,20},{1,25},{... | collective-permute-start | bytes 49160 | tf_op jit(solution)/shard_map/ppermute | solution.py:172
  314.1 1.4 collective-permute-done.3
  315.5 0.8 collective-permute-start.5
  316.4 3.8 collective-permute-done.5
  320.2 0.8 collective-permute-start.7
  321.0 3.8 collective-permute-done.7
  324.8 2.6 collective-permute-start.9
  327.5 2.9 collective-permute-done.9
  330.4 3.5 collective-permute-start.11
  333.9 4.3 collective-permute-done.11
  338.2 1.3 collective-permute-start.13
  339.5 5.4 collective-permute-done.13
  344.9 1.6 collective-permute-start.18
  346.8 1.9 bitcast_dynamic-update-slice_fusion.6
  348.7 0.9 collective-permute-start.20
  349.6 1.9 bitcast_dynamic-update-slice_fusion.5
  351.5 1.9 bitcast_dynamic-update-slice_fusion.4
  353.3 1.9 bitcast_dynamic-update-slice_fusion.3
  355.2 29.1 %collective-permute-done.18 = bf16[2,8,128,128]{3,2,1,0:T(8,128)(2,1)S(1)} collective-permute-done((bf16[2,8,128,128]{3,2,1,0:T(8,128)(2,1)}, bf16[2,8,128,128]{3,2,1,0:T(8,128)(2,1)S(1)}, u32[]{:S(2)}, u32[]{:S(2)}) %collective-permute-start.18) | collective-permute-done | bytes 524320 | tf_op jit(solution)/shard_map/ppermute | solution.py:171
  384.4 0.8 bitcast_dynamic-update-slice_fusion.2
  385.2 0.8 bitcast_dynamic-update-slice_fusion.1
  386.0 0.8 bitcast_dynamic-update-slice_fusion
  386.9 4.5 multiply_reduce_fusion
  391.4 0.9 fusion.4
  392.6 0.9 copy.35
  393.6 70.7 %all-gather.2.cloned.1.call-done = bf16[2048,1024]{1,0:T(8,128)(2,1)} async-done(((bf16[256,1024]{1,0:T(8,128)(2,1)}), bf16[2048,1024]{1,0:T(8,128)(2,1)}) %all-gather.2.cloned.1.call-update) | async-done | bytes 4194320 | tf_op jit(solution)/shard_map/all_gather | solution.py:199
  464.3 8.3 %convolution_convert_fusion = bf16[2048,1024]{1,0:T(8,128)(2,1)} fusion(bf16[2048,1024]{1,0:T(8,128)(2,1)} %all-gather.2.cloned.1.call-done, bf16[1024,1024]{1,0:T(8,128)(2,1)S(1)} %copy-done), kind=kOutput, calls=%fused_computation.1 | convolution fusion | flops 4297064448 | bytes 10485760 | tf_op jit(solution)/shard_map/dot_general | solution.py:200
  472.7 41.7 %reduce-scatter.2.cloned.1.call-done = bf16[512,1024]{1,0:T(8,128)(2,1)} async-done(((bf16[2048,1024]{1,0:T(8,128)(2,1)}), bf16[512,1024]{1,0:T(8,128)(2,1)}) %reduce-scatter.2.cloned.1.call-update) | async-done | bytes 1048592 | tf_op jit(solution)/shard_map/reduce_scatter | solution.py:201
  514.5 2.2 constant_dynamic-slice_fusion
  516.7 5.5 collective-permute-start.21
  522.2 1.5 collective-permute-start.22
  523.6 34.2 %collective-permute-done.21 = bf16[256,1024]{1,0:T(8,128)(2,1)S(1)} collective-permute-done((bf16[256,1024]{1,0:T(8,128)(2,1)}, bf16[256,1024]{1,0:T(8,128)(2,1)S(1)}, u32[]{:S(2)}, u32[]{:S(2)}) %collective-permute-start.21) | collective-permute-done | bytes 524320 | tf_op jit(solution)/shard_map/ppermute | solution.py:216
  558.0 11.6 %collective-permute-done.22 = bf16[256,1024]{1,0:T(8,128)(2,1)S(1)} collective-permute-done((bf16[256,1024]{1,0:T(8,128)(2,1)}, bf16[256,1024]{1,0:T(8,128)(2,1)S(1)}, u32[]{:S(2)}, u32[]{:S(2)}) %collective-permute-start.22) | collective-permute-done | bytes 524320 | tf_op jit(solution)/shard_map/ppermute | solution.py:216
  569.7 0.8 constant_dynamic-update-slice_fusion.10
  (73 shorter events, 7.5 us)
Async XLA Ops:
  6.5 457.8 %copy-start = (bf16[1024,1024]{1,0:T(8,128)(2,1)S(1)}, bf16[1024,1024]{1,0:T(8,128)(2,1)}, u32[]{:S(2)}) copy-start(bf16[1024,1024]{1,0:T(8,128)(2,1)} %param.9) | copy-start | bytes 6291460
  6.5 106.7 %collective-permute-start = (bf16[2,128,1024]{2,1,0:T(8,128)(2,1)}, bf16[2,128,1024]{2,1,0:T(8,128)(2,1)}, u32[]{:S(2)}, u32[]{:S(2)}) collective-permute-start(bf16[2,128,1024]{2,1,0:T(8,128)(2,1)} %bitcast.179), channel_id=1, source_target_pairs={{0,4},{4,8},{8,12},{12,16},{16,20},{20,24},{24,28},{28,0},{1,5},{5... | collective-permute-start | bytes 1572872 | tf_op jit(solution)/shard_map/ppermute | solution.py:160
  8.0 115.3 %collective-permute-start.2 = (bf16[2,128,1024]{2,1,0:T(8,128)(2,1)}, bf16[2,128,1024]{2,1,0:T(8,128)(2,1)}, u32[]{:S(2)}, u32[]{:S(2)}) collective-permute-start(bf16[2,128,1024]{2,1,0:T(8,128)(2,1)} %bitcast.180), channel_id=1, source_target_pairs={{0,8},{4,12},{8,16},{12,20},{16,24},{20,28},{24,0},{28,4},{1,9},{5... | collective-permute-start | bytes 1572872 | tf_op jit(solution)/shard_map/ppermute | solution.py:160
  9.6 145.6 %collective-permute-start.4 = (bf16[2,128,1024]{2,1,0:T(8,128)(2,1)}, bf16[2,128,1024]{2,1,0:T(8,128)(2,1)}, u32[]{:S(2)}, u32[]{:S(2)}) collective-permute-start(bf16[2,128,1024]{2,1,0:T(8,128)(2,1)} %bitcast.181), channel_id=1, source_target_pairs={{0,12},{4,16},{8,20},{12,24},{16,28},{20,0},{24,4},{28,8},{1,13},{... | collective-permute-start | bytes 1572872 | tf_op jit(solution)/shard_map/ppermute | solution.py:160
  12.2 158.0 %collective-permute-start.6 = (bf16[2,128,1024]{2,1,0:T(8,128)(2,1)}, bf16[2,128,1024]{2,1,0:T(8,128)(2,1)}, u32[]{:S(2)}, u32[]{:S(2)}) collective-permute-start(bf16[2,128,1024]{2,1,0:T(8,128)(2,1)} %bitcast.182), channel_id=1, source_target_pairs={{0,16},{4,20},{8,24},{12,28},{16,0},{20,4},{24,8},{28,12},{1,17},{... | collective-permute-start | bytes 1572872 | tf_op jit(solution)/shard_map/ppermute | solution.py:160
  13.4 200.0 %collective-permute-start.8 = (bf16[2,128,1024]{2,1,0:T(8,128)(2,1)}, bf16[2,128,1024]{2,1,0:T(8,128)(2,1)}, u32[]{:S(2)}, u32[]{:S(2)}) collective-permute-start(bf16[2,128,1024]{2,1,0:T(8,128)(2,1)} %bitcast.183), channel_id=1, source_target_pairs={{0,20},{4,24},{8,28},{12,0},{16,4},{20,8},{24,12},{28,16},{1,21},{... | collective-permute-start | bytes 1572872 | tf_op jit(solution)/shard_map/ppermute | solution.py:160
  18.8 72.1 %all-to-all-start = ((s32[3,8,8]{2,0,1:T(4,128)}), s32[3,8,8]{2,0,1:T(4,128)S(1)}, u32[]{:S(2)}, u32[]{:S(2)}) async-start(s32[3,8,8]{2,0,1:T(4,128)} %copy.19), calls=%async_computation | async-start | bytes 32768 | tf_op jit(solution)/shard_map/all_to_all | solution.py:148
  22.1 442.2 %all-gather.2.cloned.1.call-start = ((), (), s32[]{:S(2)}) async-start(), calls=%async_computation.2 | async-start | bytes 4718592 | tf_op jit(solution)/shard_map/all_gather | solution.py:199
  113.2 131.4 %collective-permute-start.10 = (bf16[2,128,1024]{2,1,0:T(8,128)(2,1)}, bf16[2,128,1024]{2,1,0:T(8,128)(2,1)}, u32[]{:S(2)}, u32[]{:S(2)}) collective-permute-start(bf16[2,128,1024]{2,1,0:T(8,128)(2,1)} %bitcast.186), channel_id=1, source_target_pairs={{0,24},{4,28},{8,0},{12,4},{16,8},{20,12},{24,16},{28,20},{1,25},{... | collective-permute-start | bytes 1572872 | tf_op jit(solution)/shard_map/ppermute | solution.py:160
  123.3 134.3 %collective-permute-start.12 = (bf16[2,128,1024]{2,1,0:T(8,128)(2,1)}, bf16[2,128,1024]{2,1,0:T(8,128)(2,1)}, u32[]{:S(2)}, u32[]{:S(2)}) collective-permute-start(bf16[2,128,1024]{2,1,0:T(8,128)(2,1)} %bitcast.187), channel_id=1, source_target_pairs={{0,28},{4,0},{8,4},{12,8},{16,12},{20,16},{24,20},{28,24},{1,29},{... | collective-permute-start | bytes 1572872 | tf_op jit(solution)/shard_map/ppermute | solution.py:160
  155.2 191.5 %collective-permute-start.14 = (bf16[2,8,128,128]{3,2,1,0:T(8,128)(2,1)}, bf16[2,8,128,128]{3,2,1,0:T(8,128)(2,1)}, u32[]{:S(2)}, u32[]{:S(2)}) collective-permute-start(bf16[2,8,128,128]{3,2,1,0:T(8,128)(2,1)} %bitcast.207), channel_id=1, source_target_pairs={{0,28},{4,0},{8,4},{12,8},{16,12},{20,16},{24,20},{28,24},{1,29},{... | collective-permute-start | bytes 1572872 | tf_op jit(solution)/shard_map/ppermute | solution.py:171
  170.2 43.2 %copy-start.5 = (f32[1,2,8,128]{3,2,1,0:T(8,128)S(1)}, f32[1,2,8,128]{3,2,1,0:T(8,128)}, u32[]{:S(2)}) copy-start(f32[1,2,8,128]{3,2,1,0:T(8,128)} %get-tuple-element.35) | copy-start | bytes 24580
  170.2 43.2 %copy-start.6 = (f32[1,2,8,128]{3,2,1,0:T(8,128)S(1)}, f32[1,2,8,128]{3,2,1,0:T(8,128)}, u32[]{:S(2)}) copy-start(f32[1,2,8,128]{3,2,1,0:T(8,128)} %get-tuple-element.36) | copy-start | bytes 24580
  170.2 178.4 %collective-permute-start.15 = (bf16[2,8,128,128]{3,2,1,0:T(8,128)(2,1)}, bf16[2,8,128,128]{3,2,1,0:T(8,128)(2,1)}, u32[]{:S(2)}, u32[]{:S(2)}) collective-permute-start(bf16[2,8,128,128]{3,2,1,0:T(8,128)(2,1)} %bitcast.208), channel_id=1, source_target_pairs={{0,24},{4,28},{8,0},{12,4},{16,8},{20,12},{24,16},{28,20},{1,25},{... | collective-permute-start | bytes 1572872 | tf_op jit(solution)/shard_map/ppermute | solution.py:171
  213.4 30.5 %copy-start.3 = (f32[1,2,8,128]{3,2,1,0:T(8,128)S(1)}, f32[1,2,8,128]{3,2,1,0:T(8,128)}, u32[]{:S(2)}) copy-start(f32[1,2,8,128]{3,2,1,0:T(8,128)} %get-tuple-element.37) | copy-start | bytes 24580
  213.4 30.5 %copy-start.4 = (f32[1,2,8,128]{3,2,1,0:T(8,128)S(1)}, f32[1,2,8,128]{3,2,1,0:T(8,128)}, u32[]{:S(2)}) copy-start(f32[1,2,8,128]{3,2,1,0:T(8,128)} %get-tuple-element.38) | copy-start | bytes 24580
  213.4 138.0 %collective-permute-start.16 = (bf16[2,8,128,128]{3,2,1,0:T(8,128)(2,1)}, bf16[2,8,128,128]{3,2,1,0:T(8,128)(2,1)}, u32[]{:S(2)}, u32[]{:S(2)}) collective-permute-start(bf16[2,8,128,128]{3,2,1,0:T(8,128)(2,1)} %bitcast.209), channel_id=1, source_target_pairs={{0,20},{4,24},{8,28},{12,0},{16,4},{20,8},{24,12},{28,16},{1,21},{... | collective-permute-start | bytes 1572872 | tf_op jit(solution)/shard_map/ppermute | solution.py:171
  244.6 108.7 %collective-permute-start.17 = (bf16[2,8,128,128]{3,2,1,0:T(8,128)(2,1)}, bf16[2,8,128,128]{3,2,1,0:T(8,128)(2,1)}, u32[]{:S(2)}, u32[]{:S(2)}) collective-permute-start(bf16[2,8,128,128]{3,2,1,0:T(8,128)(2,1)} %bitcast.210), channel_id=1, source_target_pairs={{0,16},{4,20},{8,24},{12,28},{16,0},{20,4},{24,8},{28,12},{1,17},{... | collective-permute-start | bytes 1572872 | tf_op jit(solution)/shard_map/ppermute | solution.py:171
  257.6 19.1 %collective-permute-start.1 = (f32[2,2,8,128]{3,2,0,1:T(8,128)S(1)}, f32[2,2,8,128]{3,2,0,1:T(8,128)S(1)}, u32[]{:S(2)}, u32[]{:S(2)}) collective-permute-start(f32[2,2,8,128]{3,2,0,1:T(8,128)S(1)} %pad_maximum_fusion), channel_id=1, source_target_pairs={{0,28},{4,0},{8,4},{12,8},{16,12},{20,16},{24,20},{28,24},{1,29},{... | collective-permute-start | bytes 49160 | tf_op jit(solution)/shard_map/ppermute | solution.py:172
  276.7 38.8 %collective-permute-start.3 = (f32[2,2,8,128]{3,2,0,1:T(8,128)S(1)}, f32[2,2,8,128]{3,2,0,1:T(8,128)S(1)}, u32[]{:S(2)}, u32[]{:S(2)}) collective-permute-start(f32[2,2,8,128]{3,2,0,1:T(8,128)S(1)} %pad_maximum_fusion.1), channel_id=1, source_target_pairs={{0,24},{4,28},{8,0},{12,4},{16,8},{20,12},{24,16},{28,20},{1,25},{... | collective-permute-start | bytes 49160 | tf_op jit(solution)/shard_map/ppermute | solution.py:172
  315.5 4.6 collective-permute-start.5
  320.2 4.6 collective-permute-start.7
  324.8 5.5 collective-permute-start.9
  330.4 7.8 %collective-permute-start.11 = (f32[2,2,8,128]{3,2,0,1:T(8,128)S(1)}, f32[2,2,8,128]{3,2,0,1:T(8,128)S(1)}, u32[]{:S(2)}, u32[]{:S(2)}) collective-permute-start(f32[2,2,8,128]{3,2,0,1:T(8,128)S(1)} %pad_maximum_fusion.5), channel_id=1, source_target_pairs={{0,8},{4,12},{8,16},{12,20},{16,24},{20,28},{24,0},{28,4},{1,9},{5... | collective-permute-start | bytes 49160 | tf_op jit(solution)/shard_map/ppermute | solution.py:172
  338.2 6.7 %collective-permute-start.13 = (f32[2,2,8,128]{3,2,0,1:T(8,128)S(1)}, f32[2,2,8,128]{3,2,0,1:T(8,128)S(1)}, u32[]{:S(2)}, u32[]{:S(2)}) collective-permute-start(f32[2,2,8,128]{3,2,0,1:T(8,128)S(1)} %pad_maximum_fusion.6), channel_id=1, source_target_pairs={{0,4},{4,8},{8,12},{12,16},{16,20},{20,24},{24,28},{28,0},{1,5},{5... | collective-permute-start | bytes 49160 | tf_op jit(solution)/shard_map/ppermute | solution.py:172
  344.9 39.4 %collective-permute-start.18 = (bf16[2,8,128,128]{3,2,1,0:T(8,128)(2,1)}, bf16[2,8,128,128]{3,2,1,0:T(8,128)(2,1)S(1)}, u32[]{:S(2)}, u32[]{:S(2)}) collective-permute-start(bf16[2,8,128,128]{3,2,1,0:T(8,128)(2,1)} %bitcast.211), channel_id=1, source_target_pairs={{0,12},{4,16},{8,20},{12,24},{16,28},{20,0},{24,4},{28,8},{1,13},{... | collective-permute-start | bytes 1572872 | tf_op jit(solution)/shard_map/ppermute | solution.py:171
  346.7 38.5 %collective-permute-start.19 = (bf16[2,8,128,128]{3,2,1,0:T(8,128)(2,1)}, bf16[2,8,128,128]{3,2,1,0:T(8,128)(2,1)S(1)}, u32[]{:S(2)}, u32[]{:S(2)}) collective-permute-start(bf16[2,8,128,128]{3,2,1,0:T(8,128)(2,1)} %bitcast.212), channel_id=1, source_target_pairs={{0,8},{4,12},{8,16},{12,20},{16,24},{20,28},{24,0},{28,4},{1,9},{5... | collective-permute-start | bytes 1572872 | tf_op jit(solution)/shard_map/ppermute | solution.py:171
  348.7 37.4 %collective-permute-start.20 = (bf16[2,8,128,128]{3,2,1,0:T(8,128)(2,1)}, bf16[2,8,128,128]{3,2,1,0:T(8,128)(2,1)S(1)}, u32[]{:S(2)}, u32[]{:S(2)}) collective-permute-start(bf16[2,8,128,128]{3,2,1,0:T(8,128)(2,1)} %bitcast.213), channel_id=1, source_target_pairs={{0,4},{4,8},{8,12},{12,16},{16,20},{20,24},{24,28},{28,0},{1,5},{5... | collective-permute-start | bytes 1572872 | tf_op jit(solution)/shard_map/ppermute | solution.py:171
  355.2 36.1 %copy-start.2 = (bf16[256,256]{1,0:T(8,128)(2,1)S(1)}, bf16[256,256]{1,0:T(8,128)(2,1)}, u32[]{:S(2)}) copy-start(bf16[256,256]{1,0:T(8,128)(2,1)} %param.7) | copy-start | bytes 393220
  393.5 120.9 %reduce-scatter.2.cloned.1.call-start = ((), (), s32[]{:S(2)}) async-start(), calls=%async_computation.3 | async-start | bytes 5242880 | tf_op jit(solution)/shard_map/reduce_scatter | solution.py:201
  516.7 41.2 %collective-permute-start.21 = (bf16[256,1024]{1,0:T(8,128)(2,1)}, bf16[256,1024]{1,0:T(8,128)(2,1)S(1)}, u32[]{:S(2)}, u32[]{:S(2)}) collective-permute-start(bf16[256,1024]{1,0:T(8,128)(2,1)} %get-tuple-element.59), channel_id=1, source_target_pairs={{0,0},{1,8},{2,16},{3,24},{4,4},{5,12},{6,20},{7,28},{8,1},{9,9},{... | collective-permute-start | bytes 1572872 | tf_op jit(solution)/shard_map/ppermute | solution.py:216
  522.2 47.5 %collective-permute-start.22 = (bf16[256,1024]{1,0:T(8,128)(2,1)}, bf16[256,1024]{1,0:T(8,128)(2,1)S(1)}, u32[]{:S(2)}, u32[]{:S(2)}) collective-permute-start(bf16[256,1024]{1,0:T(8,128)(2,1)} %get-tuple-element.58), channel_id=1, source_target_pairs={{0,4},{1,12},{2,20},{3,28},{4,0},{5,8},{6,16},{7,24},{8,5},{9,13},... | collective-permute-start | bytes 1572872 | tf_op jit(solution)/shard_map/ppermute | solution.py:216
  558.0 11.6 %copy-start.1 = (bf16[256,2048]{1,0:T(8,128)(2,1)}, bf16[256,2048]{1,0:T(8,128)(2,1)S(1)}, u32[]{:S(2)}) copy-start(bf16[256,2048]{1,0:T(8,128)(2,1)S(1)} %constant_dynamic-update-slice_fusion.9) | copy-start | bytes 3145732
Sparse Core Ops, SparseCore 0:
  393.7 70.6 all-gather.1
  472.8 41.6 reduce-scatter.1

commit v6 on v4

--- a/solution.py
+++ b/solution.py
@@ -1,3 +1,4 @@
+import functools
 import math
 
 import jax
@@ -13,7 +14,7 @@
 FLOOR = -1e30
 
 
-def slot_kernel(rows_ref, pick_ref, valid_ref, which_ref, q_ref, kv_ref,
+def slot_kernel(only, rows_ref, pick_ref, valid_ref, which_ref, q_ref, kv_ref,
                 acc_out, peak_out, total_out, acc_sc, peak_sc, total_sc):
     r = pl.program_id(0)
     k = pl.program_id(1)
@@ -28,9 +29,9 @@
 
     i = r * cap + k
 
-    @pl.when(valid_ref[i] > 0)
+    @pl.when((valid_ref[i] > 0) & (which_ref[i] == only))
     def _():
-        j = which_ref[i]
+        j = 0
         keys = kv_ref[0, :, 0:HD]
         values = kv_ref[0, :, HD:2 * HD]
         q = jnp.concatenate([q_ref[0, :, h * HD:(h + 1) * HD] for h in range(heads)], axis=0)
@@ -64,14 +65,15 @@
                 )
 
 
-def slot_attention(rows, pick, valid, which, q_blocks, store, n_req, cap, n_query):
+def slot_attention(rows, pick, valid, which, q_blocks, store, n_req, cap, only):
+    n_query = 1
     width = q_blocks.shape[2]
     heads = width // HD
     n_slots = n_req * cap
     stacked = heads * QLEN
     flops = n_slots * heads * QLEN * PLEN * HD * 4
     return pl.pallas_call(
-        slot_kernel,
+        functools.partial(slot_kernel, only),
         out_shape=(
             jax.ShapeDtypeStruct((n_req, n_query, stacked, HD), jnp.bfloat16),
             jax.ShapeDtypeStruct((n_req, n_query, heads, QLEN), jnp.float32),
@@ -96,8 +98,8 @@
             ],
         ),
         cost_estimate=pl.CostEstimate(
-            flops=flops,
-            transcendentals=n_slots * heads * QLEN * PLEN,
+            flops=flops // 2,
+            transcendentals=n_slots * heads * QLEN * PLEN // 2,
             bytes_accessed=n_slots * (QLEN * width * 2 + PLEN * 2 * HD * 2)
             + n_req * n_query * stacked * HD * 2,
         ),
@@ -153,31 +155,31 @@
 
     everyone_q = lax.all_gather(queries, "cache", axis=0, tiled=True)
     q_blocks = everyone_q.reshape(n_cache * query_count, QLEN, width)
-    merged_acc, merged_peak, merged_total = slot_attention(
-        asked_rows, pick, asked[2].reshape(n_cache * capacity), asked_query.reshape(n_cache * capacity),
-        q_blocks, passage_store, n_cache, capacity, query_count,
-    )
-    merged_acc = merged_acc.reshape(n_cache, query_count, heads, QLEN, HD)
-    stats = jnp.stack([merged_peak, merged_total], axis=2)
-    back_acc = lax.all_to_all(
-        merged_acc, "cache", split_axis=0, concat_axis=0, tiled=True
-    )
-    back_stats = lax.all_to_all(stats, "cache", split_axis=0, concat_axis=0, tiled=True)
-
     own_acc, own_peak, own_total = own_part(
         queries.reshape(query_count, QLEN, width),
         own_kv.reshape(query_count, QLEN, own_kv.shape[1]),
     )
-    far_peak = back_stats[:, :, 0][..., None]
-    far_total = back_stats[:, :, 1][..., None]
-    top = jnp.maximum(jnp.max(far_peak, axis=0), own_peak)
-    far_scale = jnp.exp(far_peak - top[None])
-    own_scale = jnp.exp(own_peak - top)
-    numer = jnp.sum(far_scale * back_acc.astype(jnp.float32), axis=0) + own_scale * own_acc
-    denom = jnp.sum(far_scale * far_total, axis=0) + own_scale * own_total
-    attended = (numer / denom).astype(jnp.bfloat16)
-    attended = jnp.transpose(attended, (0, 2, 1, 3)).reshape(query_count * QLEN, width)
-    return project(attended, out_weight)
+    outs = []
+    for only in range(query_count):
+        merged_acc, merged_peak, merged_total = slot_attention(
+            asked_rows, pick, asked[2].reshape(n_cache * capacity), asked_query.reshape(n_cache * capacity),
+            q_blocks, passage_store, n_cache, capacity, only,
+        )
+        merged_acc = merged_acc.reshape(n_cache, heads, QLEN, HD)
+        stats = jnp.stack([merged_peak[:, 0], merged_total[:, 0]], axis=1)
+        back_acc = lax.all_to_all(merged_acc, "cache", split_axis=0, concat_axis=0, tiled=True)
+        back_stats = lax.all_to_all(stats, "cache", split_axis=0, concat_axis=0, tiled=True)
+        far_peak = back_stats[:, 0][..., None]
+        far_total = back_stats[:, 1][..., None]
+        top = jnp.maximum(jnp.max(far_peak, axis=0), own_peak[only])
+        far_scale = jnp.exp(far_peak - top[None])
+        own_scale = jnp.exp(own_peak[only] - top)
+        numer = jnp.sum(far_scale * back_acc.astype(jnp.float32), axis=0) + own_scale * own_acc[only]
+        denom = jnp.sum(far_scale * far_total, axis=0) + own_scale * own_total[only]
+        attended = (numer / denom).astype(jnp.bfloat16)
+        attended = jnp.transpose(attended, (1, 0, 2)).reshape(QLEN, width)
+        outs.append(project(attended, out_weight))
+    return jnp.concatenate(outs, axis=0)
 
 
 def project(attended, out_weight):

time: 577 us -> 657 us (1.14)
  starting transfers between devices: 17.5 us -> 85.1 us
  Pallas kernels: 77.7 us -> 125 us
  waiting for transfers between devices: 318 us -> 285 us
  blocking collectives: 126 us -> 110 us
    all_to_all x1, blocking collectives: 126 us -> 59.2 us  [shards(): lax.all_to_all(stats, 'cache', split_axis=0, concat_axis=0, tiled=True)]
    all_to_all x0 -> x1, starting transfers between devices: none -> 58.8 us  [shards(): lax.all_to_all(stats, 'cache', split_axis=0, concat_axis=0, tiled=True)]
    all_to_all x1, waiting for transfers between devices: 90.8 us -> 40.5 us  [shards(): lax.all_to_all(merged_acc, 'cache', split_axis=0, concat_axis=0, tiled=True)]
    all_to_all x0 -> x1, blocking collectives: none -> 50.3 us  [shards(): lax.all_to_all(merged_acc, 'cache', split_axis=0, concat_axis=0, tiled=True)]
    pallas_call x1 -> x2, Pallas kernels: 77.7 us -> 125 us  [slot_attention(): pl.pallas_call(functools.partial(slot_kernel, only), out_shape=(jax.Shape...]
    all_gather x1 -> x2, waiting for transfers between devices: 72.5 us -> 95.2 us  [project(): everyone = lax.all_gather(attended, 'cache', axis=0, tiled=True)]
    ppermute x2 -> x4, waiting for transfers between devices: 45.9 us -> 29.2 us  [project(): got = lax.ppermute(piece, ('cache', 'stream'), perm)]
    reduce_scatter x1 -> x2, waiting for transfers between devices: 41.7 us -> 52.9 us  [project(): lax.psum_scatter(partial_sums.astype(jnp.bfloat16), 'stream', scatter_dim...]
  transfers between devices with their start and end apart: 7 -> 12, of which waited for: 7 -> 10; matrix products, arithmetic and copies ran while one was open for 1% -> 4% of each run, Pallas kernels for 0% -> 11%
where the time goes in v6:
time: 657 us; the launch traced here: 655 us
  waiting for transfers between devices  285 us (43%)
  Pallas kernels  125 us (19%)
  blocking collectives  110 us (17%)
  starting transfers between devices  85.1 us (13%)
  between operations  13.4 us (2%)
  other arithmetic  12.8 us (2%)
  local copies, waits for them, and re-layouts  12.4 us (2%)
  matrix products  11.3 us (2%)
    pallas_call x2, Pallas kernels, slot_attention(): pl.pallas_call(functools.partial(slot_kernel, only), out_shape=(jax.Shape...  125 us
    all_gather x2, waiting for transfers between devices, project(): everyone = lax.all_gather(attended, 'cache', axis=0, tiled=True)  95.2 us
    all_gather x1, waiting for transfers between devices, shards(): everyone_q = lax.all_gather(queries, 'cache', axis=0, tiled=True)  59.7 us
    all_to_all x1, blocking collectives, shards(): lax.all_to_all(stats, 'cache', split_axis=0, concat_axis=0, tiled=True)  59.2 us
    all_to_all x1, starting transfers between devices, shards(): lax.all_to_all(stats, 'cache', split_axis=0, concat_axis=0, tiled=True)  58.8 us
    reduce_scatter x2, waiting for transfers between devices, project(): lax.psum_scatter(partial_sums.astype(jnp.bfloat16), 'stream', scatter_dim...  52.9 us
    all_to_all x1, blocking collectives, shards(): lax.all_to_all(merged_acc, 'cache', split_axis=0, concat_axis=0, tiled=True)  50.3 us
    all_to_all x1, waiting for transfers between devices, shards(): lax.all_to_all(merged_acc, 'cache', split_axis=0, concat_axis=0, tiled=True)  40.5 us
  transfers between devices with their start and end apart: 12, of which 10 were waited for; matrix products, arithmetic and copies ran while one was open for 4% of the time, Pallas kernels for 11%

profile of v6, /device:TPU:4, one launch (start us, length us, event | category | flops | bytes accessed | tf_op | source)
XLA Modules:
  0.0 655.2 jit_solution(9444541688767349808)
XLA Ops:
  6.5 0.7 all-gather.4.cloned.1.call-update
  7.3 0.8 eq.56
  8.0 0.8 select_reduce_fusion.2
  8.9 0.2 convert_reduce_fusion.1
  9.1 0.1 select_reduce_fusion.1
  9.2 0.1 stack.18
  9.2 0.1 stack.19
  9.3 0.1 stack.20
  9.4 0.6 copy.20
  10.0 5.8 all-to-all-start
  15.8 0.1 add.115
  15.9 0.1 add.116
  16.0 6.5 all-to-all-done
  22.6 0.1 squeeze.23.which_ref
  22.6 0.7 reshape_squeeze.10.valid_ref
  23.3 0.6 reshape_squeeze.4.rows_ref
  23.8 0.6 add.117.pick_ref
  24.4 59.7 %all-gather.4.cloned.1.call-done = bf16[2048,1024]{1,0:T(8,128)(2,1)} async-done(((bf16[256,1024]{1,0:T(8,128)(2,1)}), bf16[2048,1024]{1,0:T(8,128)(2,1)}) %all-gather.4.cloned.1.call-update) | async-done | bytes 4194320 | tf_op jit(solution)/shard_map/all_gather | solution.py:156
  84.1 50.6 %shard_map.65 = (bf16[8,1,1024,128]{3,2,1,0:T(8,128)(2,1)}, f32[8,1,8,128]{3,2,1,0:T(8,128)}, f32[8,1,8,128]{3,2,1,0:T(8,128)}) custom-call(s32[64]{0:T(128)} %reshape_squeeze.4.rows_ref, s32[64]{0:T(128)} %add.117.pick_ref, s32[64]{0:T(128)} %reshape_squeeze.10.valid_ref, s32[64]{0:T(128)} %copy-done.4, bf16[16,128,1024]{2,1,0:T(8,128)(2,1)} %bitcast.127, ...), custom_call_target="tpu_custom_call" | custom-call | flops 8589934592 | bytes 35651584 | tf_op jit(solution)/shard_map/pallas_call | solution.py:75
  134.7 1.4 pad_maximum_fusion.2
  136.1 58.8 %all-to-all-start.3 = ((f32[8,2,8,128]{3,2,1,0:T(8,128)}), f32[8,2,8,128]{3,2,1,0:T(8,128)S(1)}, u32[]{:S(2)}, u32[]{:S(2)}) async-start(f32[8,2,8,128]{3,2,1,0:T(8,128)} %pad_maximum_fusion.2), calls=%async_computation.4 | async-start | bytes 131072 | tf_op jit(solution)/shard_map/all_to_all | solution.py:171
  194.9 74.6 %shard_map.64 = (bf16[8,1,1024,128]{3,2,1,0:T(8,128)(2,1)}, f32[8,1,8,128]{3,2,1,0:T(8,128)}, f32[8,1,8,128]{3,2,1,0:T(8,128)}) custom-call(s32[64]{0:T(128)} %reshape_squeeze.4.rows_ref, s32[64]{0:T(128)} %add.117.pick_ref, s32[64]{0:T(128)} %reshape_squeeze.10.valid_ref, s32[64]{0:T(128)} %copy-done.4, bf16[16,128,1024]{2,1,0:T(8,128)(2,1)} %bitcast.128, ...), custom_call_target="tpu_custom_call" | custom-call | flops 8589934592 | bytes 35651584 | tf_op jit(solution)/shard_map/pallas_call | solution.py:75
  269.5 0.8 pad_maximum_fusion.1
  270.3 0.0 all-to-all-done.3
  270.3 59.2 %all_to_all.25 = f32[8,2,8,128]{3,2,1,0:T(8,128)S(1)} all-to-all(f32[8,2,8,128]{3,2,1,0:T(8,128)S(1)} %pad_maximum_fusion.1), channel_id=1, replica_groups=mesh['cache'=8,'stream'=4] {'cache'}, dimensions={0} | all-to-all | bytes 131072 | tf_op jit(solution)/shard_map/all_to_all | solution.py:171
  329.5 50.3 %all_to_all.26 = bf16[8,8,128,128]{3,2,1,0:T(8,128)(2,1)} all-to-all(bf16[8,8,128,128]{3,2,1,0:T(8,128)(2,1)} %bitcast.121), channel_id=1, replica_groups=mesh['cache'=8,'stream'=4] {'cache'}, dimensions={0} | all-to-all | bytes 4194304 | tf_op jit(solution)/shard_map/all_to_all | solution.py:170
  379.8 4.5 all-to-all-start.2
  384.3 0.0 all-gather.6.cloned.1.call-start
  384.3 0.1 copy.35
  384.5 0.3 fusion.31
  384.8 0.2 fusion.2
  385.0 0.3 fusion.4
  385.5 0.9 copy-done.1
  386.4 2.1 multiply_reduce_fusion
  388.5 2.0 copy.27
  390.5 40.5 %all-to-all-done.2 = bf16[8,8,128,128]{3,2,1,0:T(8,128)(2,1)} async-done(((bf16[8,8,128,128]{3,2,1,0:T(8,128)(2,1)}), bf16[8,8,128,128]{3,2,1,0:T(8,128)(2,1)}, u32[]{:S(2)}, u32[]{:S(2)}) %all-to-all-start.2) | async-done | bytes 2097184 | tf_op jit(solution)/shard_map/all_to_all | solution.py:170
  431.0 3.3 multiply_reduce_fusion.1
  434.3 2.0 copy.25
  436.4 2.2 fusion.14
  438.6 0.0 all-gather.6.cloned.1.call-update
  438.6 0.0 all-gather.8.cloned.1.call-start
  438.6 0.7 all-gather.8.cloned.1.call-update
  439.3 0.0 reduce-scatter.3.cloned.1.call-start
  439.4 49.4 %all-gather.6.cloned.1.call-done = bf16[1024,1024]{0,1:T(8,128)(2,1)} async-done(((bf16[128,1024]{0,1:T(8,128)(2,1)}), bf16[1024,1024]{0,1:T(8,128)(2,1)}) %all-gather.6.cloned.1.call-update) | async-done | bytes 2097168 | tf_op jit(solution)/shard_map/all_gather | solution.py:190
  488.8 5.3 convolution_convert_fusion.1
  494.1 0.0 reduce-scatter.3.cloned.1.call-update
  494.1 0.2 reduce-scatter.5.cloned.1.call-start
  494.4 45.8 %all-gather.8.cloned.1.call-done = bf16[1024,1024]{0,1:T(8,128)(2,1)} async-done(((bf16[128,1024]{0,1:T(8,128)(2,1)}), bf16[1024,1024]{0,1:T(8,128)(2,1)}) %all-gather.8.cloned.1.call-update) | async-done | bytes 2097168 | tf_op jit(solution)/shard_map/all_gather | solution.py:190
  540.1 5.3 convolution_convert_fusion
  545.4 0.0 reduce-scatter.5.cloned.1.call-update
  545.5 25.5 %reduce-scatter.3.cloned.1.call-done = bf16[256,1024]{1,0:T(8,128)(2,1)} async-done(((bf16[1024,1024]{1,0:T(8,128)(2,1)}), bf16[256,1024]{1,0:T(8,128)(2,1)}) %reduce-scatter.3.cloned.1.call-update) | async-done | bytes 524304 | tf_op jit(solution)/shard_map/reduce_scatter | solution.py:192
  571.0 1.1 constant_dynamic-slice_fusion.2
  572.1 5.5 collective-permute-start
  577.5 27.4 %reduce-scatter.5.cloned.1.call-done = bf16[256,1024]{1,0:T(8,128)(2,1)} async-done(((bf16[1024,1024]{1,0:T(8,128)(2,1)}), bf16[256,1024]{1,0:T(8,128)(2,1)}) %reduce-scatter.5.cloned.1.call-update) | async-done | bytes 524304 | tf_op jit(solution)/shard_map/reduce_scatter | solution.py:192
  605.0 1.1 constant_dynamic-slice_fusion
  606.0 5.5 collective-permute-start.2
  611.5 1.5 collective-permute-start.1
  613.0 3.3 collective-permute-start.3
  616.4 19.5 %collective-permute-done.2 = bf16[128,1024]{1,0:T(8,128)(2,1)} collective-permute-done((bf16[128,1024]{1,0:T(8,128)(2,1)S(1)}, bf16[128,1024]{1,0:T(8,128)(2,1)}, u32[]{:S(2)}, u32[]{:S(2)}) %collective-permute-start.2) | collective-permute-done | bytes 262176 | tf_op jit(solution)/shard_map/ppermute | solution.py:207
  635.9 1.0 constant_dynamic-update-slice_fusion.1
  636.9 5.6 collective-permute-done.1
  642.5 1.0 constant_dynamic-update-slice_fusion.2
  643.4 4.2 collective-permute-done.3
  647.6 1.1 pad_maximum_fusion
  (29 shorter events, 0.3 us)
Async XLA Ops:
  6.5 482.2 %copy-start = (bf16[1024,1024]{1,0:T(8,128)(2,1)S(1)}, bf16[1024,1024]{1,0:T(8,128)(2,1)}, u32[]{:S(2)}) copy-start(bf16[1024,1024]{1,0:T(8,128)(2,1)} %param.9) | copy-start | bytes 6291460
  6.5 77.6 %all-gather.4.cloned.1.call-start = ((), (), s32[]{:S(2)}) async-start(), calls=%async_computation.7 | async-start | bytes 4718592 | tf_op jit(solution)/shard_map/all_gather | solution.py:156
  10.0 12.5 %all-to-all-start = ((s32[3,8,8]{2,0,1:T(4,128)}), s32[3,8,8]{2,0,1:T(4,128)S(1)}, u32[]{:S(2)}, u32[]{:S(2)}) async-start(s32[3,8,8]{2,0,1:T(4,128)} %copy.20), calls=%async_computation | async-start | bytes 32768 | tf_op jit(solution)/shard_map/all_to_all | solution.py:150
  22.6 61.5 %copy-start.4 = (s32[64]{0:T(128)}, s32[64]{0:T(128)S(1)}, u32[]{:S(2)}) copy-start(s32[64]{0:T(128)S(1)} %squeeze.23.which_ref) | copy-start | bytes 772
  136.1 134.2 %all-to-all-start.3 = ((f32[8,2,8,128]{3,2,1,0:T(8,128)}), f32[8,2,8,128]{3,2,1,0:T(8,128)S(1)}, u32[]{:S(2)}, u32[]{:S(2)}) async-start(f32[8,2,8,128]{3,2,1,0:T(8,128)} %pad_maximum_fusion.2), calls=%async_computation.4 | async-start | bytes 131072 | tf_op jit(solution)/shard_map/all_to_all | solution.py:171
  379.8 4.5 copy-start.2
  379.8 4.7 copy-start.3
  379.8 51.2 %all-to-all-start.2 = ((bf16[8,8,128,128]{3,2,1,0:T(8,128)(2,1)}), bf16[8,8,128,128]{3,2,1,0:T(8,128)(2,1)}, u32[]{:S(2)}, u32[]{:S(2)}) async-start(bf16[8,8,128,128]{3,2,1,0:T(8,128)(2,1)} %bitcast.120), calls=%async_computation.2 | async-start | bytes 4194304 | tf_op jit(solution)/shard_map/all_to_all | solution.py:170
  384.3 104.5 %all-gather.6.cloned.1.call-start = ((), (), s32[]{:S(2)}) async-start(), calls=%async_computation.8 | async-start | bytes 2359296 | tf_op jit(solution)/shard_map/all_gather | solution.py:190
  384.8 1.6 copy-start.1
  438.6 101.5 %all-gather.8.cloned.1.call-start = ((), (), s32[]{:S(2)}) async-start(), calls=%async_computation.10 | async-start | bytes 2359296 | tf_op jit(solution)/shard_map/all_gather | solution.py:190
  439.3 131.7 %reduce-scatter.3.cloned.1.call-start = ((), (), s32[]{:S(2)}) async-start(), calls=%async_computation.9 | async-start | bytes 2621440 | tf_op jit(solution)/shard_map/reduce_scatter | solution.py:192
  494.1 110.8 %reduce-scatter.5.cloned.1.call-start = ((), (), s32[]{:S(2)}) async-start(), calls=%async_computation.11 | async-start | bytes 2621440 | tf_op jit(solution)/shard_map/reduce_scatter | solution.py:192
  572.1 44.3 %collective-permute-start = (bf16[128,1024]{1,0:T(8,128)(2,1)S(1)}, bf16[128,1024]{1,0:T(8,128)(2,1)S(1)}, u32[]{:S(2)}, u32[]{:S(2)}) collective-permute-start(bf16[128,1024]{1,0:T(8,128)(2,1)S(1)} %get-tuple-element.30), channel_id=1, source_target_pairs={{0,0},{1,8},{2,16},{3,24},{4,4},{5,12},{6,20},{7,28},{8,1},{9,9},{... | collective-permute-start | bytes 786440 | tf_op jit(solution)/shard_map/ppermute | solution.py:207
  606.0 29.8 %collective-permute-start.2 = (bf16[128,1024]{1,0:T(8,128)(2,1)S(1)}, bf16[128,1024]{1,0:T(8,128)(2,1)}, u32[]{:S(2)}, u32[]{:S(2)}) collective-permute-start(bf16[128,1024]{1,0:T(8,128)(2,1)S(1)} %get-tuple-element.32), channel_id=1, source_target_pairs={{0,0},{1,8},{2,16},{3,24},{4,4},{5,12},{6,20},{7,28},{8,1},{9,9},{... | collective-permute-start | bytes 786440 | tf_op jit(solution)/shard_map/ppermute | solution.py:207
  611.5 30.9 %collective-permute-start.1 = (bf16[128,1024]{1,0:T(8,128)(2,1)S(1)}, bf16[128,1024]{1,0:T(8,128)(2,1)}, u32[]{:S(2)}, u32[]{:S(2)}) collective-permute-start(bf16[128,1024]{1,0:T(8,128)(2,1)S(1)} %get-tuple-element.29), channel_id=1, source_target_pairs={{0,4},{1,12},{2,20},{3,28},{4,0},{5,8},{6,16},{7,24},{8,5},{9,13},... | collective-permute-start | bytes 786440 | tf_op jit(solution)/shard_map/ppermute | solution.py:207
  613.0 34.6 %collective-permute-start.3 = (bf16[128,1024]{1,0:T(8,128)(2,1)S(1)}, bf16[128,1024]{1,0:T(8,128)(2,1)S(1)}, u32[]{:S(2)}, u32[]{:S(2)}) collective-permute-start(bf16[128,1024]{1,0:T(8,128)(2,1)S(1)} %get-tuple-element.31), channel_id=1, source_target_pairs={{0,4},{1,12},{2,20},{3,28},{4,0},{5,8},{6,16},{7,24},{8,5},{9,13},... | collective-permute-start | bytes 786440 | tf_op jit(solution)/shard_map/ppermute | solution.py:207
Sparse Core Ops, SparseCore 0:
  9.5 74.5 all-gather.3
  438.7 50.0 all-gather.5
  490.8 49.2 all-gather.7
  542.5 28.4 reduce-scatter.2
  573.5 31.3 reduce-scatter.4

commit v7 on v4

--- a/solution.py
+++ b/solution.py
@@ -13,12 +13,13 @@
 FLOOR = -1e30
 
 
-def slot_kernel(rows_ref, pick_ref, valid_ref, which_ref, q_ref, kv_ref,
+def slot_kernel(rows_ref, pick_ref, valid_ref, which_ref, q0_ref, kv0_ref, q1_ref, kv1_ref,
                 acc_out, peak_out, total_out, acc_sc, peak_sc, total_sc):
     r = pl.program_id(0)
     k = pl.program_id(1)
-    cap = pl.num_programs(1)
-    heads = q_ref.shape[2] // HD
+    pairs = pl.num_programs(1)
+    heads = q0_ref.shape[2] // HD
+    fold = math.log2(math.e) / math.sqrt(HD)
 
     @pl.when(k == 0)
     def _():
@@ -26,28 +27,29 @@
         peak_sc[...] = jnp.full_like(peak_sc, FLOOR)
         total_sc[...] = jnp.zeros_like(total_sc)
 
-    i = r * cap + k
-
-    @pl.when(valid_ref[i] > 0)
-    def _():
-        j = which_ref[i]
-        keys = kv_ref[0, :, 0:HD]
-        values = kv_ref[0, :, HD:2 * HD]
-        q = jnp.concatenate([q_ref[0, :, h * HD:(h + 1) * HD] for h in range(heads)], axis=0)
-        s = lax.dot_general(
-            q, keys, (((1,), (1,)), ((), ())), preferred_element_type=jnp.float32
-        ) * (1.0 / math.sqrt(HD))
-        old = peak_sc[j]
-        new = jnp.maximum(old, jnp.max(s, axis=1, keepdims=True))
-        fade = jnp.exp(old - new)
-        p = jnp.exp(s - new)
-        total_sc[j] = fade * total_sc[j] + jnp.sum(p, axis=1, keepdims=True)
-        acc_sc[j] = fade * acc_sc[j] + jnp.dot(
-            p.astype(jnp.bfloat16), values, preferred_element_type=jnp.float32
-        )
-        peak_sc[j] = new
-
-    @pl.when(k == cap - 1)
+    for half, q_ref, kv_ref in ((0, q0_ref, kv0_ref), (1, q1_ref, kv1_ref)):
+        i = (r * pairs + k) * 2 + half
+
+        @pl.when(valid_ref[i] > 0)
+        def _():
+            j = which_ref[i]
+            keys = kv_ref[0, :, 0:HD]
+            values = kv_ref[0, :, HD:2 * HD]
+            q = jnp.concatenate([q_ref[0, :, h * HD:(h + 1) * HD] for h in range(heads)], axis=0)
+            s = lax.dot_general(
+                q, keys, (((1,), (1,)), ((), ())), preferred_element_type=jnp.float32
+            )
+            old = peak_sc[j]
+            new = jnp.maximum(old, jnp.max(s, axis=1, keepdims=True))
+            fade = jnp.exp2((old - new) * fold)
+            p = jnp.exp2((s - new) * fold)
+            total_sc[j] = fade * total_sc[j] + jnp.sum(p, axis=1, keepdims=True)
+            acc_sc[j] = fade * acc_sc[j] + jnp.dot(
+                p.astype(jnp.bfloat16), values, preferred_element_type=jnp.float32
+            )
+            peak_sc[j] = new
+
+    @pl.when(k == pairs - 1)
     def _():
         acc_out[0] = acc_sc[...].astype(acc_out.dtype)
         eye = lax.broadcasted_iota(jnp.int32, (QLEN, QLEN), 0) == lax.broadcasted_iota(
@@ -58,7 +60,7 @@
                 rows = pl.ds(h * QLEN, QLEN)
                 peak_out[0, j, pl.ds(h, 1), :] = jnp.sum(
                     jnp.where(eye, peak_sc[j, rows, :], 0.0), axis=0, keepdims=True
-                )
+                ) * (1.0 / math.sqrt(HD))
                 total_out[0, j, pl.ds(h, 1), :] = jnp.sum(
                     jnp.where(eye, total_sc[j, rows, :], 0.0), axis=0, keepdims=True
                 )
@@ -68,8 +70,15 @@
     width = q_blocks.shape[2]
     heads = width // HD
     n_slots = n_req * cap
+    pairs = cap // 2
     stacked = heads * QLEN
     flops = n_slots * heads * QLEN * PLEN * HD * 4
+    q_spec = lambda half: pl.BlockSpec(
+        (1, QLEN, width), lambda r, k, rw, pk, vd, wh: (pk[(r * pairs + k) * 2 + half], 0, 0)
+    )
+    kv_spec = lambda half: pl.BlockSpec(
+        (1, PLEN, 2 * HD), lambda r, k, rw, pk, vd, wh: (rw[(r * pairs + k) * 2 + half], 0, 0)
+    )
     return pl.pallas_call(
         slot_kernel,
         out_shape=(
@@ -79,11 +88,8 @@
         ),
         grid_spec=pltpu.PrefetchScalarGridSpec(
             num_scalar_prefetch=4,
-            grid=(n_req, cap),
-            in_specs=[
-                pl.BlockSpec((1, QLEN, width), lambda r, k, rw, pk, vd, wh: (pk[r * cap + k], 0, 0)),
-                pl.BlockSpec((1, PLEN, 2 * HD), lambda r, k, rw, pk, vd, wh: (rw[r * cap + k], 0, 0)),
-            ],
+            grid=(n_req, pairs),
+            in_specs=[q_spec(0), kv_spec(0), q_spec(1), kv_spec(1)],
             out_specs=[
                 pl.BlockSpec((1, n_query, stacked, HD), lambda r, k, rw, pk, vd, wh: (r, 0, 0, 0)),
                 pl.BlockSpec((1, n_query, heads, QLEN), lambda r, k, rw, pk, vd, wh: (r, 0, 0, 0)),
@@ -101,7 +107,7 @@
             bytes_accessed=n_slots * (QLEN * width * 2 + PLEN * 2 * HD * 2)
             + n_req * n_query * stacked * HD * 2,
         ),
-    )(rows, pick, valid, which, q_blocks, store)
+    )(rows, pick, valid, which, q_blocks, store, q_blocks, store)
 
 
 def own_part(query_rows, own_rows):
@@ -131,6 +137,7 @@
     heads = width // HD
     wanted_count = query_count * per_query
     capacity = max(2, (2 * wanted_count + n_cache - 1) // n_cache)
+    capacity += capacity % 2
     wanted = retrieved.reshape(wanted_count)
     id_match = wanted[:, None] == jnp.arange(slot_total, dtype=jnp.int32)[None, :]
     store_slots = jnp.sum(jnp.where(id_match, passage_slot[None, :], 0), axis=1)

time: 577 us -> 578 us (level)
  Pallas kernels: 77.7 us -> 94.7 us
  blocking collectives: 126 us -> 109 us
    pallas_call x1, Pallas kernels: 77.7 us -> 94.7 us  [slot_attention(): pl.pallas_call(slot_kernel, out_shape=(jax.ShapeDtypeStruct((n_req, n_que...]
    all_to_all x1, blocking collectives: 126 us -> 109 us  [shards(): lax.all_to_all(stats, 'cache', split_axis=0, concat_axis=0, tiled=True)]
where the time goes in v7:
time: 578 us; the launch traced here: 577 us
  waiting for transfers between devices  318 us (55%)
  blocking collectives  109 us (19%)
  Pallas kernels  94.7 us (16%)
  starting transfers between devices  17.5 us (3%)
  between operations  13.3 us (2%)
  matrix products  9.57 us (2%)
  local copies, waits for them, and re-layouts  7.67 us (1%)
  other arithmetic  7.34 us (1%)
    all_to_all x1, blocking collectives, shards(): lax.all_to_all(stats, 'cache', split_axis=0, concat_axis=0, tiled=True)  109 us
    pallas_call x1, Pallas kernels, slot_attention(): pl.pallas_call(slot_kernel, out_shape=(jax.ShapeDtypeStruct((n_req, n_que...  94.7 us
    all_to_all x1, waiting for transfers between devices, shards(): lax.all_to_all(merged_acc, 'cache', split_axis=0, concat_axis=0, tiled=True)  90.8 us
    all_gather x1, waiting for transfers between devices, project(): everyone = lax.all_gather(attended, 'cache', axis=0, tiled=True)  72.5 us
    all_gather x1, waiting for transfers between devices, shards(): everyone_q = lax.all_gather(queries, 'cache', axis=0, tiled=True)  59.7 us
    ppermute x2, waiting for transfers between devices, project(): got = lax.ppermute(piece, ('cache', 'stream'), perm)  45.9 us
    reduce_scatter x1, waiting for transfers between devices, project(): lax.psum_scatter(partial_sums.astype(jnp.bfloat16), 'stream', scatter_dim...  41.7 us
  transfers between devices with their start and end apart: 7, of which 7 were waited for; matrix products, arithmetic and copies ran while one was open for 1% of the time, Pallas kernels for 0%

profile of v7, /device:TPU:4, one launch (start us, length us, event | category | flops | bytes accessed | tf_op | source)
XLA Modules:
  0.0 576.8 jit_solution(3973168291913850394)
XLA Ops:
  6.5 0.0 copy-start
  6.5 0.0 all-gather.3.cloned.1.call-start
  6.5 0.7 all-gather.3.cloned.1.call-update
  7.3 0.8 eq.50
  8.0 0.8 select_reduce_fusion.2
  8.9 0.2 convert_reduce_fusion.1
  9.1 0.1 select_reduce_fusion.1
  9.2 0.1 stack.21
  9.2 0.1 stack.23
  9.3 0.1 stack.22
  9.4 0.6 copy.18
  10.0 5.8 %all-to-all-start = ((s32[3,8,8]{2,0,1:T(4,128)}), s32[3,8,8]{2,0,1:T(4,128)S(1)}, u32[]{:S(2)}, u32[]{:S(2)}) async-start(s32[3,8,8]{2,0,1:T(4,128)} %copy.18), calls=%async_computation | async-start | bytes 32768 | tf_op jit(solution)/shard_map/all_to_all | solution.py:155
  15.8 0.1 add.93
  15.9 0.1 add.94
  16.0 6.5 %all-to-all-done = s32[3,8,8]{2,0,1:T(4,128)S(1)} async-done(((s32[3,8,8]{2,0,1:T(4,128)}), s32[3,8,8]{2,0,1:T(4,128)S(1)}, u32[]{:S(2)}, u32[]{:S(2)}) %all-to-all-start) | async-done | bytes 800 | tf_op jit(solution)/shard_map/all_to_all | solution.py:155
  22.6 0.6 reshape_squeeze.8.valid_ref
  23.2 0.1 squeeze.3.which_ref
  23.3 0.0 copy-start.4
  23.3 0.6 reshape_squeeze.7.rows_ref
  23.8 0.6 add.95.pick_ref
  24.4 59.7 %all-gather.3.cloned.1.call-done = bf16[2048,1024]{1,0:T(8,128)(2,1)} async-done(((bf16[256,1024]{1,0:T(8,128)(2,1)}), bf16[2048,1024]{1,0:T(8,128)(2,1)}) %all-gather.3.cloned.1.call-update) | async-done | bytes 4194320 | tf_op jit(solution)/shard_map/all_gather | solution.py:161
  84.1 0.0 copy-done.4
  84.1 94.7 %shard_map.64 = (bf16[8,2,1024,128]{3,2,1,0:T(8,128)(2,1)}, f32[8,2,8,128]{3,2,1,0:T(8,128)}, f32[8,2,8,128]{3,2,1,0:T(8,128)}) custom-call(s32[64]{0:T(128)} %reshape_squeeze.7.rows_ref, s32[64]{0:T(128)} %add.95.pick_ref, s32[64]{0:T(128)} %reshape_squeeze.8.valid_ref, s32[64]{0:T(128)} %copy-done.4, bf16[16,128,1024]{2,1,0:T(8,128)(2,1)} %bitcast.84, ...), custom_call_target="tpu_custom_call" | custom-call | flops 17179869184 | bytes 37748736 | tf_op jit(solution)/shard_map/pallas_call | solution.py:82
  178.8 0.9 pad_maximum_fusion
  179.7 108.8 %all_to_all.15 = f32[8,2,2,8,128]{4,3,1,2,0:T(8,128)S(1)} all-to-all(f32[8,2,2,8,128]{4,3,1,2,0:T(8,128)S(1)} %copy.19), channel_id=1, replica_groups=mesh['cache'=8,'stream'=4] {'cache'}, dimensions={0} | all-to-all | bytes 262144 | tf_op jit(solution)/shard_map/all_to_all | solution.py:172
  288.5 0.0 copy-start.1
  288.5 0.0 copy-start.3
  288.5 4.7 all-to-all-start.2
  293.2 0.0 all-gather.5.cloned.1.call-start
  293.2 0.0 copy-done.1
  293.3 0.1 copy.28
  293.4 0.0 copy-done.3
  293.4 0.3 fusion.19
  293.7 0.2 fusion.6
  294.0 90.8 %all-to-all-done.2 = bf16[8,2,8,128,128]{4,3,2,1,0:T(8,128)(2,1)} async-done(((bf16[8,2,8,128,128]{4,3,2,1,0:T(8,128)(2,1)}), bf16[8,2,8,128,128]{4,3,2,1,0:T(8,128)(2,1)}, u32[]{:S(2)}, u32[]{:S(2)}) %all-to-all-start.2) | async-done | bytes 4194336 | tf_op jit(solution)/shard_map/all_to_all | solution.py:169
  384.8 4.5 multiply_reduce_fusion
  389.3 0.9 fusion.5
  390.2 0.3 copy.23
  390.6 0.9 copy.35
  391.5 0.0 all-gather.5.cloned.1.call-update
  391.5 0.0 reduce-scatter.2.cloned.1.call-start
  391.6 72.5 %all-gather.5.cloned.1.call-done = bf16[2048,1024]{1,0:T(8,128)(2,1)} async-done(((bf16[256,1024]{1,0:T(8,128)(2,1)}), bf16[2048,1024]{1,0:T(8,128)(2,1)}) %all-gather.5.cloned.1.call-update) | async-done | bytes 4194320 | tf_op jit(solution)/shard_map/all_gather | solution.py:195
  464.1 0.0 copy-done
  464.1 8.3 %convolution_convert_fusion = bf16[2048,1024]{1,0:T(8,128)(2,1)} fusion(bf16[2048,1024]{1,0:T(8,128)(2,1)} %all-gather.5.cloned.1.call-done, bf16[1024,1024]{1,0:T(8,128)(2,1)S(1)} %copy-done), kind=kOutput, calls=%fused_computation.1 | convolution fusion | flops 4297064448 | bytes 10485760 | tf_op jit(solution)/shard_map/dot_general | solution.py:196
  472.4 0.0 reduce-scatter.2.cloned.1.call-update
  472.5 41.7 %reduce-scatter.2.cloned.1.call-done = bf16[512,1024]{1,0:T(8,128)(2,1)} async-done(((bf16[2048,1024]{1,0:T(8,128)(2,1)}), bf16[512,1024]{1,0:T(8,128)(2,1)}) %reduce-scatter.2.cloned.1.call-update) | async-done | bytes 1048592 | tf_op jit(solution)/shard_map/reduce_scatter | solution.py:197
  514.2 2.2 constant_dynamic-slice_fusion
  516.4 5.5 collective-permute-start
  521.9 1.5 collective-permute-start.1
  523.4 34.2 %collective-permute-done = bf16[256,1024]{1,0:T(8,128)(2,1)S(1)} collective-permute-done((bf16[256,1024]{1,0:T(8,128)(2,1)}, bf16[256,1024]{1,0:T(8,128)(2,1)S(1)}, u32[]{:S(2)}, u32[]{:S(2)}) %collective-permute-start) | collective-permute-done | bytes 524320 | tf_op jit(solution)/shard_map/ppermute | solution.py:212
  557.6 0.1 broadcast_in_dim.57
  557.7 0.1 constant_dynamic-update-slice_fusion.1
  557.8 0.0 copy-start.2
  557.8 11.6 %collective-permute-done.1 = bf16[256,1024]{1,0:T(8,128)(2,1)S(1)} collective-permute-done((bf16[256,1024]{1,0:T(8,128)(2,1)}, bf16[256,1024]{1,0:T(8,128)(2,1)S(1)}, u32[]{:S(2)}, u32[]{:S(2)}) %collective-permute-start.1) | collective-permute-done | bytes 524320 | tf_op jit(solution)/shard_map/ppermute | solution.py:212
  569.4 0.0 copy-done.2
  569.4 0.8 constant_dynamic-update-slice_fusion
  (12 shorter events, 0.2 us)
Async XLA Ops:
  6.5 457.5 %copy-start = (bf16[1024,1024]{1,0:T(8,128)(2,1)S(1)}, bf16[1024,1024]{1,0:T(8,128)(2,1)}, u32[]{:S(2)}) copy-start(bf16[1024,1024]{1,0:T(8,128)(2,1)} %param.9) | copy-start | bytes 6291460
  6.5 77.6 %all-gather.3.cloned.1.call-start = ((), (), s32[]{:S(2)}) async-start(), calls=%async_computation.4 | async-start | bytes 4718592 | tf_op jit(solution)/shard_map/all_gather | solution.py:161
  10.0 12.5 %all-to-all-start = ((s32[3,8,8]{2,0,1:T(4,128)}), s32[3,8,8]{2,0,1:T(4,128)S(1)}, u32[]{:S(2)}, u32[]{:S(2)}) async-start(s32[3,8,8]{2,0,1:T(4,128)} %copy.18), calls=%async_computation | async-start | bytes 32768 | tf_op jit(solution)/shard_map/all_to_all | solution.py:155
  23.3 60.8 %copy-start.4 = (s32[64]{0:T(128)}, s32[64]{0:T(128)S(1)}, u32[]{:S(2)}) copy-start(s32[64]{0:T(128)S(1)} %squeeze.3.which_ref) | copy-start | bytes 772
  288.5 4.7 copy-start.1
  288.5 4.9 copy-start.3
  288.5 96.3 %all-to-all-start.2 = ((bf16[8,2,8,128,128]{4,3,2,1,0:T(8,128)(2,1)}), bf16[8,2,8,128,128]{4,3,2,1,0:T(8,128)(2,1)}, u32[]{:S(2)}, u32[]{:S(2)}) async-start(bf16[8,2,8,128,128]{4,3,2,1,0:T(8,128)(2,1)} %bitcast.75), calls=%async_computation.2 | async-start | bytes 8388608 | tf_op jit(solution)/shard_map/all_to_all | solution.py:169
  293.2 170.9 %all-gather.5.cloned.1.call-start = ((), (), s32[]{:S(2)}) async-start(), calls=%async_computation.5 | async-start | bytes 4718592 | tf_op jit(solution)/shard_map/all_gather | solution.py:195
  391.5 122.7 %reduce-scatter.2.cloned.1.call-start = ((), (), s32[]{:S(2)}) async-start(), calls=%async_computation.6 | async-start | bytes 5242880 | tf_op jit(solution)/shard_map/reduce_scatter | solution.py:197
  516.4 41.2 %collective-permute-start = (bf16[256,1024]{1,0:T(8,128)(2,1)}, bf16[256,1024]{1,0:T(8,128)(2,1)S(1)}, u32[]{:S(2)}, u32[]{:S(2)}) collective-permute-start(bf16[256,1024]{1,0:T(8,128)(2,1)} %get-tuple-element.20), channel_id=1, source_target_pairs={{0,0},{1,8},{2,16},{3,24},{4,4},{5,12},{6,20},{7,28},{8,1},{9,9},{... | collective-permute-start | bytes 1572872 | tf_op jit(solution)/shard_map/ppermute | solution.py:212
  521.9 47.5 %collective-permute-start.1 = (bf16[256,1024]{1,0:T(8,128)(2,1)}, bf16[256,1024]{1,0:T(8,128)(2,1)S(1)}, u32[]{:S(2)}, u32[]{:S(2)}) collective-permute-start(bf16[256,1024]{1,0:T(8,128)(2,1)} %get-tuple-element.19), channel_id=1, source_target_pairs={{0,4},{1,12},{2,20},{3,28},{4,0},{5,8},{6,16},{7,24},{8,5},{9,13},... | collective-permute-start | bytes 1572872 | tf_op jit(solution)/shard_map/ppermute | solution.py:212
  557.8 11.6 %copy-start.2 = (bf16[256,2048]{1,0:T(8,128)(2,1)}, bf16[256,2048]{1,0:T(8,128)(2,1)S(1)}, u32[]{:S(2)}) copy-start(bf16[256,2048]{1,0:T(8,128)(2,1)S(1)} %constant_dynamic-update-slice_fusion.1) | copy-start | bytes 3145732
Sparse Core Ops, SparseCore 0:
  9.5 74.5 all-gather.2
  391.6 72.4 all-gather.4
  472.6 41.6 reduce-scatter.1

commit v8 on v7

--- a/solution.py
+++ b/solution.py
@@ -11,6 +11,7 @@
 QLEN = 128
 PLEN = 512
 FLOOR = -1e30
+LIVE = -1e20
 
 
 def slot_kernel(rows_ref, pick_ref, valid_ref, which_ref, q0_ref, kv0_ref, q1_ref, kv1_ref,
@@ -82,7 +83,7 @@
     return pl.pallas_call(
         slot_kernel,
         out_shape=(
-            jax.ShapeDtypeStruct((n_req, n_query, stacked, HD), jnp.bfloat16),
+            jax.ShapeDtypeStruct((n_req, n_query, stacked, HD), jnp.float32),
             jax.ShapeDtypeStruct((n_req, n_query, heads, QLEN), jnp.float32),
             jax.ShapeDtypeStruct((n_req, n_query, heads, QLEN), jnp.float32),
         ),
@@ -164,19 +165,32 @@
         asked_rows, pick, asked[2].reshape(n_cache * capacity), asked_query.reshape(n_cache * capacity),
         q_blocks, passage_store, n_cache, capacity, query_count,
     )
-    merged_acc = merged_acc.reshape(n_cache, query_count, heads, QLEN, HD)
-    stats = jnp.stack([merged_peak, merged_total], axis=2)
-    back_acc = lax.all_to_all(
-        merged_acc, "cache", split_axis=0, concat_axis=0, tiled=True
-    )
-    back_stats = lax.all_to_all(stats, "cache", split_axis=0, concat_axis=0, tiled=True)
+    peak_ref = lax.reduce_precision(merged_peak, exponent_bits=8, mantissa_bits=7)
+    shift = jnp.where(merged_peak > LIVE, jnp.exp(merged_peak - peak_ref), 0.0)
+    sent_acc = (merged_acc.reshape(n_cache, query_count, heads, QLEN, HD) * shift[..., None]).astype(
+        jnp.bfloat16
+    )
+    sent_total = merged_total * shift
+    total_hi = lax.reduce_precision(sent_total, exponent_bits=8, mantissa_bits=7)
+    total_lo = sent_total - total_hi
+    stats = jnp.stack([peak_ref, total_hi, total_lo], axis=2).astype(jnp.bfloat16)
+    packed = jnp.concatenate(
+        [sent_acc.reshape(n_cache, query_count, heads * QLEN, HD),
+         stats.reshape(n_cache, query_count, 3 * heads, QLEN)],
+        axis=2,
+    )
+    back = lax.all_to_all(packed, "cache", split_axis=0, concat_axis=0, tiled=True)
+    back_acc = back[:, :, :heads * QLEN].reshape(n_cache, query_count, heads, QLEN, HD)
+    back_stats = back[:, :, heads * QLEN:].astype(jnp.float32).reshape(
+        n_cache, query_count, 3, heads, QLEN
+    )
 
     own_acc, own_peak, own_total = own_part(
         queries.reshape(query_count, QLEN, width),
         own_kv.reshape(query_count, QLEN, own_kv.shape[1]),
     )
     far_peak = back_stats[:, :, 0][..., None]
-    far_total = back_stats[:, :, 1][..., None]
+    far_total = (back_stats[:, :, 1] + back_stats[:, :, 2])[..., None]
     top = jnp.maximum(jnp.max(far_peak, axis=0), own_peak)
     far_scale = jnp.exp(far_peak - top[None])
     own_scale = jnp.exp(own_peak - top)

time: 578 us -> 577 us (level)
  blocking collectives: 109 us -> 0 us
  starting transfers between devices: 17.5 us -> 114 us
  other arithmetic: 7.34 us -> 15.7 us
    all_to_all x1 -> x0, blocking collectives: 109 us -> none  [shards(): lax.all_to_all(stats, 'cache', split_axis=0, concat_axis=0, tiled=True)]
    all_to_all x1, starting transfers between devices: 4.68 us -> 101 us  [shards(): lax.all_to_all(packed, 'cache', split_axis=0, concat_axis=0, tiled=True)]
where the time goes in v8:
time: 577 us; the launch traced here: 576 us
  waiting for transfers between devices  321 us (56%)
  starting transfers between devices  114 us (20%)
  Pallas kernels  94.9 us (16%)
  other arithmetic  15.7 us (3%)
  between operations  13.4 us (2%)
  matrix products  9.57 us (2%)
  local copies, waits for them, and re-layouts  7.74 us (1%)
    all_to_all x1, starting transfers between devices, shards(): lax.all_to_all(packed, 'cache', split_axis=0, concat_axis=0, tiled=True)  101 us
    pallas_call x1, Pallas kernels, slot_attention(): pl.pallas_call(slot_kernel, out_shape=(jax.ShapeDtypeStruct((n_req, n_que...  94.9 us
    all_to_all x1, waiting for transfers between devices, shards(): lax.all_to_all(packed, 'cache', split_axis=0, concat_axis=0, tiled=True)  93.5 us
    all_gather x1, waiting for transfers between devices, project(): everyone = lax.all_gather(attended, 'cache', axis=0, tiled=True)  72.6 us
    all_gather x1, waiting for transfers between devices, shards(): everyone_q = lax.all_gather(queries, 'cache', axis=0, tiled=True)  59.8 us
    ppermute x2, waiting for transfers between devices, project(): got = lax.ppermute(piece, ('cache', 'stream'), perm)  45.9 us
    reduce_scatter x1, waiting for transfers between devices, project(): lax.psum_scatter(partial_sums.astype(jnp.bfloat16), 'stream', scatter_dim...  41.7 us
  transfers between devices with their start and end apart: 7, of which 7 were waited for; matrix products, arithmetic and copies ran while one was open for 1% of the time, Pallas kernels for 0%

profile of v8, /device:TPU:4, one launch (start us, length us, event | category | flops | bytes accessed | tf_op | source)
XLA Modules:
  0.0 575.6 jit_solution(11547925556562786426)
XLA Ops:
  6.5 0.0 copy-start
  6.5 0.0 all-gather.3.cloned.1.call-start
  6.5 0.7 all-gather.3.cloned.1.call-update
  7.3 0.8 eq.50
  8.0 0.8 select_reduce_fusion.2
  8.9 0.2 convert_reduce_fusion.1
  9.1 0.1 select_reduce_fusion.1
  9.2 0.1 stack.28
  9.2 0.1 stack.29
  9.3 0.1 stack.30
  9.4 0.6 copy.21
  10.0 5.8 %all-to-all-start = ((s32[3,8,8]{2,0,1:T(4,128)}), s32[3,8,8]{2,0,1:T(4,128)S(1)}, u32[]{:S(2)}, u32[]{:S(2)}) async-start(s32[3,8,8]{2,0,1:T(4,128)} %copy.21), calls=%async_computation | async-start | bytes 32768 | tf_op jit(solution)/shard_map/all_to_all | solution.py:156
  15.8 0.1 add.106
  15.9 0.1 add.107
  16.0 6.5 %all-to-all-done = s32[3,8,8]{2,0,1:T(4,128)S(1)} async-done(((s32[3,8,8]{2,0,1:T(4,128)}), s32[3,8,8]{2,0,1:T(4,128)S(1)}, u32[]{:S(2)}, u32[]{:S(2)}) %all-to-all-start) | async-done | bytes 800 | tf_op jit(solution)/shard_map/all_to_all | solution.py:156
  22.6 0.1 squeeze.2.which_ref
  22.6 0.0 copy-start.4
  22.6 0.6 reshape_squeeze.7.rows_ref
  23.3 0.6 reshape_squeeze.8.valid_ref
  23.8 0.5 add.108.pick_ref
  24.4 59.8 %all-gather.3.cloned.1.call-done = bf16[2048,1024]{1,0:T(8,128)(2,1)} async-done(((bf16[256,1024]{1,0:T(8,128)(2,1)}), bf16[2048,1024]{1,0:T(8,128)(2,1)}) %all-gather.3.cloned.1.call-update) | async-done | bytes 4194320 | tf_op jit(solution)/shard_map/all_gather | solution.py:162
  84.1 0.0 copy-done.4
  84.1 94.9 %shard_map.64 = (f32[8,2,1024,128]{3,2,1,0:T(8,128)}, f32[8,2,8,128]{3,2,1,0:T(8,128)}, f32[8,2,8,128]{3,2,1,0:T(8,128)}) custom-call(s32[64]{0:T(128)} %reshape_squeeze.7.rows_ref, s32[64]{0:T(128)} %add.108.pick_ref, s32[64]{0:T(128)} %reshape_squeeze.8.valid_ref, s32[64]{0:T(128)} %copy-done.4, bf16[16,128,1024]{2,1,0:T(8,128)(2,1)} %bitcast.108, ...), custom_call_target="tpu_custom_call" | custom-call | flops 17179869184 | bytes 37748736 | tf_op jit(solution)/shard_map/pallas_call | solution.py:83
  179.0 0.9 fusion.21
  180.0 5.2 multiply_convert_fusion
  185.2 2.3 pad_maximum_fusion
  187.5 0.0 copy-start.1
  187.5 0.0 copy-start.3
  187.5 100.7 %all-to-all-start.1 = ((bf16[8,2,1048,128]{3,2,1,0:T(8,128)(2,1)}), bf16[8,2,1048,128]{3,2,1,0:T(8,128)(2,1)}, u32[]{:S(2)}, u32[]{:S(2)}) async-start(bf16[8,2,1048,128]{3,2,1,0:T(8,128)(2,1)} %pad_maximum_fusion), calls=%async_computation.1 | async-start | bytes 8585216 | tf_op jit(solution)/shard_map/all_to_all | solution.py:182
  288.2 0.0 all-gather.5.cloned.1.call-start
  288.3 0.0 copy-done.1
  288.3 0.1 copy.31
  288.4 0.0 copy-done.3
  288.4 0.3 fusion.27
  288.8 0.2 fusion.6
  288.9 93.5 %all-to-all-done.1 = bf16[8,2,1048,128]{3,2,1,0:T(8,128)(2,1)} async-done(((bf16[8,2,1048,128]{3,2,1,0:T(8,128)(2,1)}), bf16[8,2,1048,128]{3,2,1,0:T(8,128)(2,1)}, u32[]{:S(2)}, u32[]{:S(2)}) %all-to-all-start.1) | async-done | bytes 4292640 | tf_op jit(solution)/shard_map/all_to_all | solution.py:182
  382.5 0.9 fusion.11
  383.6 4.5 multiply_reduce_fusion
  388.0 0.9 fusion.5
  389.0 0.3 copy.26
  389.3 0.9 copy.41
  390.2 0.0 all-gather.5.cloned.1.call-update
  390.2 0.0 reduce-scatter.2.cloned.1.call-start
  390.3 72.6 %all-gather.5.cloned.1.call-done = bf16[2048,1024]{1,0:T(8,128)(2,1)} async-done(((bf16[256,1024]{1,0:T(8,128)(2,1)}), bf16[2048,1024]{1,0:T(8,128)(2,1)}) %all-gather.5.cloned.1.call-update) | async-done | bytes 4194320 | tf_op jit(solution)/shard_map/all_gather | solution.py:209
  462.8 0.0 copy-done
  462.8 8.3 %convolution_convert_fusion = bf16[2048,1024]{1,0:T(8,128)(2,1)} fusion(bf16[2048,1024]{1,0:T(8,128)(2,1)} %all-gather.5.cloned.1.call-done, bf16[1024,1024]{1,0:T(8,128)(2,1)S(1)} %copy-done), kind=kOutput, calls=%fused_computation.3 | convolution fusion | flops 4297064448 | bytes 10485760 | tf_op jit(solution)/shard_map/dot_general | solution.py:210
  471.2 0.0 reduce-scatter.2.cloned.1.call-update
  471.3 41.7 %reduce-scatter.2.cloned.1.call-done = bf16[512,1024]{1,0:T(8,128)(2,1)} async-done(((bf16[2048,1024]{1,0:T(8,128)(2,1)}), bf16[512,1024]{1,0:T(8,128)(2,1)}) %reduce-scatter.2.cloned.1.call-update) | async-done | bytes 1048592 | tf_op jit(solution)/shard_map/reduce_scatter | solution.py:211
  513.0 2.2 constant_dynamic-slice_fusion
  515.2 5.5 collective-permute-start
  520.7 1.5 collective-permute-start.1
  522.2 34.2 %collective-permute-done = bf16[256,1024]{1,0:T(8,128)(2,1)S(1)} collective-permute-done((bf16[256,1024]{1,0:T(8,128)(2,1)}, bf16[256,1024]{1,0:T(8,128)(2,1)S(1)}, u32[]{:S(2)}, u32[]{:S(2)}) %collective-permute-start) | collective-permute-done | bytes 524320 | tf_op jit(solution)/shard_map/ppermute | solution.py:226
  556.4 0.1 broadcast_in_dim.63
  556.5 0.1 constant_dynamic-update-slice_fusion.1
  556.5 0.0 copy-start.2
  556.6 11.6 %collective-permute-done.1 = bf16[256,1024]{1,0:T(8,128)(2,1)S(1)} collective-permute-done((bf16[256,1024]{1,0:T(8,128)(2,1)}, bf16[256,1024]{1,0:T(8,128)(2,1)S(1)}, u32[]{:S(2)}, u32[]{:S(2)}) %collective-permute-start.1) | collective-permute-done | bytes 524320 | tf_op jit(solution)/shard_map/ppermute | solution.py:226
  568.2 0.0 copy-done.2
  568.2 0.8 constant_dynamic-update-slice_fusion
  (17 shorter events, 0.3 us)
Async XLA Ops:
  6.5 456.3 %copy-start = (bf16[1024,1024]{1,0:T(8,128)(2,1)S(1)}, bf16[1024,1024]{1,0:T(8,128)(2,1)}, u32[]{:S(2)}) copy-start(bf16[1024,1024]{1,0:T(8,128)(2,1)} %param.9) | copy-start | bytes 6291460
  6.5 77.6 %all-gather.3.cloned.1.call-start = ((), (), s32[]{:S(2)}) async-start(), calls=%async_computation.3 | async-start | bytes 4718592 | tf_op jit(solution)/shard_map/all_gather | solution.py:162
  10.0 12.5 %all-to-all-start = ((s32[3,8,8]{2,0,1:T(4,128)}), s32[3,8,8]{2,0,1:T(4,128)S(1)}, u32[]{:S(2)}, u32[]{:S(2)}) async-start(s32[3,8,8]{2,0,1:T(4,128)} %copy.21), calls=%async_computation | async-start | bytes 32768 | tf_op jit(solution)/shard_map/all_to_all | solution.py:156
  22.6 61.5 %copy-start.4 = (s32[64]{0:T(128)}, s32[64]{0:T(128)S(1)}, u32[]{:S(2)}) copy-start(s32[64]{0:T(128)S(1)} %squeeze.2.which_ref) | copy-start | bytes 772
  187.5 100.8 %copy-start.1 = (bf16[256,1024]{1,0:T(8,128)(2,1)S(1)}, bf16[256,1024]{1,0:T(8,128)(2,1)}, u32[]{:S(2)}) copy-start(bf16[256,1024]{1,0:T(8,128)(2,1)} %param.6) | copy-start | bytes 1572868
  187.5 100.9 %copy-start.3 = (bf16[256,256]{1,0:T(8,128)(2,1)S(1)}, bf16[256,256]{1,0:T(8,128)(2,1)}, u32[]{:S(2)}) copy-start(bf16[256,256]{1,0:T(8,128)(2,1)} %param.7) | copy-start | bytes 393220
  187.5 194.9 %all-to-all-start.1 = ((bf16[8,2,1048,128]{3,2,1,0:T(8,128)(2,1)}), bf16[8,2,1048,128]{3,2,1,0:T(8,128)(2,1)}, u32[]{:S(2)}, u32[]{:S(2)}) async-start(bf16[8,2,1048,128]{3,2,1,0:T(8,128)(2,1)} %pad_maximum_fusion), calls=%async_computation.1 | async-start | bytes 8585216 | tf_op jit(solution)/shard_map/all_to_all | solution.py:182
  288.2 174.6 %all-gather.5.cloned.1.call-start = ((), (), s32[]{:S(2)}) async-start(), calls=%async_computation.4 | async-start | bytes 4718592 | tf_op jit(solution)/shard_map/all_gather | solution.py:209
  390.2 122.7 %reduce-scatter.2.cloned.1.call-start = ((), (), s32[]{:S(2)}) async-start(), calls=%async_computation.5 | async-start | bytes 5242880 | tf_op jit(solution)/shard_map/reduce_scatter | solution.py:211
  515.2 41.2 %collective-permute-start = (bf16[256,1024]{1,0:T(8,128)(2,1)}, bf16[256,1024]{1,0:T(8,128)(2,1)S(1)}, u32[]{:S(2)}, u32[]{:S(2)}) collective-permute-start(bf16[256,1024]{1,0:T(8,128)(2,1)} %get-tuple-element.20), channel_id=1, source_target_pairs={{0,0},{1,8},{2,16},{3,24},{4,4},{5,12},{6,20},{7,28},{8,1},{9,9},{... | collective-permute-start | bytes 1572872 | tf_op jit(solution)/shard_map/ppermute | solution.py:226
  520.7 47.5 %collective-permute-start.1 = (bf16[256,1024]{1,0:T(8,128)(2,1)}, bf16[256,1024]{1,0:T(8,128)(2,1)S(1)}, u32[]{:S(2)}, u32[]{:S(2)}) collective-permute-start(bf16[256,1024]{1,0:T(8,128)(2,1)} %get-tuple-element.19), channel_id=1, source_target_pairs={{0,4},{1,12},{2,20},{3,28},{4,0},{5,8},{6,16},{7,24},{8,5},{9,13},... | collective-permute-start | bytes 1572872 | tf_op jit(solution)/shard_map/ppermute | solution.py:226
  556.5 11.6 %copy-start.2 = (bf16[256,2048]{1,0:T(8,128)(2,1)}, bf16[256,2048]{1,0:T(8,128)(2,1)S(1)}, u32[]{:S(2)}) copy-start(bf16[256,2048]{1,0:T(8,128)(2,1)S(1)} %constant_dynamic-update-slice_fusion.1) | copy-start | bytes 3145732
Sparse Core Ops, SparseCore 0:
  9.5 74.5 all-gather.2
  390.4 72.4 all-gather.4
  471.3 41.6 reduce-scatter.1

commit v9 on v8

--- a/solution.py
+++ b/solution.py
@@ -161,9 +161,19 @@
 
     everyone_q = lax.all_gather(queries, "cache", axis=0, tiled=True)
     q_blocks = everyone_q.reshape(n_cache * query_count, QLEN, width)
-    merged_acc, merged_peak, merged_total = slot_attention(
-        asked_rows, pick, asked[2].reshape(n_cache * capacity), asked_query.reshape(n_cache * capacity),
+    me = lax.axis_index("cache")
+    mine = lax.dynamic_index_in_dim(asked, me, axis=1, keepdims=False)
+    near = slot_attention(
+        mine[0], mine[1], mine[2], mine[1], queries.reshape(query_count, QLEN, width),
+        passage_store, 1, capacity, query_count,
+    )
+    others = jnp.where(requester == me, 0, asked[2]).reshape(n_cache * capacity)
+    far = slot_attention(
+        asked_rows, pick, others, asked_query.reshape(n_cache * capacity),
         q_blocks, passage_store, n_cache, capacity, query_count,
+    )
+    merged_acc, merged_peak, merged_total = (
+        lax.dynamic_update_slice_in_dim(b, a, me, axis=0) for a, b in zip(near, far)
     )
     peak_ref = lax.reduce_precision(merged_peak, exponent_bits=8, mantissa_bits=7)
     shift = jnp.where(merged_peak > LIVE, jnp.exp(merged_peak - peak_ref), 0.0)

time: 577 us -> 560 us (0.971)
  Pallas kernels: 94.9 us -> 199 us
  starting transfers between devices: 114 us -> 17.7 us
  waiting for transfers between devices: 321 us -> 293 us
    pallas_call x1 -> x2, Pallas kernels: 94.9 us -> 199 us  [slot_attention(): pl.pallas_call(slot_kernel, out_shape=(jax.ShapeDtypeStruct((n_req, n_que...]
    all_to_all x1, starting transfers between devices: 101 us -> 4.68 us  [shards(): lax.all_to_all(packed, 'cache', split_axis=0, concat_axis=0, tiled=True)]
    all_gather x1, waiting for transfers between devices: 59.8 us -> 32.6 us  [shards(): everyone_q = lax.all_gather(queries, 'cache', axis=0, tiled=True)]
  transfers between devices with their start and end apart: 7 -> 7, of which waited for: 7 -> 7; matrix products, arithmetic and copies ran while one was open for 1% -> 1% of each run, Pallas kernels for 0% -> 5%
where the time goes in v9:
time: 560 us
  waiting for transfers between devices  293 us (52%)
  Pallas kernels  199 us (36%)
  starting transfers between devices  17.7 us (3%)
  other arithmetic  16.2 us (3%)
  between operations  13.4 us (2%)
  local copies, waits for them, and re-layouts  10.3 us (2%)
  matrix products  9.57 us (2%)
    pallas_call x2, Pallas kernels, slot_attention(): pl.pallas_call(slot_kernel, out_shape=(jax.ShapeDtypeStruct((n_req, n_que...  199 us
    all_to_all x1, waiting for transfers between devices, shards(): lax.all_to_all(packed, 'cache', split_axis=0, concat_axis=0, tiled=True)  93.5 us
    all_gather x1, waiting for transfers between devices, project(): everyone = lax.all_gather(attended, 'cache', axis=0, tiled=True)  72.5 us
    ppermute x2, waiting for transfers between devices, project(): got = lax.ppermute(piece, ('cache', 'stream'), perm)  45.9 us
    reduce_scatter x1, waiting for transfers between devices, project(): lax.psum_scatter(partial_sums.astype(jnp.bfloat16), 'stream', scatter_dim...  41.7 us
    all_gather x1, waiting for transfers between devices, shards(): everyone_q = lax.all_gather(queries, 'cache', axis=0, tiled=True)  32.6 us
  transfers between devices with their start and end apart: 7, of which 7 were waited for; matrix products, arithmetic and copies ran while one was open for 1% of the time, Pallas kernels for 5%

profile of v9, /device:TPU:4, one launch (start us, length us, event | category | flops | bytes accessed | tf_op | source)
XLA Modules:
  0.0 559.7 jit_solution(13242618354002384804)
XLA Ops:
  6.5 0.0 copy-start
  6.5 0.0 all-gather.3.cloned.1.call-start
  6.5 0.7 all-gather.3.cloned.1.call-update
  7.3 0.8 eq.61
  8.0 0.8 select_reduce_fusion.2
  8.9 0.2 convert_reduce_fusion.1
  9.1 0.1 select_reduce_fusion.1
  9.2 0.1 stack.28
  9.2 0.1 stack.29
  9.3 0.1 stack.30
  9.4 0.6 copy.21
  10.0 5.8 %all-to-all-start = ((s32[3,8,8]{2,0,1:T(4,128)}), s32[3,8,8]{2,0,1:T(4,128)S(1)}, u32[]{:S(2)}, u32[]{:S(2)}) async-start(s32[3,8,8]{2,0,1:T(4,128)} %copy.21), calls=%async_computation | async-start | bytes 32768 | tf_op jit(solution)/shard_map/all_to_all | solution.py:156
  15.9 0.1 broadcast_in_dim.83
  15.9 0.1 broadcast_in_dim.84
  16.0 0.1 add.113
  16.1 0.1 add.114
  16.2 6.3 %all-to-all-done = s32[3,8,8]{2,0,1:T(4,128)S(1)} async-done(((s32[3,8,8]{2,0,1:T(4,128)}), s32[3,8,8]{2,0,1:T(4,128)S(1)}, u32[]{:S(2)}, u32[]{:S(2)}) %all-to-all-start) | async-done | bytes 800 | tf_op jit(solution)/shard_map/all_to_all | solution.py:156
  22.6 0.1 squeeze.21
  22.6 0.1 squeeze.20.which_ref
  22.7 0.6 reshape_squeeze.4.rows_ref
  23.3 0.5 add.115.pick_ref
  23.8 0.6 slice_bitcast_fusion.6
  24.4 26.6 %shard_map.65 = (f32[1,2,1024,128]{3,2,1,0:T(8,128)}, f32[1,2,8,128]{3,2,1,0:T(8,128)}, f32[1,2,8,128]{3,2,1,0:T(8,128)}) custom-call(s32[8]{0:T(128)} %get-tuple-element.33.rows_ref, s32[8]{0:T(128)} %get-tuple-element.32.pick_ref.which_ref, s32[8]{0:T(128)} %get-tuple-element.31.valid_ref, s32[8]{0:T(128)} %get-tuple-element.32.pick_ref.which_ref, ...), custom_call_target="tpu_custom_call" | custom-call | flops 2147483648 | bytes 4718592 | tf_op jit(solution)/shard_map/pallas_call | solution.py:83
  51.0 0.0 copy-done.7
  51.0 0.5 broadcast_select_fusion.valid_ref
  51.6 32.6 %all-gather.3.cloned.1.call-done = bf16[2048,1024]{1,0:T(8,128)(2,1)} async-done(((bf16[256,1024]{1,0:T(8,128)(2,1)}), bf16[2048,1024]{1,0:T(8,128)(2,1)}) %all-gather.3.cloned.1.call-update) | async-done | bytes 4194320 | tf_op jit(solution)/shard_map/all_gather | solution.py:162
  84.1 172.7 %shard_map.64 = (f32[8,2,1024,128]{3,2,1,0:T(8,128)}, f32[8,2,8,128]{3,2,1,0:T(8,128)}, f32[8,2,8,128]{3,2,1,0:T(8,128)}) custom-call(s32[64]{0:T(128)} %reshape_squeeze.4.rows_ref, s32[64]{0:T(128)} %add.115.pick_ref, s32[64]{0:T(128)} %broadcast_select_fusion.valid_ref, s32[64]{0:T(128)} %copy-done.7, bf16[16,128,1024]{2,1,0:T(8,128)(2,1)} %bitcast.117, ...), custom_call_target="tpu_custom_call" | custom-call | flops 17179869184 | bytes 37748736 | tf_op jit(solution)/shard_map/pallas_call | solution.py:83
  256.8 0.0 copy-done.6
  256.8 0.6 constant_dynamic-update-slice_fusion.2
  257.4 0.0 copy-done.5
  257.4 0.6 constant_dynamic-update-slice_fusion.3
  258.0 0.9 fusion.21
  259.0 0.0 copy-done.2
  259.0 1.1 constant_dynamic-update-slice_fusion.4
  260.0 5.2 multiply_convert_fusion
  265.3 2.3 pad_maximum_fusion
  267.6 4.7 all-to-all-start.1
  272.2 0.2 all-gather.5.cloned.1.call-start
  272.5 0.0 copy-done.1
  272.5 0.1 copy.31
  272.6 0.3 fusion.27
  272.9 0.2 fusion.6
  273.1 93.5 %all-to-all-done.1 = bf16[8,2,1048,128]{3,2,1,0:T(8,128)(2,1)} async-done(((bf16[8,2,1048,128]{3,2,1,0:T(8,128)(2,1)}), bf16[8,2,1048,128]{3,2,1,0:T(8,128)(2,1)}, u32[]{:S(2)}, u32[]{:S(2)}) %all-to-all-start.1) | async-done | bytes 4292640 | tf_op jit(solution)/shard_map/all_to_all | solution.py:192
  366.6 0.9 fusion.11
  367.7 4.5 multiply_reduce_fusion
  372.2 0.9 fusion.5
  373.1 0.3 copy.26
  373.5 0.9 copy.41
  374.4 0.0 all-gather.5.cloned.1.call-update
  374.4 0.0 reduce-scatter.2.cloned.1.call-start
  374.5 72.5 %all-gather.5.cloned.1.call-done = bf16[2048,1024]{1,0:T(8,128)(2,1)} async-done(((bf16[256,1024]{1,0:T(8,128)(2,1)}), bf16[2048,1024]{1,0:T(8,128)(2,1)}) %all-gather.5.cloned.1.call-update) | async-done | bytes 4194320 | tf_op jit(solution)/shard_map/all_gather | solution.py:219
  447.0 8.3 %convolution_convert_fusion = bf16[2048,1024]{1,0:T(8,128)(2,1)} fusion(bf16[2048,1024]{1,0:T(8,128)(2,1)} %all-gather.5.cloned.1.call-done, bf16[1024,1024]{1,0:T(8,128)(2,1)S(1)} %copy-done), kind=kOutput, calls=%fused_computation.3 | convolution fusion | flops 4297064448 | bytes 10485760 | tf_op jit(solution)/shard_map/dot_general | solution.py:220
  455.3 0.0 reduce-scatter.2.cloned.1.call-update
  455.4 41.7 %reduce-scatter.2.cloned.1.call-done = bf16[512,1024]{1,0:T(8,128)(2,1)} async-done(((bf16[2048,1024]{1,0:T(8,128)(2,1)}), bf16[512,1024]{1,0:T(8,128)(2,1)}) %reduce-scatter.2.cloned.1.call-update) | async-done | bytes 1048592 | tf_op jit(solution)/shard_map/reduce_scatter | solution.py:221
  497.1 2.2 constant_dynamic-slice_fusion
  499.4 5.5 collective-permute-start
  504.8 1.5 collective-permute-start.1
  506.3 34.2 %collective-permute-done = bf16[256,1024]{1,0:T(8,128)(2,1)S(1)} collective-permute-done((bf16[256,1024]{1,0:T(8,128)(2,1)}, bf16[256,1024]{1,0:T(8,128)(2,1)S(1)}, u32[]{:S(2)}, u32[]{:S(2)}) %collective-permute-start) | collective-permute-done | bytes 524320 | tf_op jit(solution)/shard_map/ppermute | solution.py:236
  540.5 0.1 broadcast_in_dim.77
  540.6 0.1 constant_dynamic-update-slice_fusion.1
  540.7 0.0 copy-start.3
  540.7 11.6 %collective-permute-done.1 = bf16[256,1024]{1,0:T(8,128)(2,1)S(1)} collective-permute-done((bf16[256,1024]{1,0:T(8,128)(2,1)}, bf16[256,1024]{1,0:T(8,128)(2,1)S(1)}, u32[]{:S(2)}, u32[]{:S(2)}) %collective-permute-start.1) | collective-permute-done | bytes 524320 | tf_op jit(solution)/shard_map/ppermute | solution.py:236
  552.3 0.0 copy-done.3
  552.3 0.8 constant_dynamic-update-slice_fusion
  (27 shorter events, 0.3 us)
Async XLA Ops:
  6.5 440.4 %copy-start = (bf16[1024,1024]{1,0:T(8,128)(2,1)S(1)}, bf16[1024,1024]{1,0:T(8,128)(2,1)}, u32[]{:S(2)}) copy-start(bf16[1024,1024]{1,0:T(8,128)(2,1)} %param.9) | copy-start | bytes 6291460
  6.5 77.6 %all-gather.3.cloned.1.call-start = ((), (), s32[]{:S(2)}) async-start(), calls=%async_computation.3 | async-start | bytes 4718592 | tf_op jit(solution)/shard_map/all_gather | solution.py:162
  10.0 12.5 %all-to-all-start = ((s32[3,8,8]{2,0,1:T(4,128)}), s32[3,8,8]{2,0,1:T(4,128)S(1)}, u32[]{:S(2)}, u32[]{:S(2)}) async-start(s32[3,8,8]{2,0,1:T(4,128)} %copy.21), calls=%async_computation | async-start | bytes 32768 | tf_op jit(solution)/shard_map/all_to_all | solution.py:156
  22.7 28.3 %copy-start.7 = (s32[64]{0:T(128)}, s32[64]{0:T(128)S(1)}, u32[]{:S(2)}) copy-start(s32[64]{0:T(128)S(1)} %squeeze.20.which_ref) | copy-start | bytes 772
  84.1 172.7 %copy-start.6 = (f32[1,2,8,128]{3,2,1,0:T(8,128)S(1)}, f32[1,2,8,128]{3,2,1,0:T(8,128)}, u32[]{:S(2)}) copy-start(f32[1,2,8,128]{3,2,1,0:T(8,128)} %get-tuple-element.16) | copy-start | bytes 24580
  84.1 173.3 %copy-start.5 = (f32[1,2,8,128]{3,2,1,0:T(8,128)S(1)}, f32[1,2,8,128]{3,2,1,0:T(8,128)}, u32[]{:S(2)}) copy-start(f32[1,2,8,128]{3,2,1,0:T(8,128)} %get-tuple-element.14) | copy-start | bytes 24580
  84.1 174.8 %copy-start.2 = (f32[1,2,1024,128]{3,2,1,0:T(8,128)S(1)}, f32[1,2,1024,128]{3,2,1,0:T(8,128)}, u32[]{:S(2)}) copy-start(f32[1,2,1024,128]{3,2,1,0:T(8,128)} %get-tuple-element.12) | copy-start | bytes 3145732
  267.6 4.9 copy-start.1
  267.6 5.1 copy-start.4
  267.6 99.1 %all-to-all-start.1 = ((bf16[8,2,1048,128]{3,2,1,0:T(8,128)(2,1)}), bf16[8,2,1048,128]{3,2,1,0:T(8,128)(2,1)}, u32[]{:S(2)}, u32[]{:S(2)}) async-start(bf16[8,2,1048,128]{3,2,1,0:T(8,128)(2,1)} %pad_maximum_fusion), calls=%async_computation.1 | async-start | bytes 8585216 | tf_op jit(solution)/shard_map/all_to_all | solution.py:192
  272.2 174.7 %all-gather.5.cloned.1.call-start = ((), (), s32[]{:S(2)}) async-start(), calls=%async_computation.4 | async-start | bytes 4718592 | tf_op jit(solution)/shard_map/all_gather | solution.py:219
  374.4 122.7 %reduce-scatter.2.cloned.1.call-start = ((), (), s32[]{:S(2)}) async-start(), calls=%async_computation.5 | async-start | bytes 5242880 | tf_op jit(solution)/shard_map/reduce_scatter | solution.py:221
  499.4 41.2 %collective-permute-start = (bf16[256,1024]{1,0:T(8,128)(2,1)}, bf16[256,1024]{1,0:T(8,128)(2,1)S(1)}, u32[]{:S(2)}, u32[]{:S(2)}) collective-permute-start(bf16[256,1024]{1,0:T(8,128)(2,1)} %get-tuple-element.26), channel_id=1, source_target_pairs={{0,0},{1,8},{2,16},{3,24},{4,4},{5,12},{6,20},{7,28},{8,1},{9,9},{... | collective-permute-start | bytes 1572872 | tf_op jit(solution)/shard_map/ppermute | solution.py:236
  504.8 47.5 %collective-permute-start.1 = (bf16[256,1024]{1,0:T(8,128)(2,1)}, bf16[256,1024]{1,0:T(8,128)(2,1)S(1)}, u32[]{:S(2)}, u32[]{:S(2)}) collective-permute-start(bf16[256,1024]{1,0:T(8,128)(2,1)} %get-tuple-element.25), channel_id=1, source_target_pairs={{0,4},{1,12},{2,20},{3,28},{4,0},{5,8},{6,16},{7,24},{8,5},{9,13},... | collective-permute-start | bytes 1572872 | tf_op jit(solution)/shard_map/ppermute | solution.py:236
  540.7 11.6 %copy-start.3 = (bf16[256,2048]{1,0:T(8,128)(2,1)}, bf16[256,2048]{1,0:T(8,128)(2,1)S(1)}, u32[]{:S(2)}) copy-start(bf16[256,2048]{1,0:T(8,128)(2,1)S(1)} %constant_dynamic-update-slice_fusion.1) | copy-start | bytes 3145732
Sparse Core Ops, SparseCore 0:
  9.5 74.5 all-gather.2
  374.5 72.4 all-gather.4
  455.5 41.6 reduce-scatter.1

commit v10 on v9

--- a/solution.py
+++ b/solution.py
@@ -167,13 +167,27 @@
         mine[0], mine[1], mine[2], mine[1], queries.reshape(query_count, QLEN, width),
         passage_store, 1, capacity, query_count,
     )
-    others = jnp.where(requester == me, 0, asked[2]).reshape(n_cache * capacity)
+    mate = me + 1 - 2 * (me % 2)
+    mate_q = lax.ppermute(
+        queries.reshape(query_count, QLEN, width), "cache",
+        [(c, c + 1 - 2 * (c % 2)) for c in range(n_cache)],
+    )
+    theirs = lax.dynamic_index_in_dim(asked, mate, axis=1, keepdims=False)
+    beside = slot_attention(
+        theirs[0], theirs[1], theirs[2], theirs[1], mate_q,
+        passage_store, 1, capacity, query_count,
+    )
+    skip = (requester == me) | (requester == mate)
+    others = jnp.where(skip, 0, asked[2]).reshape(n_cache * capacity)
     far = slot_attention(
         asked_rows, pick, others, asked_query.reshape(n_cache * capacity),
         q_blocks, passage_store, n_cache, capacity, query_count,
     )
     merged_acc, merged_peak, merged_total = (
-        lax.dynamic_update_slice_in_dim(b, a, me, axis=0) for a, b in zip(near, far)
+        lax.dynamic_update_slice_in_dim(
+            lax.dynamic_update_slice_in_dim(b, a, me, axis=0), m, mate, axis=0
+        )
+        for a, m, b in zip(near, beside, far)
     )
     peak_ref = lax.reduce_precision(merged_peak, exponent_bits=8, mantissa_bits=7)
     shift = jnp.where(merged_peak > LIVE, jnp.exp(merged_peak - peak_ref), 0.0)

time: 560 us -> 545 us (0.973)
  Pallas kernels: 199 us -> 119 us
  starting transfers between devices: 17.7 us -> 74.9 us
    pallas_call x2 -> x3, Pallas kernels: 199 us -> 119 us  [slot_attention(): pl.pallas_call(slot_kernel, out_shape=(jax.ShapeDtypeStruct((n_req, n_que...]
    all_to_all x1, starting transfers between devices: 4.68 us -> 60.1 us  [shards(): lax.all_to_all(packed, 'cache', split_axis=0, concat_axis=0, tiled=True)]
  transfers between devices with their start and end apart: 7 -> 8, of which waited for: 7 -> 7; matrix products, arithmetic and copies ran while one was open for 1% -> 1% of each run, Pallas kernels for 5% -> 5%
where the time goes in v10:
time: 545 us; the launch traced here: 543 us
  waiting for transfers between devices  295 us (54%)
  Pallas kernels  119 us (22%)
  starting transfers between devices  74.9 us (14%)
  other arithmetic  16.3 us (3%)
  local copies, waits for them, and re-layouts  15.1 us (3%)
  between operations  13.4 us (2%)
  matrix products  9.57 us (2%)
    pallas_call x3, Pallas kernels, slot_attention(): pl.pallas_call(slot_kernel, out_shape=(jax.ShapeDtypeStruct((n_req, n_que...  119 us
    all_to_all x1, waiting for transfers between devices, shards(): lax.all_to_all(packed, 'cache', split_axis=0, concat_axis=0, tiled=True)  93.5 us
    all_gather x1, waiting for transfers between devices, project(): everyone = lax.all_gather(attended, 'cache', axis=0, tiled=True)  72.6 us
    all_to_all x1, starting transfers between devices, shards(): lax.all_to_all(packed, 'cache', split_axis=0, concat_axis=0, tiled=True)  60.1 us
    ppermute x2, waiting for transfers between devices, project(): got = lax.ppermute(piece, ('cache', 'stream'), perm)  45.8 us
    reduce_scatter x1, waiting for transfers between devices, project(): lax.psum_scatter(partial_sums.astype(jnp.bfloat16), 'stream', scatter_dim...  41.7 us
    all_gather x1, waiting for transfers between devices, shards(): everyone_q = lax.all_gather(queries, 'cache', axis=0, tiled=True)  35.8 us
  transfers between devices with their start and end apart: 8, of which 7 were waited for; matrix products, arithmetic and copies ran while one was open for 1% of the time, Pallas kernels for 5%

profile of v10, /device:TPU:4, one launch (start us, length us, event | category | flops | bytes accessed | tf_op | source)
XLA Modules:
  0.0 542.7 jit_solution(1094520807615612400)
XLA Ops:
  6.5 0.7 all-gather.3.cloned.1.call-update
  7.3 0.8 eq.73
  8.0 0.8 select_reduce_fusion.2
  8.9 0.2 convert_reduce_fusion.1
  9.1 0.1 select_reduce_fusion.1
  9.2 0.1 stack.28
  9.2 0.1 stack.29
  9.3 0.1 stack.30
  9.4 0.6 copy.21
  10.0 5.8 %all-to-all-start = ((s32[3,8,8]{2,0,1:T(4,128)}), s32[3,8,8]{2,0,1:T(4,128)S(1)}, u32[]{:S(2)}, u32[]{:S(2)}) async-start(s32[3,8,8]{2,0,1:T(4,128)} %copy.21), calls=%async_computation | async-start | bytes 32768 | tf_op jit(solution)/shard_map/all_to_all | solution.py:156
  15.8 2.0 collective-permute-start
  17.9 0.1 broadcast_in_dim.83
  17.9 0.1 broadcast_in_dim.84
  18.0 0.1 add.123
  18.1 0.1 add.124
  18.2 4.3 all-to-all-done
  22.5 0.6 slice_bitcast_fusion.9
  23.1 12.5 %shard_map.65 = (f32[1,2,1024,128]{3,2,1,0:T(8,128)}, f32[1,2,8,128]{3,2,1,0:T(8,128)}, f32[1,2,8,128]{3,2,1,0:T(8,128)}) custom-call(s32[8]{0:T(128)} %get-tuple-element.44.rows_ref, s32[8]{0:T(128)} %get-tuple-element.43.pick_ref.which_ref, s32[8]{0:T(128)} %get-tuple-element.42.valid_ref, s32[8]{0:T(128)} %get-tuple-element.43.pick_ref.which_ref, ...), custom_call_target="tpu_custom_call" | custom-call | flops 2147483648 | bytes 4718592 | tf_op jit(solution)/shard_map/pallas_call | solution.py:83
  35.6 0.1 squeeze.32
  35.7 0.1 squeeze.31.which_ref
  35.8 0.6 reshape_squeeze.4.rows_ref
  36.4 0.6 add.125.pick_ref
  37.0 0.5 broadcast_select_fusion.valid_ref
  37.5 0.5 slice_bitcast_fusion.6
  38.0 0.0 collective-permute-done.q0_ref.q1_ref
  38.0 0.8 copy-done.2
  38.8 12.6 %shard_map.66 = (f32[1,2,1024,128]{3,2,1,0:T(8,128)}, f32[1,2,8,128]{3,2,1,0:T(8,128)}, f32[1,2,8,128]{3,2,1,0:T(8,128)}) custom-call(s32[8]{0:T(128)} %get-tuple-element.41.rows_ref, s32[8]{0:T(128)} %get-tuple-element.40.pick_ref.which_ref, s32[8]{0:T(128)} %get-tuple-element.39.valid_ref, s32[8]{0:T(128)} %get-tuple-element.40.pick_ref.which_ref, ...), custom_call_target="tpu_custom_call" | custom-call | flops 2147483648 | bytes 4718592 | tf_op jit(solution)/shard_map/pallas_call | solution.py:83
  51.4 35.8 %all-gather.3.cloned.1.call-done = bf16[2048,1024]{1,0:T(8,128)(2,1)} async-done(((bf16[256,1024]{1,0:T(8,128)(2,1)}), bf16[2048,1024]{1,0:T(8,128)(2,1)}) %all-gather.3.cloned.1.call-update) | async-done | bytes 4194320 | tf_op jit(solution)/shard_map/all_gather | solution.py:162
  87.3 93.7 %shard_map.64 = (f32[8,2,1024,128]{3,2,1,0:T(8,128)}, f32[8,2,8,128]{3,2,1,0:T(8,128)}, f32[8,2,8,128]{3,2,1,0:T(8,128)}) custom-call(s32[64]{0:T(128)} %reshape_squeeze.4.rows_ref, s32[64]{0:T(128)} %add.125.pick_ref, s32[64]{0:T(128)} %broadcast_select_fusion.valid_ref, s32[64]{0:T(128)} %copy-done.10, bf16[16,128,1024]{2,1,0:T(8,128)(2,1)} %bitcast.124, ...), custom_call_target="tpu_custom_call" | custom-call | flops 17179869184 | bytes 37748736 | tf_op jit(solution)/shard_map/pallas_call | solution.py:83
  181.0 0.6 constant_dynamic-update-slice_fusion.5
  181.6 0.6 constant_dynamic-update-slice_fusion.4
  182.2 0.6 constant_dynamic-update-slice_fusion.3
  182.8 0.6 constant_dynamic-update-slice_fusion.2
  183.4 0.9 fusion.21
  184.3 1.1 constant_dynamic-update-slice_fusion.7
  185.4 2.3 constant_dynamic-update-slice_fusion.6
  187.7 5.2 multiply_convert_fusion
  193.0 2.3 pad_maximum_fusion
  195.3 60.1 %all-to-all-start.1 = ((bf16[8,2,1048,128]{3,2,1,0:T(8,128)(2,1)}), bf16[8,2,1048,128]{3,2,1,0:T(8,128)(2,1)}, u32[]{:S(2)}, u32[]{:S(2)}) async-start(bf16[8,2,1048,128]{3,2,1,0:T(8,128)(2,1)} %pad_maximum_fusion), calls=%async_computation.1 | async-start | bytes 8585216 | tf_op jit(solution)/shard_map/all_to_all | solution.py:206
  255.4 0.0 all-gather.5.cloned.1.call-start
  255.4 0.1 copy.31
  255.5 0.3 fusion.27
  255.9 0.2 fusion.6
  256.0 93.5 %all-to-all-done.1 = bf16[8,2,1048,128]{3,2,1,0:T(8,128)(2,1)} async-done(((bf16[8,2,1048,128]{3,2,1,0:T(8,128)(2,1)}), bf16[8,2,1048,128]{3,2,1,0:T(8,128)(2,1)}, u32[]{:S(2)}, u32[]{:S(2)}) %all-to-all-start.1) | async-done | bytes 4292640 | tf_op jit(solution)/shard_map/all_to_all | solution.py:206
  349.6 0.9 fusion.11
  350.7 4.5 multiply_reduce_fusion
  355.2 0.9 fusion.5
  356.1 0.3 copy.26
  356.4 0.9 copy.41
  357.3 0.0 all-gather.5.cloned.1.call-update
  357.4 0.0 reduce-scatter.2.cloned.1.call-start
  357.4 72.6 %all-gather.5.cloned.1.call-done = bf16[2048,1024]{1,0:T(8,128)(2,1)} async-done(((bf16[256,1024]{1,0:T(8,128)(2,1)}), bf16[2048,1024]{1,0:T(8,128)(2,1)}) %all-gather.5.cloned.1.call-update) | async-done | bytes 4194320 | tf_op jit(solution)/shard_map/all_gather | solution.py:233
  430.0 8.3 %convolution_convert_fusion = bf16[2048,1024]{1,0:T(8,128)(2,1)} fusion(bf16[2048,1024]{1,0:T(8,128)(2,1)} %all-gather.5.cloned.1.call-done, bf16[1024,1024]{1,0:T(8,128)(2,1)S(1)} %copy-done), kind=kOutput, calls=%fused_computation.3 | convolution fusion | flops 4297064448 | bytes 10485760 | tf_op jit(solution)/shard_map/dot_general | solution.py:234
  438.3 0.0 reduce-scatter.2.cloned.1.call-update
  438.4 41.7 %reduce-scatter.2.cloned.1.call-done = bf16[512,1024]{1,0:T(8,128)(2,1)} async-done(((bf16[2048,1024]{1,0:T(8,128)(2,1)}), bf16[512,1024]{1,0:T(8,128)(2,1)}) %reduce-scatter.2.cloned.1.call-update) | async-done | bytes 1048592 | tf_op jit(solution)/shard_map/reduce_scatter | solution.py:235
  480.1 2.2 constant_dynamic-slice_fusion
  482.3 5.5 %collective-permute-start.1 = (bf16[256,1024]{1,0:T(8,128)(2,1)}, bf16[256,1024]{1,0:T(8,128)(2,1)S(1)}, u32[]{:S(2)}, u32[]{:S(2)}) collective-permute-start(bf16[256,1024]{1,0:T(8,128)(2,1)} %get-tuple-element.32), channel_id=1, source_target_pairs={{0,0},{1,8},{2,16},{3,24},{4,4},{5,12},{6,20},{7,28},{8,1},{9,9},{... | collective-permute-start | bytes 1572872 | tf_op jit(solution)/shard_map/ppermute | solution.py:250
  487.8 1.5 collective-permute-start.2
  489.3 34.2 %collective-permute-done.1 = bf16[256,1024]{1,0:T(8,128)(2,1)S(1)} collective-permute-done((bf16[256,1024]{1,0:T(8,128)(2,1)}, bf16[256,1024]{1,0:T(8,128)(2,1)S(1)}, u32[]{:S(2)}, u32[]{:S(2)}) %collective-permute-start.1) | collective-permute-done | bytes 524320 | tf_op jit(solution)/shard_map/ppermute | solution.py:250
  523.5 0.1 broadcast_in_dim.77
  523.6 0.1 constant_dynamic-update-slice_fusion.1
  523.7 0.0 copy-start.4
  523.7 11.6 %collective-permute-done.2 = bf16[256,1024]{1,0:T(8,128)(2,1)S(1)} collective-permute-done((bf16[256,1024]{1,0:T(8,128)(2,1)}, bf16[256,1024]{1,0:T(8,128)(2,1)S(1)}, u32[]{:S(2)}, u32[]{:S(2)}) %collective-permute-start.2) | collective-permute-done | bytes 524320 | tf_op jit(solution)/shard_map/ppermute | solution.py:250
  535.3 0.8 constant_dynamic-update-slice_fusion
  (40 shorter events, 0.3 us)
Async XLA Ops:
  6.5 423.4 %copy-start = (bf16[1024,1024]{1,0:T(8,128)(2,1)S(1)}, bf16[1024,1024]{1,0:T(8,128)(2,1)}, u32[]{:S(2)}) copy-start(bf16[1024,1024]{1,0:T(8,128)(2,1)} %param.9) | copy-start | bytes 6291460
  6.5 80.7 %all-gather.3.cloned.1.call-start = ((), (), s32[]{:S(2)}) async-start(), calls=%async_computation.3 | async-start | bytes 4718592 | tf_op jit(solution)/shard_map/all_gather | solution.py:162
  10.0 12.5 %all-to-all-start = ((s32[3,8,8]{2,0,1:T(4,128)}), s32[3,8,8]{2,0,1:T(4,128)S(1)}, u32[]{:S(2)}, u32[]{:S(2)}) async-start(s32[3,8,8]{2,0,1:T(4,128)} %copy.21), calls=%async_computation | async-start | bytes 32768 | tf_op jit(solution)/shard_map/all_to_all | solution.py:156
  15.8 22.2 %collective-permute-start = (bf16[2,128,1024]{2,1,0:T(8,128)(2,1)}, bf16[2,128,1024]{2,1,0:T(8,128)(2,1)S(1)}, u32[]{:S(2)}, u32[]{:S(2)}) collective-permute-start(bf16[2,128,1024]{2,1,0:T(8,128)(2,1)} %bitcast.109), channel_id=1, source_target_pairs={{0,4},{4,0},{8,12},{12,8},{16,20},{20,16},{24,28},{28,24},{1,5},{5... | collective-permute-start | bytes 1572872 | tf_op jit(solution)/shard_map/ppermute | solution.py:171
  35.8 15.6 %copy-start.10 = (s32[64]{0:T(128)}, s32[64]{0:T(128)S(1)}, u32[]{:S(2)}) copy-start(s32[64]{0:T(128)S(1)} %squeeze.31.which_ref) | copy-start | bytes 772
  38.0 0.8 copy-start.2
  87.3 93.7 %copy-start.7 = (f32[1,2,8,128]{3,2,1,0:T(8,128)S(1)}, f32[1,2,8,128]{3,2,1,0:T(8,128)}, u32[]{:S(2)}) copy-start(f32[1,2,8,128]{3,2,1,0:T(8,128)} %get-tuple-element.18) | copy-start | bytes 24580
  87.3 94.3 %copy-start.9 = (f32[1,2,8,128]{3,2,1,0:T(8,128)S(1)}, f32[1,2,8,128]{3,2,1,0:T(8,128)}, u32[]{:S(2)}) copy-start(f32[1,2,8,128]{3,2,1,0:T(8,128)} %get-tuple-element.19) | copy-start | bytes 24580
  87.3 94.9 %copy-start.6 = (f32[1,2,8,128]{3,2,1,0:T(8,128)S(1)}, f32[1,2,8,128]{3,2,1,0:T(8,128)}, u32[]{:S(2)}) copy-start(f32[1,2,8,128]{3,2,1,0:T(8,128)} %get-tuple-element.21) | copy-start | bytes 24580
  87.3 95.5 %copy-start.8 = (f32[1,2,8,128]{3,2,1,0:T(8,128)S(1)}, f32[1,2,8,128]{3,2,1,0:T(8,128)}, u32[]{:S(2)}) copy-start(f32[1,2,8,128]{3,2,1,0:T(8,128)} %get-tuple-element.22) | copy-start | bytes 24580
  87.3 97.1 %copy-start.3 = (f32[1,2,1024,128]{3,2,1,0:T(8,128)S(1)}, f32[1,2,1024,128]{3,2,1,0:T(8,128)}, u32[]{:S(2)}) copy-start(f32[1,2,1024,128]{3,2,1,0:T(8,128)} %get-tuple-element.15) | copy-start | bytes 3145732
  195.3 60.1 %copy-start.1 = (bf16[256,1024]{1,0:T(8,128)(2,1)S(1)}, bf16[256,1024]{1,0:T(8,128)(2,1)}, u32[]{:S(2)}) copy-start(bf16[256,1024]{1,0:T(8,128)(2,1)} %param.6) | copy-start | bytes 1572868
  195.3 60.3 %copy-start.5 = (bf16[256,256]{1,0:T(8,128)(2,1)S(1)}, bf16[256,256]{1,0:T(8,128)(2,1)}, u32[]{:S(2)}) copy-start(bf16[256,256]{1,0:T(8,128)(2,1)} %param.7) | copy-start | bytes 393220
  195.3 154.3 %all-to-all-start.1 = ((bf16[8,2,1048,128]{3,2,1,0:T(8,128)(2,1)}), bf16[8,2,1048,128]{3,2,1,0:T(8,128)(2,1)}, u32[]{:S(2)}, u32[]{:S(2)}) async-start(bf16[8,2,1048,128]{3,2,1,0:T(8,128)(2,1)} %pad_maximum_fusion), calls=%async_computation.1 | async-start | bytes 8585216 | tf_op jit(solution)/shard_map/all_to_all | solution.py:206
  255.4 174.6 %all-gather.5.cloned.1.call-start = ((), (), s32[]{:S(2)}) async-start(), calls=%async_computation.4 | async-start | bytes 4718592 | tf_op jit(solution)/shard_map/all_gather | solution.py:233
  357.4 122.7 %reduce-scatter.2.cloned.1.call-start = ((), (), s32[]{:S(2)}) async-start(), calls=%async_computation.5 | async-start | bytes 5242880 | tf_op jit(solution)/shard_map/reduce_scatter | solution.py:235
  482.3 41.2 %collective-permute-start.1 = (bf16[256,1024]{1,0:T(8,128)(2,1)}, bf16[256,1024]{1,0:T(8,128)(2,1)S(1)}, u32[]{:S(2)}, u32[]{:S(2)}) collective-permute-start(bf16[256,1024]{1,0:T(8,128)(2,1)} %get-tuple-element.32), channel_id=1, source_target_pairs={{0,0},{1,8},{2,16},{3,24},{4,4},{5,12},{6,20},{7,28},{8,1},{9,9},{... | collective-permute-start | bytes 1572872 | tf_op jit(solution)/shard_map/ppermute | solution.py:250
  487.8 47.5 %collective-permute-start.2 = (bf16[256,1024]{1,0:T(8,128)(2,1)}, bf16[256,1024]{1,0:T(8,128)(2,1)S(1)}, u32[]{:S(2)}, u32[]{:S(2)}) collective-permute-start(bf16[256,1024]{1,0:T(8,128)(2,1)} %get-tuple-element.31), channel_id=1, source_target_pairs={{0,4},{1,12},{2,20},{3,28},{4,0},{5,8},{6,16},{7,24},{8,5},{9,13},... | collective-permute-start | bytes 1572872 | tf_op jit(solution)/shard_map/ppermute | solution.py:250
  523.7 11.6 %copy-start.4 = (bf16[256,2048]{1,0:T(8,128)(2,1)}, bf16[256,2048]{1,0:T(8,128)(2,1)S(1)}, u32[]{:S(2)}) copy-start(bf16[256,2048]{1,0:T(8,128)(2,1)S(1)} %constant_dynamic-update-slice_fusion.1) | copy-start | bytes 3145732
Sparse Core Ops, SparseCore 0:
  9.5 77.7 all-gather.2
  357.5 72.4 all-gather.4
  438.4 41.6 reduce-scatter.1

commit v11 on v9

--- a/solution.py
+++ b/solution.py
@@ -167,14 +167,29 @@
         mine[0], mine[1], mine[2], mine[1], queries.reshape(query_count, QLEN, width),
         passage_store, 1, capacity, query_count,
     )
-    others = jnp.where(requester == me, 0, asked[2]).reshape(n_cache * capacity)
+    early = [(me, near)]
+    skip = requester == me
+    for flip in (1, 2):
+        mate = me + flip - 2 * (me // flip % 2) * flip
+        mate_q = lax.ppermute(
+            queries.reshape(query_count, QLEN, width), "cache",
+            [(c, c + flip - 2 * (c // flip % 2) * flip) for c in range(n_cache)],
+        )
+        theirs = lax.dynamic_index_in_dim(asked, mate, axis=1, keepdims=False)
+        early.append((mate, slot_attention(
+            theirs[0], theirs[1], theirs[2], theirs[1], mate_q,
+            passage_store, 1, capacity, query_count,
+        )))
+        skip = skip | (requester == mate)
+    others = jnp.where(skip, 0, asked[2]).reshape(n_cache * capacity)
     far = slot_attention(
         asked_rows, pick, others, asked_query.reshape(n_cache * capacity),
         q_blocks, passage_store, n_cache, capacity, query_count,
     )
-    merged_acc, merged_peak, merged_total = (
-        lax.dynamic_update_slice_in_dim(b, a, me, axis=0) for a, b in zip(near, far)
-    )
+    merged = list(far)
+    for at, part in early:
+        merged = [lax.dynamic_update_slice_in_dim(b, a, at, axis=0) for a, b in zip(part, merged)]
+    merged_acc, merged_peak, merged_total = merged
     peak_ref = lax.reduce_precision(merged_peak, exponent_bits=8, mantissa_bits=7)
     shift = jnp.where(merged_peak > LIVE, jnp.exp(merged_peak - peak_ref), 0.0)
     sent_acc = (merged_acc.reshape(n_cache, query_count, heads, QLEN, HD) * shift[..., None]).astype(

time: 560 us -> 550 us (0.982)
  starting transfers between devices: 17.7 us -> 118 us
  Pallas kernels: 199 us -> 102 us
  waiting for transfers between devices: 293 us -> 270 us
  local copies, waits for them, and re-layouts: 10.3 us -> 18.8 us
    all_to_all x1, starting transfers between devices: 4.68 us -> 104 us  [shards(): lax.all_to_all(packed, 'cache', split_axis=0, concat_axis=0, tiled=True)]
    pallas_call x2 -> x4, Pallas kernels: 199 us -> 102 us  [slot_attention(): pl.pallas_call(slot_kernel, out_shape=(jax.ShapeDtypeStruct((n_req, n_que...]
    all_gather x1, waiting for transfers between devices: 32.6 us -> 9.99 us  [shards(): everyone_q = lax.all_gather(queries, 'cache', axis=0, tiled=True)]
    dynamic_update_slice x3 -> x9, local copies, waits for them, and re-layouts: 2.26 us -> 7.98 us  [shards(): lax.dynamic_update_slice_in_dim(b, a, at, axis=0)]
  transfers between devices with their start and end apart: 7 -> 9, of which waited for: 7 -> 7; matrix products, arithmetic and copies ran while one was open for 1% -> 1% of each run, Pallas kernels for 5% -> 8%
where the time goes in v11:
time: 550 us; the launch traced here: 549 us
  waiting for transfers between devices  270 us (49%)
  starting transfers between devices  118 us (21%)
  Pallas kernels  102 us (19%)
  local copies, waits for them, and re-layouts  18.8 us (3%)
  other arithmetic  16.5 us (3%)
  between operations  13.5 us (2%)
  matrix products  9.58 us (2%)
    all_to_all x1, starting transfers between devices, shards(): lax.all_to_all(packed, 'cache', split_axis=0, concat_axis=0, tiled=True)  104 us
    pallas_call x4, Pallas kernels, slot_attention(): pl.pallas_call(slot_kernel, out_shape=(jax.ShapeDtypeStruct((n_req, n_que...  102 us
    all_to_all x1, waiting for transfers between devices, shards(): lax.all_to_all(packed, 'cache', split_axis=0, concat_axis=0, tiled=True)  90.3 us
    all_gather x1, waiting for transfers between devices, project(): everyone = lax.all_gather(attended, 'cache', axis=0, tiled=True)  72.4 us
    ppermute x2, waiting for transfers between devices, project(): got = lax.ppermute(piece, ('cache', 'stream'), perm)  45.8 us
    reduce_scatter x1, waiting for transfers between devices, project(): lax.psum_scatter(partial_sums.astype(jnp.bfloat16), 'stream', scatter_dim...  41.7 us
  transfers between devices with their start and end apart: 9, of which 7 were waited for; matrix products, arithmetic and copies ran while one was open for 1% of the time, Pallas kernels for 8%

profile of v11, /device:TPU:4, one launch (start us, length us, event | category | flops | bytes accessed | tf_op | source)
XLA Modules:
  0.0 549.0 jit_solution(6159927397843973626)
XLA Ops:
  6.5 0.7 all-gather.3.cloned.1.call-update
  7.3 1.6 collective-permute-start
  8.8 1.6 collective-permute-start.1
  10.4 0.8 eq.85
  11.2 0.8 select_reduce_fusion.2
  12.0 0.2 convert_reduce_fusion.1
  12.2 0.1 select_reduce_fusion.1
  12.3 0.1 stack.28
  12.4 0.1 stack.29
  12.5 0.1 stack.30
  12.5 0.6 copy.21
  13.2 3.9 all-to-all-start
  17.1 0.1 broadcast_in_dim.83
  17.1 0.1 broadcast_in_dim.84
  17.2 0.1 add.137
  17.3 0.1 add.138
  17.4 9.2 %all-to-all-done = s32[3,8,8]{2,0,1:T(4,128)S(1)} async-done(((s32[3,8,8]{2,0,1:T(4,128)}), s32[3,8,8]{2,0,1:T(4,128)S(1)}, u32[]{:S(2)}, u32[]{:S(2)}) %all-to-all-start) | async-done | bytes 800 | tf_op jit(solution)/shard_map/all_to_all | solution.py:156
  26.6 0.1 squeeze.43
  26.7 0.6 slice_bitcast_fusion.12
  27.3 0.6 slice_bitcast_fusion.9
  27.9 0.6 broadcast_select_fusion.valid_ref
  28.4 15.3 %shard_map.65 = (f32[1,2,1024,128]{3,2,1,0:T(8,128)}, f32[1,2,8,128]{3,2,1,0:T(8,128)}, f32[1,2,8,128]{3,2,1,0:T(8,128)}) custom-call(s32[8]{0:T(128)} %get-tuple-element.54.rows_ref, s32[8]{0:T(128)} %get-tuple-element.53.pick_ref.which_ref, s32[8]{0:T(128)} %get-tuple-element.52.valid_ref, s32[8]{0:T(128)} %get-tuple-element.53.pick_ref.which_ref, ...), custom_call_target="tpu_custom_call" | custom-call | flops 2147483648 | bytes 4718592 | tf_op jit(solution)/shard_map/pallas_call | solution.py:83
  43.7 0.1 squeeze.42.which_ref
  43.8 0.7 reshape_squeeze.4.rows_ref
  44.5 0.5 add.139.pick_ref
  45.0 0.6 slice_bitcast_fusion.6
  45.6 0.8 copy-done.3
  46.4 12.6 %shard_map.66 = (f32[1,2,1024,128]{3,2,1,0:T(8,128)}, f32[1,2,8,128]{3,2,1,0:T(8,128)}, f32[1,2,8,128]{3,2,1,0:T(8,128)}) custom-call(s32[8]{0:T(128)} %get-tuple-element.51.rows_ref, s32[8]{0:T(128)} %get-tuple-element.50.pick_ref.which_ref, s32[8]{0:T(128)} %get-tuple-element.49.valid_ref, s32[8]{0:T(128)} %get-tuple-element.50.pick_ref.which_ref, ...), custom_call_target="tpu_custom_call" | custom-call | flops 2147483648 | bytes 4718592 | tf_op jit(solution)/shard_map/pallas_call | solution.py:83
  59.0 0.8 copy-done.2
  59.8 15.5 %shard_map.67 = (f32[1,2,1024,128]{3,2,1,0:T(8,128)}, f32[1,2,8,128]{3,2,1,0:T(8,128)}, f32[1,2,8,128]{3,2,1,0:T(8,128)}) custom-call(s32[8]{0:T(128)} %get-tuple-element.48.rows_ref, s32[8]{0:T(128)} %get-tuple-element.47.pick_ref.which_ref, s32[8]{0:T(128)} %get-tuple-element.46.valid_ref, s32[8]{0:T(128)} %get-tuple-element.47.pick_ref.which_ref, ...), custom_call_target="tpu_custom_call" | custom-call | flops 2147483648 | bytes 4718592 | tf_op jit(solution)/shard_map/pallas_call | solution.py:83
  75.3 10.0 %all-gather.3.cloned.1.call-done = bf16[2048,1024]{1,0:T(8,128)(2,1)} async-done(((bf16[256,1024]{1,0:T(8,128)(2,1)}), bf16[2048,1024]{1,0:T(8,128)(2,1)}) %all-gather.3.cloned.1.call-update) | async-done | bytes 4194320 | tf_op jit(solution)/shard_map/all_gather | solution.py:162
  85.3 58.8 %shard_map.64 = (f32[8,2,1024,128]{3,2,1,0:T(8,128)}, f32[8,2,8,128]{3,2,1,0:T(8,128)}, f32[8,2,8,128]{3,2,1,0:T(8,128)}) custom-call(s32[64]{0:T(128)} %reshape_squeeze.4.rows_ref, s32[64]{0:T(128)} %add.139.pick_ref, s32[64]{0:T(128)} %broadcast_select_fusion.valid_ref, s32[64]{0:T(128)} %copy-done.14, bf16[16,128,1024]{2,1,0:T(8,128)(2,1)} %bitcast.131, ...), custom_call_target="tpu_custom_call" | custom-call | flops 17179869184 | bytes 37748736 | tf_op jit(solution)/shard_map/pallas_call | solution.py:83
  144.1 0.6 constant_dynamic-update-slice_fusion.7
  144.7 0.6 constant_dynamic-update-slice_fusion.6
  145.3 0.6 constant_dynamic-update-slice_fusion.5
  145.9 0.6 constant_dynamic-update-slice_fusion.4
  146.5 0.6 constant_dynamic-update-slice_fusion.3
  147.1 0.6 constant_dynamic-update-slice_fusion.2
  147.7 0.9 fusion.21
  148.7 1.0 constant_dynamic-update-slice_fusion.10
  149.7 2.3 constant_dynamic-update-slice_fusion.9
  152.1 1.1 constant_dynamic-update-slice_fusion.8
  153.1 5.2 multiply_convert_fusion
  158.3 2.3 pad_maximum_fusion
  160.6 104.2 %all-to-all-start.1 = ((bf16[8,2,1048,128]{3,2,1,0:T(8,128)(2,1)}), bf16[8,2,1048,128]{3,2,1,0:T(8,128)(2,1)}, u32[]{:S(2)}, u32[]{:S(2)}) async-start(bf16[8,2,1048,128]{3,2,1,0:T(8,128)(2,1)} %pad_maximum_fusion), calls=%async_computation.1 | async-start | bytes 8585216 | tf_op jit(solution)/shard_map/all_to_all | solution.py:207
  264.9 0.1 copy.31
  265.0 0.3 fusion.27
  265.4 0.2 fusion.6
  265.5 90.3 %all-to-all-done.1 = bf16[8,2,1048,128]{3,2,1,0:T(8,128)(2,1)} async-done(((bf16[8,2,1048,128]{3,2,1,0:T(8,128)(2,1)}), bf16[8,2,1048,128]{3,2,1,0:T(8,128)(2,1)}, u32[]{:S(2)}, u32[]{:S(2)}) %all-to-all-start.1) | async-done | bytes 4292640 | tf_op jit(solution)/shard_map/all_to_all | solution.py:207
  355.8 0.9 fusion.11
  356.9 4.7 multiply_reduce_fusion
  361.6 0.9 fusion.5
  362.5 0.3 copy.26
  362.9 0.9 copy.41
  363.9 72.4 %all-gather.5.cloned.1.call-done = bf16[2048,1024]{1,0:T(8,128)(2,1)} async-done(((bf16[256,1024]{1,0:T(8,128)(2,1)}), bf16[2048,1024]{1,0:T(8,128)(2,1)}) %all-gather.5.cloned.1.call-update) | async-done | bytes 4194320 | tf_op jit(solution)/shard_map/all_gather | solution.py:234
  436.3 8.3 %convolution_convert_fusion = bf16[2048,1024]{1,0:T(8,128)(2,1)} fusion(bf16[2048,1024]{1,0:T(8,128)(2,1)} %all-gather.5.cloned.1.call-done, bf16[1024,1024]{1,0:T(8,128)(2,1)S(1)} %copy-done), kind=kOutput, calls=%fused_computation.3 | convolution fusion | flops 4297064448 | bytes 10485760 | tf_op jit(solution)/shard_map/dot_general | solution.py:235
  444.7 41.7 %reduce-scatter.2.cloned.1.call-done = bf16[512,1024]{1,0:T(8,128)(2,1)} async-done(((bf16[2048,1024]{1,0:T(8,128)(2,1)}), bf16[512,1024]{1,0:T(8,128)(2,1)}) %reduce-scatter.2.cloned.1.call-update) | async-done | bytes 1048592 | tf_op jit(solution)/shard_map/reduce_scatter | solution.py:236
  486.4 2.2 constant_dynamic-slice_fusion
  488.7 5.5 collective-permute-start.2
  494.1 1.5 collective-permute-start.3
  495.6 34.2 %collective-permute-done.2 = bf16[256,1024]{1,0:T(8,128)(2,1)S(1)} collective-permute-done((bf16[256,1024]{1,0:T(8,128)(2,1)}, bf16[256,1024]{1,0:T(8,128)(2,1)S(1)}, u32[]{:S(2)}, u32[]{:S(2)}) %collective-permute-start.2) | collective-permute-done | bytes 524320 | tf_op jit(solution)/shard_map/ppermute | solution.py:251
  529.8 0.1 broadcast_in_dim.77
  530.0 11.6 %collective-permute-done.3 = bf16[256,1024]{1,0:T(8,128)(2,1)S(1)} collective-permute-done((bf16[256,1024]{1,0:T(8,128)(2,1)}, bf16[256,1024]{1,0:T(8,128)(2,1)S(1)}, u32[]{:S(2)}, u32[]{:S(2)}) %collective-permute-start.3) | collective-permute-done | bytes 524320 | tf_op jit(solution)/shard_map/ppermute | solution.py:251
  541.6 0.8 constant_dynamic-update-slice_fusion
  (55 shorter events, 0.5 us)
Async XLA Ops:
  6.5 429.7 %copy-start = (bf16[1024,1024]{1,0:T(8,128)(2,1)S(1)}, bf16[1024,1024]{1,0:T(8,128)(2,1)}, u32[]{:S(2)}) copy-start(bf16[1024,1024]{1,0:T(8,128)(2,1)} %param.9) | copy-start | bytes 6291460
  6.5 78.8 %all-gather.3.cloned.1.call-start = ((), (), s32[]{:S(2)}) async-start(), calls=%async_computation.3 | async-start | bytes 4718592 | tf_op jit(solution)/shard_map/all_gather | solution.py:162
  7.3 38.4 %collective-permute-start = (bf16[2,128,1024]{2,1,0:T(8,128)(2,1)}, bf16[2,128,1024]{2,1,0:T(8,128)(2,1)S(1)}, u32[]{:S(2)}, u32[]{:S(2)}) collective-permute-start(bf16[2,128,1024]{2,1,0:T(8,128)(2,1)} %bitcast.115), channel_id=1, source_target_pairs={{0,4},{4,0},{8,12},{12,8},{16,20},{20,16},{24,28},{28,24},{1,5},{5... | collective-permute-start | bytes 1572872 | tf_op jit(solution)/shard_map/ppermute | solution.py:174
  8.8 50.2 %collective-permute-start.1 = (bf16[2,128,1024]{2,1,0:T(8,128)(2,1)}, bf16[2,128,1024]{2,1,0:T(8,128)(2,1)S(1)}, u32[]{:S(2)}, u32[]{:S(2)}) collective-permute-start(bf16[2,128,1024]{2,1,0:T(8,128)(2,1)} %bitcast.116), channel_id=1, source_target_pairs={{0,8},{4,12},{8,0},{12,4},{16,24},{20,28},{24,16},{28,20},{1,9},{5... | collective-permute-start | bytes 1572872 | tf_op jit(solution)/shard_map/ppermute | solution.py:174
  13.2 13.4 %all-to-all-start = ((s32[3,8,8]{2,0,1:T(4,128)}), s32[3,8,8]{2,0,1:T(4,128)S(1)}, u32[]{:S(2)}, u32[]{:S(2)}) async-start(s32[3,8,8]{2,0,1:T(4,128)} %copy.21), calls=%async_computation | async-start | bytes 32768 | tf_op jit(solution)/shard_map/all_to_all | solution.py:156
  43.8 15.2 %copy-start.14 = (s32[64]{0:T(128)}, s32[64]{0:T(128)S(1)}, u32[]{:S(2)}) copy-start(s32[64]{0:T(128)S(1)} %squeeze.42.which_ref) | copy-start | bytes 772
  45.6 0.8 copy-start.3
  59.0 0.8 copy-start.2
  85.3 58.8 %copy-start.9 = (f32[1,2,8,128]{3,2,1,0:T(8,128)S(1)}, f32[1,2,8,128]{3,2,1,0:T(8,128)}, u32[]{:S(2)}) copy-start(f32[1,2,8,128]{3,2,1,0:T(8,128)} %get-tuple-element.22) | copy-start | bytes 24580
  85.3 59.4 %copy-start.11 = (f32[1,2,8,128]{3,2,1,0:T(8,128)S(1)}, f32[1,2,8,128]{3,2,1,0:T(8,128)}, u32[]{:S(2)}) copy-start(f32[1,2,8,128]{3,2,1,0:T(8,128)} %get-tuple-element.23) | copy-start | bytes 24580
  85.3 60.0 %copy-start.13 = (f32[1,2,8,128]{3,2,1,0:T(8,128)S(1)}, f32[1,2,8,128]{3,2,1,0:T(8,128)}, u32[]{:S(2)}) copy-start(f32[1,2,8,128]{3,2,1,0:T(8,128)} %get-tuple-element.24) | copy-start | bytes 24580
  85.3 60.6 %copy-start.8 = (f32[1,2,8,128]{3,2,1,0:T(8,128)S(1)}, f32[1,2,8,128]{3,2,1,0:T(8,128)}, u32[]{:S(2)}) copy-start(f32[1,2,8,128]{3,2,1,0:T(8,128)} %get-tuple-element.26) | copy-start | bytes 24580
  85.3 61.2 %copy-start.10 = (f32[1,2,8,128]{3,2,1,0:T(8,128)S(1)}, f32[1,2,8,128]{3,2,1,0:T(8,128)}, u32[]{:S(2)}) copy-start(f32[1,2,8,128]{3,2,1,0:T(8,128)} %get-tuple-element.27) | copy-start | bytes 24580
  85.3 61.8 %copy-start.12 = (f32[1,2,8,128]{3,2,1,0:T(8,128)S(1)}, f32[1,2,8,128]{3,2,1,0:T(8,128)}, u32[]{:S(2)}) copy-start(f32[1,2,8,128]{3,2,1,0:T(8,128)} %get-tuple-element.28) | copy-start | bytes 24580
  85.3 63.3 %copy-start.4 = (f32[1,2,1024,128]{3,2,1,0:T(8,128)S(1)}, f32[1,2,1024,128]{3,2,1,0:T(8,128)}, u32[]{:S(2)}) copy-start(f32[1,2,1024,128]{3,2,1,0:T(8,128)} %get-tuple-element.18) | copy-start | bytes 3145732
  148.7 3.4 copy-start.5
  160.6 104.3 %copy-start.1 = (bf16[256,1024]{1,0:T(8,128)(2,1)S(1)}, bf16[256,1024]{1,0:T(8,128)(2,1)}, u32[]{:S(2)}) copy-start(bf16[256,1024]{1,0:T(8,128)(2,1)} %param.6) | copy-start | bytes 1572868
  160.6 104.4 %copy-start.7 = (bf16[256,256]{1,0:T(8,128)(2,1)S(1)}, bf16[256,256]{1,0:T(8,128)(2,1)}, u32[]{:S(2)}) copy-start(bf16[256,256]{1,0:T(8,128)(2,1)} %param.7) | copy-start | bytes 393220
  160.6 195.2 %all-to-all-start.1 = ((bf16[8,2,1048,128]{3,2,1,0:T(8,128)(2,1)}), bf16[8,2,1048,128]{3,2,1,0:T(8,128)(2,1)}, u32[]{:S(2)}, u32[]{:S(2)}) async-start(bf16[8,2,1048,128]{3,2,1,0:T(8,128)(2,1)} %pad_maximum_fusion), calls=%async_computation.1 | async-start | bytes 8585216 | tf_op jit(solution)/shard_map/all_to_all | solution.py:207
  264.9 171.4 %all-gather.5.cloned.1.call-start = ((), (), s32[]{:S(2)}) async-start(), calls=%async_computation.4 | async-start | bytes 4718592 | tf_op jit(solution)/shard_map/all_gather | solution.py:234
  363.8 122.6 %reduce-scatter.2.cloned.1.call-start = ((), (), s32[]{:S(2)}) async-start(), calls=%async_computation.5 | async-start | bytes 5242880 | tf_op jit(solution)/shard_map/reduce_scatter | solution.py:236
  488.7 41.2 %collective-permute-start.2 = (bf16[256,1024]{1,0:T(8,128)(2,1)}, bf16[256,1024]{1,0:T(8,128)(2,1)S(1)}, u32[]{:S(2)}, u32[]{:S(2)}) collective-permute-start(bf16[256,1024]{1,0:T(8,128)(2,1)} %get-tuple-element.38), channel_id=1, source_target_pairs={{0,0},{1,8},{2,16},{3,24},{4,4},{5,12},{6,20},{7,28},{8,1},{9,9},{... | collective-permute-start | bytes 1572872 | tf_op jit(solution)/shard_map/ppermute | solution.py:251
  494.1 47.5 %collective-permute-start.3 = (bf16[256,1024]{1,0:T(8,128)(2,1)}, bf16[256,1024]{1,0:T(8,128)(2,1)S(1)}, u32[]{:S(2)}, u32[]{:S(2)}) collective-permute-start(bf16[256,1024]{1,0:T(8,128)(2,1)} %get-tuple-element.37), channel_id=1, source_target_pairs={{0,4},{1,12},{2,20},{3,28},{4,0},{5,8},{6,16},{7,24},{8,5},{9,13},... | collective-permute-start | bytes 1572872 | tf_op jit(solution)/shard_map/ppermute | solution.py:251
  530.0 11.6 %copy-start.6 = (bf16[256,2048]{1,0:T(8,128)(2,1)}, bf16[256,2048]{1,0:T(8,128)(2,1)S(1)}, u32[]{:S(2)}) copy-start(bf16[256,2048]{1,0:T(8,128)(2,1)S(1)} %constant_dynamic-update-slice_fusion.1) | copy-start | bytes 3145732
Sparse Core Ops, SparseCore 0:
  9.5 75.7 all-gather.2
  363.9 72.2 all-gather.4
  444.8 41.6 reduce-scatter.1

commit v12 on v10

--- a/solution.py
+++ b/solution.py
@@ -179,8 +179,11 @@
     )
     skip = (requester == me) | (requester == mate)
     others = jnp.where(skip, 0, asked[2]).reshape(n_cache * capacity)
+    slots = jnp.arange(n_cache * capacity, dtype=jnp.int32)
+    lead = jnp.where(others > 0, slots, slots % 2)
+    lead = lax.cummax(lead.reshape(-1, 2), axis=0).reshape(-1)
     far = slot_attention(
-        asked_rows, pick, others, asked_query.reshape(n_cache * capacity),
+        asked_rows[lead], pick[lead], others, asked_query.reshape(n_cache * capacity),
         q_blocks, passage_store, n_cache, capacity, query_count,
     )
     merged_acc, merged_peak, merged_total = (

time: 545 us -> 543 us (level)
  Pallas kernels: 119 us -> 80.6 us
  starting transfers between devices: 74.9 us -> 106 us
    pallas_call x3, Pallas kernels: 119 us -> 80.6 us  [slot_attention(): pl.pallas_call(slot_kernel, out_shape=(jax.ShapeDtypeStruct((n_req, n_que...]
    all_to_all x1, starting transfers between devices: 60.1 us -> 91.3 us  [shards(): lax.all_to_all(packed, 'cache', split_axis=0, concat_axis=0, tiled=True)]
  transfers between devices with their start and end apart: 8 -> 8, of which waited for: 7 -> 8; matrix products, arithmetic and copies ran while one was open for 1% -> 2% of each run, Pallas kernels for 5% -> 4%
where the time goes in v12:
time: 543 us
  waiting for transfers between devices  299 us (55%)
  starting transfers between devices  106 us (20%)
  Pallas kernels  80.6 us (15%)
  local copies, waits for them, and re-layouts  17.6 us (3%)
  other arithmetic  15.9 us (3%)
  between operations  13.4 us (2%)
  matrix products  9.57 us (2%)
    all_to_all x1, waiting for transfers between devices, shards(): lax.all_to_all(packed, 'cache', split_axis=0, concat_axis=0, tiled=True)  94.9 us
    all_to_all x1, starting transfers between devices, shards(): lax.all_to_all(packed, 'cache', split_axis=0, concat_axis=0, tiled=True)  91.3 us
    pallas_call x3, Pallas kernels, slot_attention(): pl.pallas_call(slot_kernel, out_shape=(jax.ShapeDtypeStruct((n_req, n_que...  80.6 us
    all_gather x1, waiting for transfers between devices, project(): everyone = lax.all_gather(attended, 'cache', axis=0, tiled=True)  72.5 us
    ppermute x2, waiting for transfers between devices, project(): got = lax.ppermute(piece, ('cache', 'stream'), perm)  45.9 us
    reduce_scatter x1, waiting for transfers between devices, project(): lax.psum_scatter(partial_sums.astype(jnp.bfloat16), 'stream', scatter_dim...  41.7 us
    all_gather x1, waiting for transfers between devices, shards(): everyone_q = lax.all_gather(queries, 'cache', axis=0, tiled=True)  38.6 us
  transfers between devices with their start and end apart: 8, of which 8 were waited for; matrix products, arithmetic and copies ran while one was open for 2% of the time, Pallas kernels for 4%

profile of v12, /device:TPU:4, one launch (start us, length us, event | category | flops | bytes accessed | tf_op | source)
XLA Modules:
  0.0 542.7 jit_solution(6795408827633313487)
XLA Ops:
  6.5 0.7 all-gather.3.cloned.1.call-update
  7.3 0.8 eq.75
  8.0 0.8 select_reduce_fusion.2
  8.9 0.2 convert_reduce_fusion.1
  9.1 0.1 select_reduce_fusion.1
  9.2 0.1 stack.28
  9.2 0.1 stack.29
  9.3 0.1 stack.30
  9.4 0.6 copy.21
  10.0 5.8 %all-to-all-start = ((s32[3,8,8]{2,0,1:T(4,128)}), s32[3,8,8]{2,0,1:T(4,128)S(1)}, u32[]{:S(2)}, u32[]{:S(2)}) async-start(s32[3,8,8]{2,0,1:T(4,128)} %copy.21), calls=%async_computation | async-start | bytes 32768 | tf_op jit(solution)/shard_map/all_to_all | solution.py:156
  15.8 2.0 collective-permute-start
  17.9 0.1 broadcast_in_dim.93
  17.9 0.1 broadcast_in_dim.94
  18.0 0.1 add.147
  18.1 0.1 add.148
  18.2 0.1 broadcast_in_dim.97
  18.3 0.1 broadcast_in_dim.98
  18.4 4.2 all-to-all-done
  22.6 0.1 squeeze.33
  22.6 0.1 fusion.23
  22.8 0.1 reshape.255
  22.9 0.1 squeeze.34.which_ref
  23.0 0.1 reshape_squeeze.4
  23.1 0.6 slice_bitcast_fusion.9
  23.7 6.9 %shard_map.65 = (f32[1,2,1024,128]{3,2,1,0:T(8,128)}, f32[1,2,8,128]{3,2,1,0:T(8,128)}, f32[1,2,8,128]{3,2,1,0:T(8,128)}) custom-call(s32[8]{0:T(128)} %get-tuple-element.45.rows_ref, s32[8]{0:T(128)} %get-tuple-element.44.pick_ref.which_ref, s32[8]{0:T(128)} %get-tuple-element.43.valid_ref, s32[8]{0:T(128)} %get-tuple-element.44.pick_ref.which_ref, ...), custom_call_target="tpu_custom_call" | custom-call | flops 2147483648 | bytes 4718592 | tf_op jit(solution)/shard_map/pallas_call | solution.py:83
  30.6 1.3 gather_fusion.1
  31.9 1.4 gather_fusion
  33.2 0.1 squeeze.35
  33.3 0.6 broadcast_select_fusion.valid_ref
  33.9 0.5 slice_bitcast_fusion.6
  34.4 0.8 collective-permute-done.q0_ref.q1_ref
  35.2 0.8 copy-done.2
  36.0 12.6 %shard_map.66 = (f32[1,2,1024,128]{3,2,1,0:T(8,128)}, f32[1,2,8,128]{3,2,1,0:T(8,128)}, f32[1,2,8,128]{3,2,1,0:T(8,128)}) custom-call(s32[8]{0:T(128)} %get-tuple-element.42.rows_ref, s32[8]{0:T(128)} %get-tuple-element.41.pick_ref.which_ref, s32[8]{0:T(128)} %get-tuple-element.40.valid_ref, s32[8]{0:T(128)} %get-tuple-element.41.pick_ref.which_ref, ...), custom_call_target="tpu_custom_call" | custom-call | flops 2147483648 | bytes 4718592 | tf_op jit(solution)/shard_map/pallas_call | solution.py:83
  48.6 38.6 %all-gather.3.cloned.1.call-done = bf16[2048,1024]{1,0:T(8,128)(2,1)} async-done(((bf16[256,1024]{1,0:T(8,128)(2,1)}), bf16[2048,1024]{1,0:T(8,128)(2,1)}) %all-gather.3.cloned.1.call-update) | async-done | bytes 4194320 | tf_op jit(solution)/shard_map/all_gather | solution.py:162
  87.3 61.1 %shard_map.64 = (f32[8,2,1024,128]{3,2,1,0:T(8,128)}, f32[8,2,8,128]{3,2,1,0:T(8,128)}, f32[8,2,8,128]{3,2,1,0:T(8,128)}) custom-call(s32[64]{0:T(128)} %gather_fusion, s32[64]{0:T(128)} %gather_fusion.1, s32[64]{0:T(128)} %broadcast_select_fusion.valid_ref, s32[64]{0:T(128)} %copy-done.10, bf16[16,128,1024]{2,1,0:T(8,128)(2,1)} %bitcast.128, ...), custom_call_target="tpu_custom_call" | custom-call | flops 17179869184 | bytes 37748736 | tf_op jit(solution)/shard_map/pallas_call | solution.py:83
  148.4 0.6 constant_dynamic-update-slice_fusion.5
  149.0 0.6 constant_dynamic-update-slice_fusion.4
  149.6 0.6 constant_dynamic-update-slice_fusion.3
  150.2 0.6 constant_dynamic-update-slice_fusion.2
  150.8 0.9 fusion.21
  151.8 1.1 constant_dynamic-update-slice_fusion.7
  152.8 2.3 constant_dynamic-update-slice_fusion.6
  155.2 5.2 multiply_convert_fusion
  160.4 2.3 pad_maximum_fusion
  162.7 91.3 %all-to-all-start.1 = ((bf16[8,2,1048,128]{3,2,1,0:T(8,128)(2,1)}), bf16[8,2,1048,128]{3,2,1,0:T(8,128)(2,1)}, u32[]{:S(2)}, u32[]{:S(2)}) async-start(bf16[8,2,1048,128]{3,2,1,0:T(8,128)(2,1)} %pad_maximum_fusion), calls=%async_computation.1 | async-start | bytes 8585216 | tf_op jit(solution)/shard_map/all_to_all | solution.py:209
  254.1 0.1 copy.31
  254.2 0.3 fusion.30
  254.6 0.2 fusion.6
  254.7 94.9 %all-to-all-done.1 = bf16[8,2,1048,128]{3,2,1,0:T(8,128)(2,1)} async-done(((bf16[8,2,1048,128]{3,2,1,0:T(8,128)(2,1)}), bf16[8,2,1048,128]{3,2,1,0:T(8,128)(2,1)}, u32[]{:S(2)}, u32[]{:S(2)}) %all-to-all-start.1) | async-done | bytes 4292640 | tf_op jit(solution)/shard_map/all_to_all | solution.py:209
  349.6 0.9 fusion.11
  350.7 4.5 multiply_reduce_fusion
  355.2 0.9 fusion.5
  356.1 0.3 copy.26
  356.5 0.9 copy.41
  357.4 72.5 %all-gather.5.cloned.1.call-done = bf16[2048,1024]{1,0:T(8,128)(2,1)} async-done(((bf16[256,1024]{1,0:T(8,128)(2,1)}), bf16[2048,1024]{1,0:T(8,128)(2,1)}) %all-gather.5.cloned.1.call-update) | async-done | bytes 4194320 | tf_op jit(solution)/shard_map/all_gather | solution.py:236
  430.0 8.3 %convolution_convert_fusion = bf16[2048,1024]{1,0:T(8,128)(2,1)} fusion(bf16[2048,1024]{1,0:T(8,128)(2,1)} %all-gather.5.cloned.1.call-done, bf16[1024,1024]{1,0:T(8,128)(2,1)S(1)} %copy-done), kind=kOutput, calls=%fused_computation.5 | convolution fusion | flops 4297064448 | bytes 10485760 | tf_op jit(solution)/shard_map/dot_general | solution.py:237
  438.4 41.7 %reduce-scatter.2.cloned.1.call-done = bf16[512,1024]{1,0:T(8,128)(2,1)} async-done(((bf16[2048,1024]{1,0:T(8,128)(2,1)}), bf16[512,1024]{1,0:T(8,128)(2,1)}) %reduce-scatter.2.cloned.1.call-update) | async-done | bytes 1048592 | tf_op jit(solution)/shard_map/reduce_scatter | solution.py:238
  480.1 2.2 constant_dynamic-slice_fusion
  482.4 5.5 %collective-permute-start.1 = (bf16[256,1024]{1,0:T(8,128)(2,1)}, bf16[256,1024]{1,0:T(8,128)(2,1)S(1)}, u32[]{:S(2)}, u32[]{:S(2)}) collective-permute-start(bf16[256,1024]{1,0:T(8,128)(2,1)} %get-tuple-element.32), channel_id=1, source_target_pairs={{0,0},{1,8},{2,16},{3,24},{4,4},{5,12},{6,20},{7,28},{8,1},{9,9},{... | collective-permute-start | bytes 1572872 | tf_op jit(solution)/shard_map/ppermute | solution.py:253
  487.8 1.5 collective-permute-start.2
  489.3 34.2 %collective-permute-done.1 = bf16[256,1024]{1,0:T(8,128)(2,1)S(1)} collective-permute-done((bf16[256,1024]{1,0:T(8,128)(2,1)}, bf16[256,1024]{1,0:T(8,128)(2,1)S(1)}, u32[]{:S(2)}, u32[]{:S(2)}) %collective-permute-start.1) | collective-permute-done | bytes 524320 | tf_op jit(solution)/shard_map/ppermute | solution.py:253
  523.5 0.1 broadcast_in_dim.87
  523.7 11.6 %collective-permute-done.2 = bf16[256,1024]{1,0:T(8,128)(2,1)S(1)} collective-permute-done((bf16[256,1024]{1,0:T(8,128)(2,1)}, bf16[256,1024]{1,0:T(8,128)(2,1)S(1)}, u32[]{:S(2)}, u32[]{:S(2)}) %collective-permute-start.2) | collective-permute-done | bytes 524320 | tf_op jit(solution)/shard_map/ppermute | solution.py:253
  535.3 0.8 constant_dynamic-update-slice_fusion
  (50 shorter events, 0.6 us)
Async XLA Ops:
  6.5 423.4 %copy-start = (bf16[1024,1024]{1,0:T(8,128)(2,1)S(1)}, bf16[1024,1024]{1,0:T(8,128)(2,1)}, u32[]{:S(2)}) copy-start(bf16[1024,1024]{1,0:T(8,128)(2,1)} %param.9) | copy-start | bytes 6291460
  6.5 80.7 %all-gather.3.cloned.1.call-start = ((), (), s32[]{:S(2)}) async-start(), calls=%async_computation.3 | async-start | bytes 4718592 | tf_op jit(solution)/shard_map/all_gather | solution.py:162
  10.0 12.5 %all-to-all-start = ((s32[3,8,8]{2,0,1:T(4,128)}), s32[3,8,8]{2,0,1:T(4,128)S(1)}, u32[]{:S(2)}, u32[]{:S(2)}) async-start(s32[3,8,8]{2,0,1:T(4,128)} %copy.21), calls=%async_computation | async-start | bytes 32768 | tf_op jit(solution)/shard_map/all_to_all | solution.py:156
  15.8 19.4 %collective-permute-start = (bf16[2,128,1024]{2,1,0:T(8,128)(2,1)}, bf16[2,128,1024]{2,1,0:T(8,128)(2,1)S(1)}, u32[]{:S(2)}, u32[]{:S(2)}) collective-permute-start(bf16[2,128,1024]{2,1,0:T(8,128)(2,1)} %bitcast.112), channel_id=1, source_target_pairs={{0,4},{4,0},{8,12},{12,8},{16,20},{20,16},{24,28},{28,24},{1,5},{5... | collective-permute-start | bytes 1572872 | tf_op jit(solution)/shard_map/ppermute | solution.py:171
  23.0 7.6 %copy-start.10 = (s32[64]{0:T(128)}, s32[64]{0:T(128)S(1)}, u32[]{:S(2)}) copy-start(s32[64]{0:T(128)S(1)} %squeeze.34.which_ref) | copy-start | bytes 772
  35.2 0.8 copy-start.2
  87.3 61.2 %copy-start.7 = (f32[1,2,8,128]{3,2,1,0:T(8,128)S(1)}, f32[1,2,8,128]{3,2,1,0:T(8,128)}, u32[]{:S(2)}) copy-start(f32[1,2,8,128]{3,2,1,0:T(8,128)} %get-tuple-element.18) | copy-start | bytes 24580
  87.3 61.8 %copy-start.9 = (f32[1,2,8,128]{3,2,1,0:T(8,128)S(1)}, f32[1,2,8,128]{3,2,1,0:T(8,128)}, u32[]{:S(2)}) copy-start(f32[1,2,8,128]{3,2,1,0:T(8,128)} %get-tuple-element.19) | copy-start | bytes 24580
  87.3 62.4 %copy-start.6 = (f32[1,2,8,128]{3,2,1,0:T(8,128)S(1)}, f32[1,2,8,128]{3,2,1,0:T(8,128)}, u32[]{:S(2)}) copy-start(f32[1,2,8,128]{3,2,1,0:T(8,128)} %get-tuple-element.21) | copy-start | bytes 24580
  87.3 63.0 %copy-start.8 = (f32[1,2,8,128]{3,2,1,0:T(8,128)S(1)}, f32[1,2,8,128]{3,2,1,0:T(8,128)}, u32[]{:S(2)}) copy-start(f32[1,2,8,128]{3,2,1,0:T(8,128)} %get-tuple-element.22) | copy-start | bytes 24580
  87.3 64.5 %copy-start.3 = (f32[1,2,1024,128]{3,2,1,0:T(8,128)S(1)}, f32[1,2,1024,128]{3,2,1,0:T(8,128)}, u32[]{:S(2)}) copy-start(f32[1,2,1024,128]{3,2,1,0:T(8,128)} %get-tuple-element.15) | copy-start | bytes 3145732
  162.7 91.4 %copy-start.1 = (bf16[256,1024]{1,0:T(8,128)(2,1)S(1)}, bf16[256,1024]{1,0:T(8,128)(2,1)}, u32[]{:S(2)}) copy-start(bf16[256,1024]{1,0:T(8,128)(2,1)} %param.6) | copy-start | bytes 1572868
  162.7 91.5 %copy-start.5 = (bf16[256,256]{1,0:T(8,128)(2,1)S(1)}, bf16[256,256]{1,0:T(8,128)(2,1)}, u32[]{:S(2)}) copy-start(bf16[256,256]{1,0:T(8,128)(2,1)} %param.7) | copy-start | bytes 393220
  162.7 186.9 %all-to-all-start.1 = ((bf16[8,2,1048,128]{3,2,1,0:T(8,128)(2,1)}), bf16[8,2,1048,128]{3,2,1,0:T(8,128)(2,1)}, u32[]{:S(2)}, u32[]{:S(2)}) async-start(bf16[8,2,1048,128]{3,2,1,0:T(8,128)(2,1)} %pad_maximum_fusion), calls=%async_computation.1 | async-start | bytes 8585216 | tf_op jit(solution)/shard_map/all_to_all | solution.py:209
  254.0 175.9 %all-gather.5.cloned.1.call-start = ((), (), s32[]{:S(2)}) async-start(), calls=%async_computation.4 | async-start | bytes 4718592 | tf_op jit(solution)/shard_map/all_gather | solution.py:236
  357.4 122.7 %reduce-scatter.2.cloned.1.call-start = ((), (), s32[]{:S(2)}) async-start(), calls=%async_computation.5 | async-start | bytes 5242880 | tf_op jit(solution)/shard_map/reduce_scatter | solution.py:238
  482.4 41.2 %collective-permute-start.1 = (bf16[256,1024]{1,0:T(8,128)(2,1)}, bf16[256,1024]{1,0:T(8,128)(2,1)S(1)}, u32[]{:S(2)}, u32[]{:S(2)}) collective-permute-start(bf16[256,1024]{1,0:T(8,128)(2,1)} %get-tuple-element.32), channel_id=1, source_target_pairs={{0,0},{1,8},{2,16},{3,24},{4,4},{5,12},{6,20},{7,28},{8,1},{9,9},{... | collective-permute-start | bytes 1572872 | tf_op jit(solution)/shard_map/ppermute | solution.py:253
  487.8 47.5 %collective-permute-start.2 = (bf16[256,1024]{1,0:T(8,128)(2,1)}, bf16[256,1024]{1,0:T(8,128)(2,1)S(1)}, u32[]{:S(2)}, u32[]{:S(2)}) collective-permute-start(bf16[256,1024]{1,0:T(8,128)(2,1)} %get-tuple-element.31), channel_id=1, source_target_pairs={{0,4},{1,12},{2,20},{3,28},{4,0},{5,8},{6,16},{7,24},{8,5},{9,13},... | collective-permute-start | bytes 1572872 | tf_op jit(solution)/shard_map/ppermute | solution.py:253
  523.7 11.6 %copy-start.4 = (bf16[256,2048]{1,0:T(8,128)(2,1)}, bf16[256,2048]{1,0:T(8,128)(2,1)S(1)}, u32[]{:S(2)}) copy-start(bf16[256,2048]{1,0:T(8,128)(2,1)S(1)} %constant_dynamic-update-slice_fusion.1) | copy-start | bytes 3145732
Sparse Core Ops, SparseCore 0:
  9.5 77.7 all-gather.2
  357.5 72.4 all-gather.4
  438.5 41.6 reduce-scatter.1
